TPU v7x, 32 devices: a whole 2x2x4 slice. The times are simulated.
32 devices in a mesh: pair: 8 (over z, y), virt: 4 (over x, core).
Axes of the slice: x: 2, y: 2, z: 4, core: 2. Of those that a mesh axis runs over, the one named last changes fastest.
Arguments:
- amps_pm: bfloat16 [64, 64, 4096], P(('pair', 'virt')), may hold values from -6 to 6
- integrals: bfloat16 [32, 4096, 2048], P(('pair', 'virt')), may hold values from -0.046875 to 0.046875
- fock_vv: bfloat16 [512, 512], replicated, may hold values from -0.25 to 0.25
- blk_tiles: int32 [32, 2], replicated, may hold values from 0 to 63, as said below
- blk_mask: int32 [32], replicated, may hold values 0 or 1
Outputs:
- sigma: bfloat16 [64, 64, 2048], P('pair', 'virt')
Inputs may be any that keep to these rules, and one draw needn't show every extreme that they name: Each row is (input tile pair, output tile pair). Integral tile r belongs to device r // 1 of the joined axis pair+virt, and its input tile pair lies in that device's virt slab: blk_tiles[r, 0] // 16 == (r) % 4. No two rows are equal.
All inputs are finite; a program needn't handle non-finite values.
Results may differ from a plain program's by a relative error of at most 0.0033.
Values may be sent and summed in bfloat16 or wider, within the bound.
No kernel may reach another device: no remote copies, remote signals or barrier semaphores. Data moves between devices by JAX's collectives and lax.ppermute only.
A program may use at most 128 MiB of HBM per device.

v0:
```python
import jax
import jax.numpy as jnp
from jax import lax
from jax.sharding import PartitionSpec as P

TILE = 64
NVT = 8
A_W = 8
AS = 32


def per_device(amps_pm, integrals, fock_vv, blk_tiles, blk_mask):
    n_virt = lax.axis_size("virt")
    n_pair = lax.axis_size("pair")
    pm_rows, n_tiles, tile_len = amps_pm.shape
    blk_dev = integrals.shape[0]
    out_cols = integrals.shape[2]
    slab = n_tiles // n_virt
    device = lax.axis_index(("pair", "virt"))
    virt_idx = lax.axis_index("virt")
    own_tiles = lax.dynamic_slice_in_dim(blk_tiles, device * blk_dev, blk_dev, 0)
    own_mask = lax.dynamic_slice_in_dim(blk_mask, device * blk_dev, blk_dev, 0).astype(jnp.float32)
    local_in = own_tiles[:, 0] - virt_idx * slab
    amps_vm = lax.all_to_all(amps_pm, "virt", split_axis=1, concat_axis=0, tiled=True)
    sub_rows = amps_pm[:, :, :out_cols].reshape(pm_rows, A_W, NVT, AS, TILE)
    fock_four = fock_vv.reshape(NVT, TILE, NVT, TILE)
    onebody = jnp.einsum(
        "pkqsd,bjqd->pkbsj", sub_rows, fock_four, preferred_element_type=jnp.float32
    )
    onebody = onebody.reshape(pm_rows, n_tiles, out_cols)
    arrived = lax.all_to_all(onebody, "virt", split_axis=1, concat_axis=0, tiled=True)
    chosen = jnp.take(lax.all_gather(amps_vm, "pair", axis=0, tiled=True), local_in, axis=1)
    product = jnp.einsum("rkc,kco->rko", chosen, integrals, preferred_element_type=jnp.float32)
    partial_value = product * own_mask[None, :, None]
    p_dev = partial_value.shape[0] // n_pair
    dest_virt = own_tiles[:, 1] // slab
    virt_ids = jnp.arange(n_virt, dtype=jnp.int32)
    select = (virt_ids[:, None] == dest_virt[None, :]).astype(jnp.float32)
    outgoing = (
        partial_value.reshape(n_pair, 1, p_dev, blk_dev, out_cols) * select[None, :, None, :, None]
    )
    outgoing = outgoing.reshape(n_pair * n_virt * p_dev, blk_dev, out_cols)
    received = lax.all_to_all(
        outgoing.astype(jnp.bfloat16), ("pair", "virt"), split_axis=0, concat_axis=1, tiled=True
    ).astype(outgoing.dtype)
    my_tiles = virt_idx * slab + jnp.arange(slab, dtype=jnp.int32)
    one_hot = (blk_tiles[:, 1][:, None] == my_tiles[None, :]).astype(jnp.float32)
    summed = jnp.einsum("pro,rt->pto", received, one_hot, precision=lax.Precision.HIGHEST)
    return (summed + arrived).astype(jnp.bfloat16)


def solution(mesh):
    return jax.shard_map(
        per_device,
        mesh=mesh,
        in_specs=(P(("pair", "virt"), None, None), P(("pair", "virt"), None, None), P(), P(), P()),
        out_specs=P("pair", "virt", None),
        check_vma=False,
    )
```

profile of v0, /device:TPU:0, one launch (start us, length us, event | category | flops | bytes accessed | tf_op | source)
XLA Modules:
  0.0 224.9 jit_solution(6049675598253406029)
XLA Ops:
  6.5 2.3 %copy.16 = bf16[2,64,4096]{2,0,1:T(2,128)(2,1)S(1)} copy(bf16[2,64,4096]{2,1,0:T(8,128)(2,1)} %param.5) | data formatting | bytes 2097152 | tf_op args[0]
  8.9 18.5 %all_to_all.54 = bf16[2,64,4096]{2,0,1:T(2,128)(2,1)S(1)} all-to-all(bf16[2,64,4096]{2,0,1:T(2,128)(2,1)S(1)} %copy.16), channel_id=1, replica_groups=mesh['pair'=8,'virt'=4] {'virt'}, dimensions={1} | all-to-all | bytes 2097152 | tf_op jit(solution)/shard_map/all_to_all | solution.py:24
  27.3 0.6 copy.17
  27.9 1.0 copy.18
  29.0 0.1 slice-done
  29.1 1.1 reshape.154
  30.2 0.5 reshape.111
  30.7 1.3 convolution_bitcast_fusion.1
  32.0 0.2 copy.30
  32.2 2.1 reshape.157
  34.3 3.5 %all-to-all-start.2 = ((f32[2,64,2048]{2,0,1:T(2,128)}), f32[2,64,2048]{2,0,1:T(2,128)S(1)}, u32[]{:S(2)}, u32[]{:S(2)}) async-start(f32[2,64,2048]{2,0,1:T(2,128)} %reshape.157), calls=%async_computation.2 | async-start | bytes 2097152 | tf_op jit(solution)/shard_map/all_to_all | solution.py:31
  37.9 0.1 constant_dynamic-slice_fusion.1
  38.0 0.5 fusion.22
  41.1 0.6 dynamic_slice.7
  43.1 0.1 mul.69
  43.2 110.7 %all-gather.2.cloned.1.call-done = bf16[64,16,4096]{2,1,0:T(8,128)(2,1)} async-done(((bf16[8,16,4096]{2,1,0:T(8,128)(2,1)}), bf16[64,16,4096]{2,1,0:T(8,128)(2,1)}) %all-gather.2.cloned.1.call-update) | async-done | bytes 8388624 | tf_op jit(solution)/shard_map/all_gather | solution.py:32
  153.9 3.5 %constant_dynamic-slice_fusion = bf16[64,1,4096]{2,1,0:T(2,128)(2,1)S(1)} fusion(bf16[64,16,4096]{2,1,0:T(8,128)(2,1)} %all-gather.2.cloned.1.call-done, s32[]{:T(128)} %bitcast.8), kind=kLoop, calls=%fused_computation.22 | loop fusion | bytes 1048580 | solution.py:32
  157.5 9.2 %fusion.7 = f32[8,8,2048]{2,1,0:T(8,128)S(1)} fusion(bf16[1,4096,2048]{2,1,0:T(8,128)(2,1)} %param.6, bf16[64,1,4096]{2,1,0:T(2,128)(2,1)S(1)} %constant_dynamic-slice_fusion, pred[]{:T(512)} %bitcast.4, f32[]{:T(128)} %bitcast.11), kind=kOutput, calls=%fused_computation.6 | convolution fusion | flops 1074135040 | bytes 17825796 | tf_op jit(solution)/shard_map/rkc,kco->rko/dot_general | solution.py:33
  166.6 0.2 mul.66
  166.9 3.5 %mul.67 = f32[256,1,2048]{2,1,0:T(1,128)} reshape(f32[8,4,8,2048]{3,2,1,0:T(8,128)S(1)} %mul.66) | data formatting | bytes 4194304 | tf_op jit(solution)/shard_map/mul | solution.py:40
  170.4 3.1 %multiply_convert_fusion = bf16[256,1,2048]{2,1,0:T(2,128)(2,1)S(1)} fusion(f32[256,1,2048]{2,1,0:T(1,128)} %mul.67, f32[256]{0:T(256)S(1)} %mul.69), kind=kLoop, calls=%fused_computation.7 | loop fusion | flops 1048576 | bytes 3146752 | tf_op jit(solution)/shard_map/convert_element_type | solution.py:44
  173.5 0.5 broadcast.110
  174.0 7.8 %reduce = bf16[256,2048]{1,0:T(8,128)(2,1)} reduce(bf16[256,1,2048]{2,1,0:T(2,128)(2,1)S(1)} %multiply_convert_fusion, bf16[]{:T(256)} %broadcast.110), dimensions={1}, to_apply=%multiply_convert_fusion.reduce_sub_computation | reduce | bytes 2097154 | tf_op jit(solution)/shard_map/convert_element_type | solution.py:44
  181.8 2.9 %reshape.158 = bf16[32,2,8192]{2,1,0:T(2,128)(2,1)} reshape(bf16[256,2048]{1,0:T(8,128)(2,1)} %reduce) | data formatting | bytes 2097152
  184.7 2.8 %all-to-all-start.1 = ((bf16[32,2,8192]{2,1,0:T(2,128)(2,1)}), bf16[32,2,8192]{2,1,0:T(2,128)(2,1)S(1)}, u32[]{:S(2)}, u32[]{:S(2)}) async-start(bf16[32,2,8192]{2,1,0:T(2,128)(2,1)} %reshape.158), calls=%async_computation.1 | async-start | bytes 2097152 | tf_op jit(solution)/shard_map/all_to_all | solution.py:43
  187.6 0.6 copy.24
  188.2 1.1 copy.25
  189.3 24.5 %all-to-all-done.1 = bf16[32,2,8192]{2,1,0:T(2,128)(2,1)S(1)} async-done(((bf16[32,2,8192]{2,1,0:T(2,128)(2,1)}), bf16[32,2,8192]{2,1,0:T(2,128)(2,1)S(1)}, u32[]{:S(2)}, u32[]{:S(2)}) %all-to-all-start.1) | async-done | bytes 1048608 | tf_op jit(solution)/shard_map/all_to_all | solution.py:43
  213.7 1.0 reshape.159
  214.8 0.6 copy.45
  215.4 0.6 copy-done
  216.0 2.0 fusion.3
  (15 shorter events, 0.1 us)
Async XLA Ops:
  6.5 147.4 %all-gather.2.cloned.1.call-start = ((), (), s32[]{:S(2)}) async-start(), calls=%async_computation.3 | async-start | bytes 9437184 | tf_op jit(solution)/shard_map/all_gather | solution.py:32
  27.9 1.2 slice-start
  28.9 1.2 copy-start.1
  32.2 5.7 %copy-start.2 = (s32[32,2]{0,1:T(2,128)S(1)}, s32[32,2]{0,1:T(2,128)}, u32[]{:S(2)}) copy-start(s32[32,2]{0,1:T(2,128)} %param.8) | copy-start | bytes 772
  32.2 8.9 %copy-start.3 = (s32[32]{0:T(128)S(1)}, s32[32]{0:T(128)}, u32[]{:S(2)}) copy-start(s32[32]{0:T(128)} %param.9) | copy-start | bytes 388
  34.3 150.4 %all-to-all-start.2 = ((f32[2,64,2048]{2,0,1:T(2,128)}), f32[2,64,2048]{2,0,1:T(2,128)S(1)}, u32[]{:S(2)}, u32[]{:S(2)}) async-start(f32[2,64,2048]{2,0,1:T(2,128)} %reshape.157), calls=%async_computation.2 | async-start | bytes 2097152 | tf_op jit(solution)/shard_map/all_to_all | solution.py:31
  184.7 29.0 %all-to-all-start.1 = ((bf16[32,2,8192]{2,1,0:T(2,128)(2,1)}), bf16[32,2,8192]{2,1,0:T(2,128)(2,1)S(1)}, u32[]{:S(2)}, u32[]{:S(2)}) async-start(bf16[32,2,8192]{2,1,0:T(2,128)(2,1)} %reshape.158), calls=%async_computation.1 | async-start | bytes 2097152 | tf_op jit(solution)/shard_map/all_to_all | solution.py:43
  214.8 1.2 copy-start
Sparse Core Ops, SparseCore 0:
  29.1 124.7 all-gather.1
where the time goes:
time: 225 us
  waiting for transfers between devices  135 us (60%)
  local copies, waits for them, and re-layouts  24 us (11%)
  blocking collectives  18.5 us (8%)
  between operations  17.5 us (8%)
  matrix products  12.5 us (6%)
  other arithmetic  10.9 us (5%)
  starting transfers between devices  6.33 us (3%)
    all_gather x1, waiting for transfers between devices, per_device(): lax.all_gather(amps_vm, 'pair', axis=0, tiled=True)  111 us
    all_to_all x1, waiting for transfers between devices, per_device(): lax.all_to_all(outgoing.astype(jnp.bfloat16), ('pair', 'virt'), split_axi...  24.5 us
    all_to_all x1, blocking collectives, per_device(): lax.all_to_all(amps_pm, 'virt', split_axis=1, concat_axis=0, tiled=True)  18.5 us
    convert_element_type x2, other arithmetic, per_device(): outgoing.astype(jnp.bfloat16)  10.9 us
    dot_general x1, matrix products, per_device(): jnp.einsum('rkc,kco->rko', chosen, integrals, preferred_element_type=jnp....  9.16 us
    unnamed x12, local copies, waits for them, and re-layouts  7.49 us
  transfers between devices with their start and end apart: 3, of which 2 were waited for; matrix products, arithmetic and copies ran while one was open for 17% of the time, Pallas kernels for 0%

commit v1 on v0

v1 whole, which is shorter than its diff:
```python
import jax
import jax.numpy as jnp
from jax import lax
from jax.sharding import PartitionSpec as P

TILE = 64
NVT = 8
AS = 32


def per_device(amps_pm, integrals, fock_vv, blk_tiles, blk_mask):
    n_virt = lax.axis_size("virt")
    n_pair = lax.axis_size("pair")
    n_dev = n_virt * n_pair
    pm_rows, n_tiles, tile_len = amps_pm.shape
    out_cols = integrals.shape[2]
    slab = n_tiles // n_virt
    device = lax.axis_index(("pair", "virt"))
    virt_idx = lax.axis_index("virt")
    p_grp = pm_rows * n_virt

    tin_all = blk_tiles[:, 0]
    picked = jnp.take(amps_pm, tin_all, axis=1)
    picked = jnp.transpose(picked, (1, 0, 2))
    chosen = lax.all_to_all(picked, ("pair", "virt"), 0, 0, tiled=True)
    chosen = chosen.reshape(n_dev * pm_rows, tile_len)

    sub = lax.all_to_all(
        amps_pm[:, :, :out_cols], "virt", split_axis=1, concat_axis=0, tiled=True
    )
    sub = sub.reshape(p_grp, slab // NVT, NVT, AS, TILE)
    fock_four = fock_vv.reshape(NVT, TILE, NVT, TILE)
    onebody = jnp.einsum(
        "pkqsd,bjqd->pkbsj", sub, fock_four, preferred_element_type=jnp.float32
    ).reshape(p_grp, slab, out_cols)

    own_tiles = lax.dynamic_index_in_dim(blk_tiles, device, 0, keepdims=False)
    own_mask = lax.dynamic_index_in_dim(blk_mask, device, 0, keepdims=False)
    product = jnp.dot(chosen, integrals[0], preferred_element_type=jnp.float32)
    product = (product * own_mask.astype(jnp.float32)).astype(jnp.bfloat16)

    dest_virt = own_tiles[1] // slab
    select = (jnp.arange(n_virt, dtype=jnp.int32) == dest_virt).astype(jnp.bfloat16)
    outgoing = product.reshape(n_pair, 1, p_grp, out_cols) * select[None, :, None, None]
    outgoing = outgoing.reshape(n_dev, p_grp, out_cols)
    received = lax.all_to_all(outgoing, ("pair", "virt"), 0, 0, tiled=True)

    my_tiles = virt_idx * slab + jnp.arange(slab, dtype=jnp.int32)
    one_hot = (blk_tiles[:, 1][:, None] == my_tiles[None, :]).astype(jnp.bfloat16)
    ladder = jnp.einsum(
        "rpo,rt->pto", received, one_hot, preferred_element_type=jnp.float32
    )
    return (ladder + onebody).astype(jnp.bfloat16)


def solution(mesh):
    return jax.shard_map(
        per_device,
        mesh=mesh,
        in_specs=(P(("pair", "virt"), None, None), P(("pair", "virt"), None, None), P(), P(), P()),
        out_specs=P("pair", "virt", None),
        check_vma=False,
    )
```

time: 225 us -> 75.8 us (0.34)
  waiting for transfers between devices: 135 us -> 29.6 us
  blocking collectives: 18.5 us -> 0 us
  between operations: 17.5 us -> 3.27 us
  local copies, waits for them, and re-layouts: 24 us -> 11.9 us
  other arithmetic: 10.9 us -> 2.74 us
  starting transfers between devices: 6.33 us -> 14.4 us
    all_gather x1 -> x0, waiting for transfers between devices: 111 us -> none  [per_device(): lax.all_gather(amps_vm, 'pair', axis=0, tiled=True)]
    all_to_all x1 -> x0, blocking collectives: 18.5 us -> none  [per_device(): lax.all_to_all(amps_pm, 'virt', split_axis=1, concat_axis=0, tiled=True)]
    convert_element_type x3 -> x1, other arithmetic: 10.9 us -> 0.01 us  [per_device(): (jnp.arange(n_virt, dtype=jnp.int32) == dest_virt).astype(jnp.bfloat16)]
    all_to_all x2 -> x3, starting transfers between devices: 6.33 us -> 14.4 us  [the longest x1 7.33 us: per_device(): chosen = lax.all_to_all(picked, ('pair', 'virt'), 0, 0, tiled=True)]
    unnamed x12 -> x3, local copies, waits for them, and re-layouts: 7.49 us -> 1.34 us
    all_to_all x2 -> x3, waiting for transfers between devices: 24.5 us -> 29.6 us  [the longest x1 22.2 us: per_device(): received = lax.all_to_all(outgoing, ('pair', 'virt'), 0, 0, tiled=True)]
    mul x4 -> x2, local copies, waits for them, and re-layouts: 3.93 us -> 0.09 us  [per_device(): product.reshape(n_pair, 1, p_grp, out_cols) * select[None, :, None, None]]
    another operation x1 -> x0, local copies, waits for them, and re-layouts: 3.53 us -> none  [per_device(): jnp.take(lax.all_gather(amps_vm, 'pair', axis=0, tiled=True), local_in, a...]
  transfers between devices with their start and end apart: 3 -> 3, of which waited for: 2 -> 2; matrix products, arithmetic and copies ran while one was open for 17% -> 25% of each run, Pallas kernels for 0% -> 0%
where the time goes in v1:
time: 75.8 us; the launch traced here: 75.2 us
  waiting for transfers between devices  29.6 us (39%)
  starting transfers between devices  14.4 us (19%)
  matrix products  13.3 us (18%)
  local copies, waits for them, and re-layouts  11.9 us (16%)
  between operations  3.27 us (4%)
  other arithmetic  2.74 us (4%)
    all_to_all x1, waiting for transfers between devices, per_device(): received = lax.all_to_all(outgoing, ('pair', 'virt'), 0, 0, tiled=True)  22.2 us
    dot_general x1, matrix products, per_device(): product = jnp.dot(chosen, integrals[0], preferred_element_type=jnp.float32)  8.79 us
    all_to_all x1, waiting for transfers between devices, per_device(): chosen = lax.all_to_all(picked, ('pair', 'virt'), 0, 0, tiled=True)  7.37 us
    all_to_all x1, starting transfers between devices, per_device(): chosen = lax.all_to_all(picked, ('pair', 'virt'), 0, 0, tiled=True)  7.33 us
    all_to_all x1, starting transfers between devices, per_device(): received = lax.all_to_all(outgoing, ('pair', 'virt'), 0, 0, tiled=True)  3.62 us
    all_to_all x1, starting transfers between devices, per_device(): lax.all_to_all(amps_pm[:, :, :out_cols], 'virt', split_axis=1, concat_axi...  3.47 us
    dot_general x1, matrix products, per_device(): jnp.einsum('rpo,rt->pto', received, one_hot, preferred_element_type=jnp.f...  3.24 us
    gather x1, local copies, waits for them, and re-layouts, per_device(): picked = jnp.take(amps_pm, tin_all, axis=1)  2.61 us
  transfers between devices with their start and end apart: 3, of which 2 were waited for; matrix products, arithmetic and copies ran while one was open for 25% of the time, Pallas kernels for 0%

profile of v1, /device:TPU:0, one launch (start us, length us, event | category | flops | bytes accessed | tf_op | source)
XLA Modules:
  0.0 75.2 jit_solution(7322697430825926333)
XLA Ops:
  0.0 0.8 %slice_bitcast_fusion = (s32[32]{0:T(128)S(1)}, s32[32]{0:T(128)S(1)}) fusion(s32[32,2]{0,1:T(2,128)} %param.8), kind=kLoop, calls=%fused_computation.24 | loop fusion | flops 96 | bytes 512 | tf_op jit(solution)/shard_map/eq | solution.py:49
  0.8 0.7 and_bitcast_fusion
  1.5 2.6 %gather_fusion = bf16[32,2,4096]{2,0,1:T(8,128)(2,1)S(1)} fusion(bf16[2,64,4096]{2,1,0:T(8,128)(2,1)} %param.5, s32[1024]{0:T(1024)S(1)} %pad_clamp_fusion), kind=kCustom, calls=%fused_computation | custom fusion | bytes 1048704 | tf_op jit(solution)/shard_map/jit(_take)/gather | solution.py:23
  4.1 0.1 broadcast_select_fusion
  4.2 1.3 %copy.15 = bf16[32,2,4096]{2,1,0:T(2,128)(2,1)} copy(bf16[32,2,4096]{2,0,1:T(8,128)(2,1)S(1)} %broadcast_select_fusion) | data formatting | bytes 1048576 | tf_op jit(solution)/shard_map/jit(_take)/select_n | solution.py:23
  5.5 0.0 copy-start
  5.5 7.3 %all-to-all-start = ((bf16[32,2,4096]{2,1,0:T(2,128)(2,1)}), bf16[32,2,4096]{2,1,0:T(2,128)(2,1)S(1)}, u32[]{:S(2)}, u32[]{:S(2)}) async-start(bf16[32,2,4096]{2,1,0:T(2,128)(2,1)} %copy.15), calls=%async_computation | async-start | bytes 1048576 | tf_op jit(solution)/shard_map/all_to_all | solution.py:25
  12.9 1.1 %slice.16 = bf16[2,64,2048]{2,1,0:T(8,128)(2,1)S(1)} slice(bf16[2,64,4096]{2,1,0:T(8,128)(2,1)} %param.5), slice={[0:2], [0:64], [0:2048]} | slice | bytes 1048576 | tf_op jit(solution)/shard_map/slice | solution.py:29
  13.9 0.8 %constant_dynamic-slice_fusion = s32[1,2]{0,1:T(2,128)S(1)} fusion(s32[32,2]{0,1:T(2,128)} %param.8, s32[]{:T(128)S(6)} %select_n.29), kind=kLoop, calls=%fused_computation.25 | loop fusion | bytes 20 | tf_op jit(solution)/shard_map/jit(dynamic_index_in_dim)/dynamic_slice | solution.py:37
  14.7 0.5 slice.15
  17.1 1.3 %copy.25 = bf16[2,64,2048]{2,0,1:T(2,128)(2,1)} copy(bf16[2,64,2048]{2,1,0:T(8,128)(2,1)S(1)} %slice.16) | data formatting | bytes 1048576
  19.1 0.1 mul.42
  19.2 1.3 %dynamic_slice.8 = s32[1]{0:T(128)} dynamic-slice(s32[32]{0:T(128)} %param.9, s32[]{:T(128)S(6)} %select_n.29), dynamic_slice_sizes={1} | dynamic-slice | bytes 12 | tf_op jit(solution)/shard_map/jit(dynamic_index_in_dim)/dynamic_slice | solution.py:38
  21.1 7.4 %all-to-all-done = bf16[32,2,4096]{2,1,0:T(2,128)(2,1)S(1)} async-done(((bf16[32,2,4096]{2,1,0:T(2,128)(2,1)}), bf16[32,2,4096]{2,1,0:T(2,128)(2,1)S(1)}, u32[]{:S(2)}, u32[]{:S(2)}) %all-to-all-start) | async-done | bytes 524320 | tf_op jit(solution)/shard_map/all_to_all | solution.py:25
  28.5 3.5 %all-to-all-start.2 = ((bf16[2,64,2048]{2,0,1:T(2,128)(2,1)}), bf16[2,64,2048]{2,0,1:T(2,128)(2,1)S(1)}, u32[]{:S(2)}, u32[]{:S(2)}) async-start(bf16[2,64,2048]{2,0,1:T(2,128)(2,1)} %copy.25), calls=%async_computation.2 | async-start | bytes 1048576 | tf_op jit(solution)/shard_map/all_to_all | solution.py:28
  31.9 0.2 reshape.34
  32.2 8.8 %fusion.10 = bf16[8,8,2048]{2,1,0:T(8,128)(2,1)S(1)} fusion(bf16[64,4096]{1,0:T(8,128)(2,1)S(1)} %reshape.34, bf16[1,4096,2048]{2,1,0:T(8,128)(2,1)} %param.6, f32[]{:T(128)} %bitcast.5), kind=kOutput, calls=%fused_computation.8 | convolution fusion | flops 1074003968 | bytes 17563652 | tf_op jit(solution)/shard_map/dot_general | solution.py:39
  41.0 1.2 %bitcast_multiply_fusion = bf16[32,8,2048]{2,1,0:T(8,128)(2,1)} fusion(bf16[32]{0:T(256)(128)(2,1)S(1)} %mul.42, bf16[8,8,2048]{2,1,0:T(8,128)(2,1)S(1)} %fusion.10), kind=kLoop, calls=%fused_computation.11 | loop fusion | flops 524288 | bytes 1310784 | tf_op jit(solution)/shard_map/mul | solution.py:44
  42.1 0.0 all-to-all-done.2
  42.1 3.6 %all-to-all-start.1 = ((bf16[32,8,2048]{2,1,0:T(8,128)(2,1)}), bf16[32,8,2048]{2,1,0:T(8,128)(2,1)}, u32[]{:S(2)}, u32[]{:S(2)}) async-start(bf16[32,8,2048]{2,1,0:T(8,128)(2,1)} %bitcast_multiply_fusion), calls=%async_computation.1 | async-start | bytes 2097152 | tf_op jit(solution)/shard_map/all_to_all | solution.py:46
  45.8 0.0 copy-done
  45.8 0.5 reshape.35
  46.3 0.2 copy.31
  46.5 1.1 %reshape.48 = bf16[8,2,8,32,64,1]{4,3,2,1,0,5:T(8,128)(2,1)S(1)} reshape(bf16[4,2,16,2048]{3,2,1,0:T(8,128)(2,1)S(1)} %bitcast.46) | data formatting | bytes 1048576 | tf_op jit(solution)/shard_map/reshape | solution.py:31
  47.6 1.3 %convolution_bitcast_fusion.1 = f32[8,2,8,32,64]{4,3,1,0,2:T(8,128)S(1)} fusion(bf16[8,2,8,32,64,1]{4,3,2,1,0,5:T(8,128)(2,1)S(1)} %reshape.48, bf16[8,64,8,64,1,1]{3,2,1,0,5,4:T(8,128)(2,1)S(1)} %bitcast.48), kind=kOutput, calls=%fused_computation.9 | convolution fusion | flops 268435456 | bytes 2097152 | tf_op jit(solution)/shard_map/pkqsd,bjqd->pkbsj/dot_general | solution.py:33
  48.8 0.2 copy.20
  49.1 0.7 reshape.37
  49.7 22.2 %all-to-all-done.1 = bf16[32,8,2048]{2,1,0:T(8,128)(2,1)} async-done(((bf16[32,8,2048]{2,1,0:T(8,128)(2,1)}), bf16[32,8,2048]{2,1,0:T(8,128)(2,1)}, u32[]{:S(2)}, u32[]{:S(2)}) %all-to-all-start.1) | async-done | bytes 1048608 | tf_op jit(solution)/shard_map/all_to_all | solution.py:46
  71.9 3.2 %fusion.3 = bf16[8,16,2048]{2,1,0:T(8,128)(2,1)} fusion(f32[8,16,2048]{2,1,0:T(8,128)S(1)} %reshape.37, bf16[32,8,2048]{2,1,0:T(8,128)(2,1)} %all-to-all-done.1, s32[32]{0:T(128)S(1)} %get-tuple-element.5, s32[16]{0:T(128)S(1)} %iota_add_fusion), kind=kOutput, calls=%fused_computation.5 | convolution fusion | flops 17302016 | bytes 2621632 | tf_op jit(solution)/shard_map/rpo,rt->pto/dot_general | solution.py:50
  (4 shorter events, 0.0 us)
Async XLA Ops:
  5.5 40.2 %copy-start = (bf16[512,512]{1,0:T(8,128)(2,1)S(1)}, bf16[512,512]{1,0:T(8,128)(2,1)}, u32[]{:S(2)}) copy-start(bf16[512,512]{1,0:T(8,128)(2,1)} %param.7) | copy-start | bytes 1572868
  5.5 22.9 %all-to-all-start = ((bf16[32,2,4096]{2,1,0:T(2,128)(2,1)}), bf16[32,2,4096]{2,1,0:T(2,128)(2,1)S(1)}, u32[]{:S(2)}, u32[]{:S(2)}) async-start(bf16[32,2,4096]{2,1,0:T(2,128)(2,1)} %copy.15), calls=%async_computation | async-start | bytes 1048576 | tf_op jit(solution)/shard_map/all_to_all | solution.py:25
  28.5 13.7 %all-to-all-start.2 = ((bf16[2,64,2048]{2,0,1:T(2,128)(2,1)}), bf16[2,64,2048]{2,0,1:T(2,128)(2,1)S(1)}, u32[]{:S(2)}, u32[]{:S(2)}) async-start(bf16[2,64,2048]{2,0,1:T(2,128)(2,1)} %copy.25), calls=%async_computation.2 | async-start | bytes 1048576 | tf_op jit(solution)/shard_map/all_to_all | solution.py:28
  42.1 29.8 %all-to-all-start.1 = ((bf16[32,8,2048]{2,1,0:T(8,128)(2,1)}), bf16[32,8,2048]{2,1,0:T(8,128)(2,1)}, u32[]{:S(2)}, u32[]{:S(2)}) async-start(bf16[32,8,2048]{2,1,0:T(8,128)(2,1)} %bitcast_multiply_fusion), calls=%async_computation.1 | async-start | bytes 2097152 | tf_op jit(solution)/shard_map/all_to_all | solution.py:46

commit v2 on v1

--- a/solution.py
+++ b/solution.py
@@ -6,6 +6,7 @@
 TILE = 64
 NVT = 8
 AS = 32
+N_CHUNK = 2
 
 
 def per_device(amps_pm, integrals, fock_vv, blk_tiles, blk_mask):
@@ -34,22 +35,40 @@
         "pkqsd,bjqd->pkbsj", sub, fock_four, preferred_element_type=jnp.float32
     ).reshape(p_grp, slab, out_cols)
 
-    own_tiles = lax.dynamic_index_in_dim(blk_tiles, device, 0, keepdims=False)
     own_mask = lax.dynamic_index_in_dim(blk_mask, device, 0, keepdims=False)
-    product = jnp.dot(chosen, integrals[0], preferred_element_type=jnp.float32)
-    product = (product * own_mask.astype(jnp.float32)).astype(jnp.bfloat16)
+    own_mask = own_mask.astype(jnp.float32)
 
-    dest_virt = own_tiles[1] // slab
-    select = (jnp.arange(n_virt, dtype=jnp.int32) == dest_virt).astype(jnp.bfloat16)
-    outgoing = product.reshape(n_pair, 1, p_grp, out_cols) * select[None, :, None, None]
-    outgoing = outgoing.reshape(n_dev, p_grp, out_cols)
-    received = lax.all_to_all(outgoing, ("pair", "virt"), 0, 0, tiled=True)
+    tout = blk_tiles[:, 1].reshape(n_pair, n_virt)
+    my_tiles = virt_idx * slab + jnp.arange(slab, dtype=jnp.int32)
+    bits = []
+    b = n_virt // 2
+    while b >= 1:
+        bits.append(b)
+        b //= 2
 
-    my_tiles = virt_idx * slab + jnp.arange(slab, dtype=jnp.int32)
-    one_hot = (blk_tiles[:, 1][:, None] == my_tiles[None, :]).astype(jnp.bfloat16)
-    ladder = jnp.einsum(
-        "rpo,rt->pto", received, one_hot, preferred_element_type=jnp.float32
-    )
+    width = out_cols // N_CHUNK
+    pieces = []
+    for c in range(N_CHUNK):
+        cols = integrals[0, :, c * width:(c + 1) * width]
+        product = jnp.dot(chosen, cols, preferred_element_type=jnp.float32)
+        product = (product * own_mask).astype(jnp.bfloat16)
+        held = lax.all_to_all(
+            product.reshape(n_pair, p_grp, width), "pair", 0, 0, tiled=True
+        )
+        blocks = [held]
+        srcs = [virt_idx]
+        for bit in bits:
+            perm = [(v, v ^ bit) for v in range(n_virt)]
+            got = [lax.ppermute(x, "virt", perm) for x in blocks]
+            blocks = blocks + got
+            srcs = srcs + [s ^ bit for s in srcs]
+        allb = jnp.concatenate(blocks, axis=0)
+        src_tiles = jnp.concatenate([jnp.take(tout, s, axis=1) for s in srcs])
+        one_hot = (src_tiles[:, None] == my_tiles[None, :]).astype(jnp.bfloat16)
+        pieces.append(
+            jnp.einsum("rpo,rt->pto", allb, one_hot, preferred_element_type=jnp.float32)
+        )
+    ladder = jnp.concatenate(pieces, axis=2) if N_CHUNK > 1 else pieces[0]
     return (ladder + onebody).astype(jnp.bfloat16)
 
 

time: 75.8 us -> 71.2 us (0.939)
  starting transfers between devices: 14.4 us -> 20 us
  waiting for transfers between devices: 29.6 us -> 24.1 us
  local copies, waits for them, and re-layouts: 11.9 us -> 8.86 us
  between operations: 3.27 us -> 0.7 us
  matrix products: 13.3 us -> 14.1 us
    all_to_all x1 -> x2, waiting for transfers between devices: 22.2 us -> 6.21 us  [per_device(): lax.all_to_all(product.reshape(n_pair, p_grp, width), 'pair', 0, 0, tiled...]
    all_to_all x1, waiting for transfers between devices: 7.37 us -> 13.1 us  [per_device(): chosen = lax.all_to_all(picked, ('pair', 'virt'), 0, 0, tiled=True)]
    all_to_all x1 -> x2, starting transfers between devices: 3.62 us -> 7.64 us  [per_device(): lax.all_to_all(product.reshape(n_pair, p_grp, width), 'pair', 0, 0, tiled...]
    all_to_all x1, waiting for transfers between devices: 0.01 us -> 2.9 us  [per_device(): lax.all_to_all(amps_pm[:, :, :out_cols], 'virt', split_axis=1, concat_axi...]
    ppermute x0 -> x6, waiting for transfers between devices: none -> 1.89 us  [per_device(): got = [lax.ppermute(x, 'virt', perm) for x in blocks]]
    ppermute x0 -> x6, starting transfers between devices: none -> 1.56 us  [per_device(): got = [lax.ppermute(x, 'virt', perm) for x in blocks]]
    mul x1 -> x0, other arithmetic: 1.17 us -> none  [per_device(): product.reshape(n_pair, 1, p_grp, out_cols) * select[None, :, None, None]]
    slice x1 -> x2, local copies, waits for them, and re-layouts: 1.08 us -> 0.01 us  [per_device(): amps_pm[:, :, :out_cols]]
  transfers between devices with their start and end apart: 3 -> 10, of which waited for: 2 -> 5; matrix products, arithmetic and copies ran while one was open for 25% -> 27% of each run, Pallas kernels for 0% -> 0%
where the time goes in v2:
time: 71.2 us; the launch traced here: 70.6 us
  waiting for transfers between devices  24.1 us (34%)
  starting transfers between devices  20 us (28%)
  matrix products  14.1 us (20%)
  local copies, waits for them, and re-layouts  8.86 us (12%)
  other arithmetic  2.83 us (4%)
    all_to_all x1, waiting for transfers between devices, per_device(): chosen = lax.all_to_all(picked, ('pair', 'virt'), 0, 0, tiled=True)  13.1 us
    dot_general x2, matrix products, per_device(): product = jnp.dot(chosen, cols, preferred_element_type=jnp.float32)  11.3 us
    all_to_all x2, starting transfers between devices, per_device(): lax.all_to_all(product.reshape(n_pair, p_grp, width), 'pair', 0, 0, tiled...  7.64 us
    all_to_all x1, starting transfers between devices, per_device(): chosen = lax.all_to_all(picked, ('pair', 'virt'), 0, 0, tiled=True)  7.33 us
    all_to_all x2, waiting for transfers between devices, per_device(): lax.all_to_all(product.reshape(n_pair, p_grp, width), 'pair', 0, 0, tiled...  6.21 us
    all_to_all x1, starting transfers between devices, per_device(): lax.all_to_all(amps_pm[:, :, :out_cols], 'virt', split_axis=1, concat_axi...  3.47 us
    all_to_all x1, waiting for transfers between devices, per_device(): lax.all_to_all(amps_pm[:, :, :out_cols], 'virt', split_axis=1, concat_axi...  2.9 us
    gather x1, local copies, waits for them, and re-layouts, per_device(): picked = jnp.take(amps_pm, tin_all, axis=1)  2.54 us
  transfers between devices with their start and end apart: 10, of which 5 were waited for; matrix products, arithmetic and copies ran while one was open for 27% of the time, Pallas kernels for 0%

profile of v2, /device:TPU:0, one launch (start us, length us, event | category | flops | bytes accessed | tf_op | source)
XLA Modules:
  0.0 70.6 jit_solution(15099087334603745560)
XLA Ops:
  0.0 0.8 %slice_reduce_fusion = (s32[32]{0:T(128)S(1)}, s32[32]{0:T(128)S(1)}) fusion(s32[32,2]{0,1:T(2,128)} %param.10), kind=kLoop, calls=%fused_computation.52 | loop fusion | flops 96 | bytes 512 | tf_op jit(solution)/shard_map/slice | solution.py:41
  0.8 0.7 and_bitcast_fusion
  1.5 2.5 %gather_fusion = bf16[32,2,4096]{2,0,1:T(8,128)(2,1)S(1)} fusion(bf16[2,64,4096]{2,1,0:T(8,128)(2,1)} %param.7, s32[1024]{0:T(1024)S(1)} %pad_clamp_fusion), kind=kCustom, calls=%fused_computation | custom fusion | bytes 1048704 | tf_op jit(solution)/shard_map/jit(_take)/gather | solution.py:24
  4.0 0.1 broadcast_select_fusion
  4.1 1.3 %copy.17 = bf16[32,2,4096]{2,1,0:T(2,128)(2,1)} copy(bf16[32,2,4096]{2,0,1:T(8,128)(2,1)S(1)} %broadcast_select_fusion) | data formatting | bytes 1048576 | tf_op jit(solution)/shard_map/jit(_take)/select_n | solution.py:24
  5.5 7.3 %all-to-all-start = ((bf16[32,2,4096]{2,1,0:T(2,128)(2,1)}), bf16[32,2,4096]{2,1,0:T(2,128)(2,1)S(1)}, u32[]{:S(2)}, u32[]{:S(2)}) async-start(bf16[32,2,4096]{2,1,0:T(2,128)(2,1)} %copy.17), calls=%async_computation | async-start | bytes 1048576 | tf_op jit(solution)/shard_map/all_to_all | solution.py:26
  12.8 1.3 %copy.32 = bf16[2,64,2048]{2,0,1:T(2,128)(2,1)} copy(bf16[2,64,2048]{2,1,0:T(8,128)(2,1)S(1)} %slice-done) | data formatting | bytes 1048576
  14.1 0.6 dynamic_slice.4
  15.3 13.1 %all-to-all-done = bf16[32,2,4096]{2,1,0:T(2,128)(2,1)S(1)} async-done(((bf16[32,2,4096]{2,1,0:T(2,128)(2,1)}), bf16[32,2,4096]{2,1,0:T(2,128)(2,1)S(1)}, u32[]{:S(2)}, u32[]{:S(2)}) %all-to-all-start) | async-done | bytes 524320 | tf_op jit(solution)/shard_map/all_to_all | solution.py:26
  28.4 3.5 %all-to-all-start.3 = ((bf16[2,64,2048]{2,0,1:T(2,128)(2,1)}), bf16[2,64,2048]{2,0,1:T(2,128)(2,1)S(1)}, u32[]{:S(2)}, u32[]{:S(2)}) async-start(bf16[2,64,2048]{2,0,1:T(2,128)(2,1)} %copy.32), calls=%async_computation.3 | async-start | bytes 1048576 | tf_op jit(solution)/shard_map/all_to_all | solution.py:29
  31.9 0.2 reshape.30
  32.1 5.7 %fusion.21 = bf16[8,8,1024]{2,1,0:T(8,128)(2,1)} fusion(bf16[64,4096]{1,0:T(8,128)(2,1)S(1)} %reshape.30, bf16[1,4096,2048]{2,1,0:T(8,128)(2,1)} %param.8, f32[]{:T(128)} %bitcast.4), kind=kOutput, calls=%fused_computation.15 | convolution fusion | flops 537001984 | bytes 9044480 | tf_op jit(solution)/shard_map/dot_general | solution.py:53
  37.8 2.9 %all-to-all-done.3 = bf16[2,64,2048]{2,0,1:T(2,128)(2,1)S(1)} async-done(((bf16[2,64,2048]{2,0,1:T(2,128)(2,1)}), bf16[2,64,2048]{2,0,1:T(2,128)(2,1)S(1)}, u32[]{:S(2)}, u32[]{:S(2)}) %all-to-all-start.3) | async-done | bytes 524320 | tf_op jit(solution)/shard_map/all_to_all | solution.py:29
  40.7 3.4 %all-to-all-start.2 = ((bf16[8,8,1024]{2,1,0:T(8,128)(2,1)}), bf16[8,8,1024]{2,1,0:T(8,128)(2,1)S(1)}, u32[]{:S(2)}, u32[]{:S(2)}) async-start(bf16[8,8,1024]{2,1,0:T(8,128)(2,1)} %fusion.21), calls=%async_computation.2 | async-start | bytes 262144 | tf_op jit(solution)/shard_map/all_to_all | solution.py:55
  44.0 5.6 %fusion.18 = bf16[8,8,1024]{2,1,0:T(8,128)(2,1)} fusion(bf16[64,4096]{1,0:T(8,128)(2,1)S(1)} %reshape.30, bf16[1,4096,2048]{2,1,0:T(8,128)(2,1)} %param.8, f32[]{:T(128)} %bitcast.4), kind=kOutput, calls=%fused_computation.14 | convolution fusion | flops 537001984 | bytes 9044480 | tf_op jit(solution)/shard_map/dot_general | solution.py:53
  49.7 1.7 %all-to-all-done.2 = bf16[8,8,1024]{2,1,0:T(8,128)(2,1)S(1)} async-done(((bf16[8,8,1024]{2,1,0:T(8,128)(2,1)}), bf16[8,8,1024]{2,1,0:T(8,128)(2,1)S(1)}, u32[]{:S(2)}, u32[]{:S(2)}) %all-to-all-start.2) | async-done | bytes 131104 | tf_op jit(solution)/shard_map/all_to_all | solution.py:55
  51.3 4.3 %all-to-all-start.1 = ((bf16[8,8,1024]{2,1,0:T(8,128)(2,1)}), bf16[8,8,1024]{2,1,0:T(8,128)(2,1)S(1)}, u32[]{:S(2)}, u32[]{:S(2)}) async-start(bf16[8,8,1024]{2,1,0:T(8,128)(2,1)} %fusion.18), calls=%async_computation.1 | async-start | bytes 262144 | tf_op jit(solution)/shard_map/all_to_all | solution.py:55
  55.7 0.5 collective-permute-start.3
  56.1 0.5 reshape.33
  56.8 0.2 select_reduce_fusion.3
  57.1 0.2 copy.36
  57.2 1.1 %reshape.139 = bf16[8,2,8,32,64,1]{4,3,2,1,0,5:T(8,128)(2,1)S(1)} reshape(bf16[4,2,16,2048]{3,2,1,0:T(8,128)(2,1)S(1)} %bitcast.53) | data formatting | bytes 1048576 | tf_op jit(solution)/shard_map/reshape | solution.py:32
  58.4 4.5 %all-to-all-done.1 = bf16[8,8,1024]{2,1,0:T(8,128)(2,1)S(1)} async-done(((bf16[8,8,1024]{2,1,0:T(8,128)(2,1)}), bf16[8,8,1024]{2,1,0:T(8,128)(2,1)S(1)}, u32[]{:S(2)}, u32[]{:S(2)}) %all-to-all-start.1) | async-done | bytes 131104 | tf_op jit(solution)/shard_map/all_to_all | solution.py:55
  63.0 0.5 collective-permute-start
  63.5 1.3 %convolution_bitcast_fusion = f32[8,2,8,32,64]{4,3,1,0,2:T(8,128)S(1)} fusion(bf16[8,2,8,32,64,1]{4,3,2,1,0,5:T(8,128)(2,1)S(1)} %reshape.139, bf16[8,64,8,64,1,1]{3,2,1,0,5,4:T(8,128)(2,1)S(1)} %bitcast.55), kind=kOutput, calls=%fused_computation.7 | convolution fusion | flops 268435456 | bytes 2097152 | tf_op jit(solution)/shard_map/pkqsd,bjqd->pkbsj/dot_general | solution.py:34
  64.8 0.2 copy.27
  65.0 0.7 reshape.35
  65.6 0.6 collective-permute-start.1
  66.2 1.9 %collective-permute-done = bf16[8,8,1024]{2,0,1:T(8,128)(2,1)S(1)} collective-permute-done((bf16[8,8,1024]{2,0,1:T(8,128)(2,1)S(1)}, bf16[8,8,1024]{2,0,1:T(8,128)(2,1)S(1)}, u32[]{:S(2)}, u32[]{:S(2)}) %collective-permute-start) | collective-permute-done | bytes 131104 | tf_op jit(solution)/shard_map/ppermute | solution.py:62
  68.1 1.3 %convolution_bitcast_fusion.1 = f32[8,16,1024]{2,1,0:T(8,128)S(1)} fusion(bf16[8,8,1024]{2,0,1:T(8,128)(2,1)} %collective-permute-done.5, bf16[8,8,1024]{2,0,1:T(8,128)(2,1)} %collective-permute-done.4, bf16[8,8,1024]{2,0,1:T(8,128)(2,1)} %collective-permute-done.3, bf16[8,8,1024]{2,0,1:T(8,128)(2,1)S(1)} %copy.23, s32[32]{0:T(128)S(1)} %pad_add_fusion, ...), kind=kOutput, calls=%fused_computation.8 | convolution fusion | flops 10486272 | bytes 1048768 | tf_op jit(solution)/shard_map/rpo,rt->pto/dot_general | solution.py:69
  69.4 0.3 convolution_bitcast_fusion.2
  69.7 0.9 %fusion.24 = bf16[8,16,2048]{2,1,0:T(8,128)(2,1)} fusion(f32[8,16,2048]{2,1,0:T(8,128)S(1)} %reshape.35, f32[8,16,1024]{2,1,0:T(8,128)S(1)} %convolution_bitcast_fusion.1, f32[8,16,1024]{2,1,0:T(8,128)S(1)} %convolution_bitcast_fusion.2), kind=kLoop, calls=%fused_computation.17 | loop fusion | flops 786432 | bytes 2621440 | tf_op jit(solution)/shard_map/convert_element_type | solution.py:72
  (20 shorter events, 0.4 us)
Async XLA Ops:
  0.0 12.8 %slice-start = ((bf16[2,64,4096]{2,1,0:T(8,128)(2,1)}), bf16[2,64,2048]{2,1,0:T(8,128)(2,1)S(1)}, s32[]{:S(2)}) async-start(bf16[2,64,4096]{2,1,0:T(8,128)(2,1)} %param.7), calls=%async_computation.4 | async-start | bytes 1048576 | tf_op jit(solution)/shard_map/slice | solution.py:30
  0.0 14.1 %copy-start.1 = (s32[32]{0:T(128)S(1)}, s32[32]{0:T(128)}, u32[]{:S(2)}) copy-start(s32[32]{0:T(128)} %param.11) | copy-start | bytes 388
  5.5 22.9 %all-to-all-start = ((bf16[32,2,4096]{2,1,0:T(2,128)(2,1)}), bf16[32,2,4096]{2,1,0:T(2,128)(2,1)S(1)}, u32[]{:S(2)}, u32[]{:S(2)}) async-start(bf16[32,2,4096]{2,1,0:T(2,128)(2,1)} %copy.17), calls=%async_computation | async-start | bytes 1048576 | tf_op jit(solution)/shard_map/all_to_all | solution.py:26
  28.4 12.3 %all-to-all-start.3 = ((bf16[2,64,2048]{2,0,1:T(2,128)(2,1)}), bf16[2,64,2048]{2,0,1:T(2,128)(2,1)S(1)}, u32[]{:S(2)}, u32[]{:S(2)}) async-start(bf16[2,64,2048]{2,0,1:T(2,128)(2,1)} %copy.32), calls=%async_computation.3 | async-start | bytes 1048576 | tf_op jit(solution)/shard_map/all_to_all | solution.py:29
  32.1 24.0 %copy-start = (bf16[512,512]{1,0:T(8,128)(2,1)S(1)}, bf16[512,512]{1,0:T(8,128)(2,1)}, u32[]{:S(2)}) copy-start(bf16[512,512]{1,0:T(8,128)(2,1)} %param.9) | copy-start | bytes 1572868
  40.7 10.7 %all-to-all-start.2 = ((bf16[8,8,1024]{2,1,0:T(8,128)(2,1)}), bf16[8,8,1024]{2,1,0:T(8,128)(2,1)S(1)}, u32[]{:S(2)}, u32[]{:S(2)}) async-start(bf16[8,8,1024]{2,1,0:T(8,128)(2,1)} %fusion.21), calls=%async_computation.2 | async-start | bytes 262144 | tf_op jit(solution)/shard_map/all_to_all | solution.py:55
  51.3 11.6 %all-to-all-start.1 = ((bf16[8,8,1024]{2,1,0:T(8,128)(2,1)}), bf16[8,8,1024]{2,1,0:T(8,128)(2,1)S(1)}, u32[]{:S(2)}, u32[]{:S(2)}) async-start(bf16[8,8,1024]{2,1,0:T(8,128)(2,1)} %fusion.18), calls=%async_computation.1 | async-start | bytes 262144 | tf_op jit(solution)/shard_map/all_to_all | solution.py:55
  55.7 7.8 %collective-permute-start.3 = (bf16[8,8,1024]{2,0,1:T(8,128)(2,1)S(1)}, bf16[8,8,1024]{2,0,1:T(8,128)(2,1)}, u32[]{:S(2)}, u32[]{:S(2)}) collective-permute-start(bf16[8,8,1024]{2,0,1:T(8,128)(2,1)S(1)} %copy.23), channel_id=1, source_target_pairs={{0,2},{1,3},{2,0},{3,1},{4,6},{5,7},{6,4},{7,5},{8,10},{9,11},{10,... | collective-permute-start | bytes 393224 | tf_op jit(solution)/shard_map/ppermute | solution.py:62
  58.3 9.7 %collective-permute-start.4 = (bf16[8,8,1024]{2,0,1:T(8,128)(2,1)S(1)}, bf16[8,8,1024]{2,0,1:T(8,128)(2,1)}, u32[]{:S(2)}, u32[]{:S(2)}) collective-permute-start(bf16[8,8,1024]{2,0,1:T(8,128)(2,1)S(1)} %copy.23), channel_id=1, source_target_pairs={{0,1},{1,0},{2,3},{3,2},{4,5},{5,4},{6,7},{7,6},{8,9},{9,8},{10,11... | collective-permute-start | bytes 393224 | tf_op jit(solution)/shard_map/ppermute | solution.py:62
  63.0 5.0 %collective-permute-start = (bf16[8,8,1024]{2,0,1:T(8,128)(2,1)S(1)}, bf16[8,8,1024]{2,0,1:T(8,128)(2,1)S(1)}, u32[]{:S(2)}, u32[]{:S(2)}) collective-permute-start(bf16[8,8,1024]{2,0,1:T(8,128)(2,1)S(1)} %copy.20), channel_id=1, source_target_pairs={{0,2},{1,3},{2,0},{3,1},{4,6},{5,7},{6,4},{7,5},{8,10},{9,11},{10,... | collective-permute-start | bytes 393224 | tf_op jit(solution)/shard_map/ppermute | solution.py:62
  63.5 4.6 %collective-permute-start.5 = (bf16[8,8,1024]{2,0,1:T(8,128)(2,1)}, bf16[8,8,1024]{2,0,1:T(8,128)(2,1)}, u32[]{:S(2)}, u32[]{:S(2)}) collective-permute-start(bf16[8,8,1024]{2,0,1:T(8,128)(2,1)} %collective-permute-done.3), channel_id=1, source_target_pairs={{0,1},{1,0},{2,3},{3,2},{4,5},{5,4},{6,7},{7,6},{8,9},{9,8},{10,11... | collective-permute-start | bytes 393224 | tf_op jit(solution)/shard_map/ppermute | solution.py:62
  65.6 3.7 %collective-permute-start.1 = (bf16[8,8,1024]{2,0,1:T(8,128)(2,1)S(1)}, bf16[8,8,1024]{2,0,1:T(8,128)(2,1)S(1)}, u32[]{:S(2)}, u32[]{:S(2)}) collective-permute-start(bf16[8,8,1024]{2,0,1:T(8,128)(2,1)S(1)} %copy.20), channel_id=1, source_target_pairs={{0,1},{1,0},{2,3},{3,2},{4,5},{5,4},{6,7},{7,6},{8,9},{9,8},{10,11... | collective-permute-start | bytes 393224 | tf_op jit(solution)/shard_map/ppermute | solution.py:62
  68.1 1.3 %collective-permute-start.2 = (bf16[8,8,1024]{2,0,1:T(8,128)(2,1)S(1)}, bf16[8,8,1024]{2,0,1:T(8,128)(2,1)S(1)}, u32[]{:S(2)}, u32[]{:S(2)}) collective-permute-start(bf16[8,8,1024]{2,0,1:T(8,128)(2,1)S(1)} %collective-permute-done), channel_id=1, source_target_pairs={{0,1},{1,0},{2,3},{3,2},{4,5},{5,4},{6,7},{7,6},{8,9},{9,8},{10,11... | collective-permute-start | bytes 393224 | tf_op jit(solution)/shard_map/ppermute | solution.py:62

commit v3 on v2

--- a/solution.py
+++ b/solution.py
@@ -6,7 +6,7 @@
 TILE = 64
 NVT = 8
 AS = 32
-N_CHUNK = 2
+N_CHUNK = 1
 
 
 def per_device(amps_pm, integrals, fock_vv, blk_tiles, blk_mask):
@@ -21,14 +21,24 @@
     p_grp = pm_rows * n_virt
 
     tin_all = blk_tiles[:, 0]
-    picked = jnp.take(amps_pm, tin_all, axis=1)
-    picked = jnp.transpose(picked, (1, 0, 2))
+    tile_ids = jnp.arange(n_tiles, dtype=jnp.int32)
+    pick = (tin_all[:, None] == tile_ids[None, :]).astype(amps_pm.dtype)
+    picked = jnp.einsum(
+        "dt,itc->dic", pick, amps_pm, preferred_element_type=jnp.float32
+    ).astype(amps_pm.dtype)
     chosen = lax.all_to_all(picked, ("pair", "virt"), 0, 0, tiled=True)
     chosen = chosen.reshape(n_dev * pm_rows, tile_len)
 
-    sub = lax.all_to_all(
-        amps_pm[:, :, :out_cols], "virt", split_axis=1, concat_axis=0, tiled=True
-    )
+    got = [lax.dynamic_slice_in_dim(amps_pm[:, :, :out_cols], virt_idx * slab, slab, 1)]
+    for k in range(1, n_virt):
+        part = lax.dynamic_slice_in_dim(
+            amps_pm[:, :, :out_cols], ((virt_idx + k) % n_virt) * slab, slab, 1
+        )
+        perm = [(u, (u + k) % n_virt) for u in range(n_virt)]
+        got.append(lax.ppermute(part, "virt", perm))
+    stacked = jnp.stack(got)
+    order = (virt_idx - jnp.arange(n_virt, dtype=jnp.int32)) % n_virt
+    sub = jnp.take(stacked, order, axis=0)
     sub = sub.reshape(p_grp, slab // NVT, NVT, AS, TILE)
     fock_four = fock_vv.reshape(NVT, TILE, NVT, TILE)
     onebody = jnp.einsum(

time: 71.2 us -> 61.9 us (0.87)
  starting transfers between devices: 20 us -> 13.9 us
  other arithmetic: 2.83 us -> 0.41 us
  matrix products: 14.1 us -> 15.9 us
  local copies, waits for them, and re-layouts: 8.86 us -> 7.22 us
  waiting for transfers between devices: 24.1 us -> 23.2 us
    all_to_all x2 -> x1, starting transfers between devices: 7.64 us -> 3.54 us  [per_device(): lax.all_to_all(product.reshape(n_pair, p_grp, width), 'pair', 0, 0, tiled...]
    all_to_all x1 -> x0, starting transfers between devices: 3.47 us -> none  [per_device(): lax.all_to_all(amps_pm[:, :, :out_cols], 'virt', split_axis=1, concat_axi...]
    all_to_all x1 -> x0, waiting for transfers between devices: 2.9 us -> none  [per_device(): lax.all_to_all(amps_pm[:, :, :out_cols], 'virt', split_axis=1, concat_axi...]
    dot_general x2 -> x1, matrix products: 11.3 us -> 9.56 us  [per_device(): product = jnp.dot(chosen, cols, preferred_element_type=jnp.float32)]
    ppermute x0 -> x3, starting transfers between devices: none -> 1.58 us  [per_device(): got.append(lax.ppermute(part, 'virt', perm))]
    dot_general x0 -> x1, matrix products: none -> 1.58 us  [per_device(): jnp.einsum('dt,itc->dic', pick, amps_pm, preferred_element_type=jnp.float32)]
    convert_element_type x0 -> x1, local copies, waits for them, and re-layouts: none -> 1.34 us  [per_device(): picked = jnp.einsum('dt,itc->dic', pick, amps_pm, preferred_element_type=...]
    unnamed x5 -> x4, local copies, waits for them, and re-layouts: 1.34 us -> 0.01 us
  transfers between devices with their start and end apart: 10 -> 8, of which waited for: 5 -> 3; matrix products, arithmetic and copies ran while one was open for 27% -> 13% of each run, Pallas kernels for 0% -> 0%
where the time goes in v3:
time: 61.9 us; the launch traced here: 61.5 us
  waiting for transfers between devices  23.2 us (37%)
  matrix products  15.9 us (26%)
  starting transfers between devices  13.9 us (22%)
  local copies, waits for them, and re-layouts  7.22 us (12%)
  between operations  0.9 us (1%)
    all_to_all x1, waiting for transfers between devices, per_device(): chosen = lax.all_to_all(picked, ('pair', 'virt'), 0, 0, tiled=True)  14.3 us
    dot_general x1, matrix products, per_device(): product = jnp.dot(chosen, cols, preferred_element_type=jnp.float32)  9.56 us
    all_to_all x1, starting transfers between devices, per_device(): chosen = lax.all_to_all(picked, ('pair', 'virt'), 0, 0, tiled=True)  7.33 us
    all_to_all x1, waiting for transfers between devices, per_device(): lax.all_to_all(product.reshape(n_pair, p_grp, width), 'pair', 0, 0, tiled...  7.1 us
    all_to_all x1, starting transfers between devices, per_device(): lax.all_to_all(product.reshape(n_pair, p_grp, width), 'pair', 0, 0, tiled...  3.54 us
    gather x2, local copies, waits for them, and re-layouts, per_device(): sub = jnp.take(stacked, order, axis=0)  2.62 us
    dot_general x1, matrix products, per_device(): jnp.einsum('pkqsd,bjqd->pkbsj', sub, fock_four, preferred_element_type=jn...  2.51 us
    dot_general x1, matrix products, per_device(): jnp.einsum('rpo,rt->pto', allb, one_hot, preferred_element_type=jnp.float32)  2.26 us
  transfers between devices with their start and end apart: 8, of which 3 were waited for; matrix products, arithmetic and copies ran while one was open for 13% of the time, Pallas kernels for 0%

profile of v3, /device:TPU:0, one launch (start us, length us, event | category | flops | bytes accessed | tf_op | source)
XLA Modules:
  0.0 61.5 jit_solution(15881261445038326103)
XLA Ops:
  0.0 0.8 %slice_reduce_fusion = (s32[32]{0:T(128)S(1)}, s32[32]{0:T(128)S(1)}) fusion(s32[32,2]{0,1:T(2,128)} %param.10), kind=kLoop, calls=%fused_computation.55 | loop fusion | bytes 512 | tf_op jit(solution)/shard_map/slice | solution.py:51
  0.8 1.6 %convolution_convert_fusion = bf16[32,2,4096]{2,0,1:T(8,128)(2,1)S(1)} fusion(bf16[2,64,4096]{2,1,0:T(8,128)(2,1)} %param.7, s32[32]{0:T(128)S(1)} %get-tuple-element.26), kind=kOutput, calls=%fused_computation.3 | convolution fusion | flops 33818624 | bytes 1572992 | tf_op jit(solution)/shard_map/dt,itc->dic/dot_general | solution.py:26
  2.4 1.3 %copy.11 = bf16[32,2,4096]{2,1,0:T(2,128)(2,1)} copy(bf16[32,2,4096]{2,0,1:T(8,128)(2,1)S(1)} %convolution_convert_fusion) | data formatting | bytes 1048576 | tf_op jit(solution)/shard_map/convert_element_type | solution.py:28
  3.7 7.3 %all-to-all-start = ((bf16[32,2,4096]{2,1,0:T(2,128)(2,1)}), bf16[32,2,4096]{2,1,0:T(2,128)(2,1)S(1)}, u32[]{:S(2)}, u32[]{:S(2)}) async-start(bf16[32,2,4096]{2,1,0:T(2,128)(2,1)} %copy.11), calls=%async_computation | async-start | bytes 1048576 | tf_op jit(solution)/shard_map/all_to_all | solution.py:29
  11.1 0.7 %dynamic_slice.16 = s32[1]{0:T(128)} dynamic-slice(s32[32]{0:T(128)S(1)} %copy-done.1, s32[]{:T(128)S(6)} %select_n.75), dynamic_slice_sizes={1} | dynamic-slice | bytes 12 | tf_op jit(solution)/shard_map/jit(dynamic_index_in_dim)/dynamic_slice | solution.py:48
  12.4 14.3 %all-to-all-done = bf16[32,2,4096]{2,1,0:T(2,128)(2,1)S(1)} async-done(((bf16[32,2,4096]{2,1,0:T(2,128)(2,1)}), bf16[32,2,4096]{2,1,0:T(2,128)(2,1)S(1)}, u32[]{:S(2)}, u32[]{:S(2)}) %all-to-all-start) | async-done | bytes 524320 | tf_op jit(solution)/shard_map/all_to_all | solution.py:29
  26.7 0.2 reshape.76
  26.9 0.0 slice-start
  26.9 9.6 %fusion.10 = bf16[8,8,2048]{2,1,0:T(8,128)(2,1)} fusion(bf16[64,4096]{1,0:T(8,128)(2,1)S(1)} %reshape.76, bf16[1,4096,2048]{2,1,0:T(8,128)(2,1)} %param.8, f32[]{:T(128)} %bitcast.4), kind=kOutput, calls=%fused_computation.9 | convolution fusion | flops 1074003968 | bytes 17563652 | tf_op jit(solution)/shard_map/dot_general | solution.py:63
  36.4 3.5 %all-to-all-start.1 = ((bf16[8,8,2048]{2,1,0:T(8,128)(2,1)}), bf16[8,8,2048]{2,1,0:T(8,128)(2,1)S(1)}, u32[]{:S(2)}, u32[]{:S(2)}) async-start(bf16[8,8,2048]{2,1,0:T(8,128)(2,1)} %fusion.10), calls=%async_computation.1 | async-start | bytes 524288 | tf_op jit(solution)/shard_map/all_to_all | solution.py:65
  40.0 0.1 dynamic-slice_bitcast_fusion
  40.0 0.9 %collective-permute-start.5 = (bf16[2,16,2048]{2,1,0:T(8,128)(2,1)S(1)}, bf16[2,16,2048]{2,1,0:T(8,128)(2,1)S(1)}, u32[]{:S(2)}, u32[]{:S(2)}) collective-permute-start(bf16[2,16,2048]{2,1,0:T(8,128)(2,1)S(1)} %get-tuple-element.22), channel_id=1, source_target_pairs={{0,3},{1,0},{2,1},{3,2},{4,7},{5,4},{6,5},{7,6},{8,11},{9,8},{10,9... | collective-permute-start | bytes 393224 | tf_op jit(solution)/shard_map/ppermute | solution.py:38
  40.9 0.0 collective-permute-start.3
  40.9 0.7 %collective-permute-start.4 = (bf16[2,16,2048]{2,1,0:T(8,128)(2,1)S(1)}, bf16[2,16,2048]{2,1,0:T(8,128)(2,1)S(1)}, u32[]{:S(2)}, u32[]{:S(2)}) collective-permute-start(bf16[2,16,2048]{2,1,0:T(8,128)(2,1)S(1)} %get-tuple-element.23), channel_id=1, source_target_pairs={{0,2},{1,3},{2,0},{3,1},{4,6},{5,7},{6,4},{7,5},{8,10},{9,11},{10,... | collective-permute-start | bytes 393224 | tf_op jit(solution)/shard_map/ppermute | solution.py:38
  41.7 0.1 reshape_squeeze.3
  41.8 0.2 select_reduce_fusion.3
  42.0 7.1 %all-to-all-done.1 = bf16[8,8,2048]{2,1,0:T(8,128)(2,1)S(1)} async-done(((bf16[8,8,2048]{2,1,0:T(8,128)(2,1)}), bf16[8,8,2048]{2,1,0:T(8,128)(2,1)S(1)}, u32[]{:S(2)}, u32[]{:S(2)}) %all-to-all-start.1) | async-done | bytes 262176 | tf_op jit(solution)/shard_map/all_to_all | solution.py:65
  49.1 0.1 copy.14
  49.3 1.4 %collective-permute-start = (bf16[8,8,2048]{2,0,1:T(8,128)(2,1)S(1)}, bf16[8,8,2048]{2,0,1:T(8,128)(2,1)}, u32[]{:S(2)}, u32[]{:S(2)}) collective-permute-start(bf16[8,8,2048]{2,0,1:T(8,128)(2,1)S(1)} %copy.14), channel_id=1, source_target_pairs={{0,2},{1,3},{2,0},{3,1},{4,6},{5,7},{6,4},{7,5},{8,10},{9,11},{10,... | collective-permute-start | bytes 786440 | tf_op jit(solution)/shard_map/ppermute | solution.py:72
  50.7 0.1 pad_add_fusion
  50.8 0.1 broadcast_in_dim.23
  50.9 0.1 broadcast_in_dim.24
  51.0 0.5 reshape.78
  51.5 0.0 collective-permute-done.5
  51.5 0.1 pad_maximum_fusion
  51.6 0.6 gather_fusion
  52.2 2.0 %gather.10 = bf16[8,2,8,32,64]{4,3,2,1,0:T(8,128)(2,1)} reshape(bf16[4,2,16,2048]{3,2,1,0:T(8,128)(2,1)S(1)} %gather_fusion) | data formatting | bytes 1048576 | tf_op jit(solution)/shard_map/jit(_take)/gather | solution.py:41
  54.2 1.8 %collective-permute-done = bf16[8,8,2048]{2,0,1:T(8,128)(2,1)} collective-permute-done((bf16[8,8,2048]{2,0,1:T(8,128)(2,1)S(1)}, bf16[8,8,2048]{2,0,1:T(8,128)(2,1)}, u32[]{:S(2)}, u32[]{:S(2)}) %collective-permute-start) | collective-permute-done | bytes 262176 | tf_op jit(solution)/shard_map/ppermute | solution.py:72
  56.0 0.0 collective-permute-start.2
  56.0 2.5 %convolution_bitcast_fusion.1 = f32[8,2,8,32,64]{4,3,2,1,0:T(8,128)S(1)} fusion(bf16[8,64,8,64,1,1]{3,2,1,0,5,4:T(8,128)(2,1)S(1)} %bitcast.50, bf16[8,2,8,32,64]{4,3,2,1,0:T(8,128)(2,1)} %gather.10, pred[8]{0:T(512)(128)(4,1)S(1)} %broadcast_in_dim.24), kind=kOutput, calls=%fused_computation.10 | convolution fusion | flops 268697600 | bytes 2097160 | tf_op jit(solution)/shard_map/pkqsd,bjqd->pkbsj/dot_general | solution.py:44
  58.6 0.7 %reshape.79 = f32[8,16,2048]{2,1,0:T(8,128)S(1)} reshape(f32[8,2,8,32,64]{4,3,2,1,0:T(8,128)S(1)} %convolution_bitcast_fusion.1) | data formatting | bytes 2097152 | tf_op jit(solution)/shard_map/reshape | solution.py:46
  59.2 2.3 %fusion.3 = bf16[8,16,2048]{2,1,0:T(8,128)(2,1)} fusion(f32[8,16,2048]{2,1,0:T(8,128)S(1)} %reshape.79, bf16[8,8,2048]{2,0,1:T(8,128)(2,1)} %collective-permute-done.2, bf16[8,8,2048]{2,0,1:T(8,128)(2,1)} %collective-permute-done.1, bf16[8,8,2048]{2,0,1:T(8,128)(2,1)} %collective-permute-done, bf16[8,8,2048]{2,0,1:T(8,128)(2,1)S(1)} %copy.14, ...), kind=kOutput, calls=%fused_computation.6 | convolution fusion | flops 21496320 | bytes 2621632 | tf_op jit(solution)/shard_map/rpo,rt->pto/dot_general | solution.py:79
  (14 shorter events, 0.1 us)
Async XLA Ops:
  0.8 10.3 %copy-start.1 = (s32[32]{0:T(128)S(1)}, s32[32]{0:T(128)}, u32[]{:S(2)}) copy-start(s32[32]{0:T(128)} %param.11) | copy-start | bytes 388
  3.7 23.0 %all-to-all-start = ((bf16[32,2,4096]{2,1,0:T(2,128)(2,1)}), bf16[32,2,4096]{2,1,0:T(2,128)(2,1)S(1)}, u32[]{:S(2)}, u32[]{:S(2)}) async-start(bf16[32,2,4096]{2,1,0:T(2,128)(2,1)} %copy.11), calls=%async_computation | async-start | bytes 1048576 | tf_op jit(solution)/shard_map/all_to_all | solution.py:29
  26.9 13.1 %slice-start = ((bf16[2,64,4096]{2,1,0:T(8,128)(2,1)}), bf16[2,64,2048]{2,1,0:T(8,128)(2,1)S(1)}, s32[]{:S(2)}) async-start(bf16[2,64,4096]{2,1,0:T(8,128)(2,1)} %param.7), calls=%async_computation.2 | async-start | bytes 1048576 | tf_op jit(solution)/shard_map/slice | solution.py:32
  36.4 14.5 %copy-start = (bf16[512,512]{1,0:T(8,128)(2,1)S(1)}, bf16[512,512]{1,0:T(8,128)(2,1)}, u32[]{:S(2)}) copy-start(bf16[512,512]{1,0:T(8,128)(2,1)} %param.9) | copy-start | bytes 1572868
  36.4 12.7 %all-to-all-start.1 = ((bf16[8,8,2048]{2,1,0:T(8,128)(2,1)}), bf16[8,8,2048]{2,1,0:T(8,128)(2,1)S(1)}, u32[]{:S(2)}, u32[]{:S(2)}) async-start(bf16[8,8,2048]{2,1,0:T(8,128)(2,1)} %fusion.10), calls=%async_computation.1 | async-start | bytes 524288 | tf_op jit(solution)/shard_map/all_to_all | solution.py:65
  40.0 11.5 %collective-permute-start.5 = (bf16[2,16,2048]{2,1,0:T(8,128)(2,1)S(1)}, bf16[2,16,2048]{2,1,0:T(8,128)(2,1)S(1)}, u32[]{:S(2)}, u32[]{:S(2)}) collective-permute-start(bf16[2,16,2048]{2,1,0:T(8,128)(2,1)S(1)} %get-tuple-element.22), channel_id=1, source_target_pairs={{0,3},{1,0},{2,1},{3,2},{4,7},{5,4},{6,5},{7,6},{8,11},{9,8},{10,9... | collective-permute-start | bytes 393224 | tf_op jit(solution)/shard_map/ppermute | solution.py:38
  40.9 10.6 %collective-permute-start.3 = (bf16[2,16,2048]{2,1,0:T(8,128)(2,1)S(1)}, bf16[2,16,2048]{2,1,0:T(8,128)(2,1)S(1)}, u32[]{:S(2)}, u32[]{:S(2)}) collective-permute-start(bf16[2,16,2048]{2,1,0:T(8,128)(2,1)S(1)} %get-tuple-element.24), channel_id=1, source_target_pairs={{0,1},{1,2},{2,3},{3,0},{4,5},{5,6},{6,7},{7,4},{8,9},{9,10},{10,1... | collective-permute-start | bytes 393224 | tf_op jit(solution)/shard_map/ppermute | solution.py:38
  40.9 10.6 %collective-permute-start.4 = (bf16[2,16,2048]{2,1,0:T(8,128)(2,1)S(1)}, bf16[2,16,2048]{2,1,0:T(8,128)(2,1)S(1)}, u32[]{:S(2)}, u32[]{:S(2)}) collective-permute-start(bf16[2,16,2048]{2,1,0:T(8,128)(2,1)S(1)} %get-tuple-element.23), channel_id=1, source_target_pairs={{0,2},{1,3},{2,0},{3,1},{4,6},{5,7},{6,4},{7,5},{8,10},{9,11},{10,... | collective-permute-start | bytes 393224 | tf_op jit(solution)/shard_map/ppermute | solution.py:38
  49.3 6.7 %collective-permute-start = (bf16[8,8,2048]{2,0,1:T(8,128)(2,1)S(1)}, bf16[8,8,2048]{2,0,1:T(8,128)(2,1)}, u32[]{:S(2)}, u32[]{:S(2)}) collective-permute-start(bf16[8,8,2048]{2,0,1:T(8,128)(2,1)S(1)} %copy.14), channel_id=1, source_target_pairs={{0,2},{1,3},{2,0},{3,1},{4,6},{5,7},{6,4},{7,5},{8,10},{9,11},{10,... | collective-permute-start | bytes 786440 | tf_op jit(solution)/shard_map/ppermute | solution.py:72
  54.2 5.0 %collective-permute-start.1 = (bf16[8,8,2048]{2,0,1:T(8,128)(2,1)S(1)}, bf16[8,8,2048]{2,0,1:T(8,128)(2,1)}, u32[]{:S(2)}, u32[]{:S(2)}) collective-permute-start(bf16[8,8,2048]{2,0,1:T(8,128)(2,1)S(1)} %copy.14), channel_id=1, source_target_pairs={{0,1},{1,0},{2,3},{3,2},{4,5},{5,4},{6,7},{7,6},{8,9},{9,8},{10,11... | collective-permute-start | bytes 786440 | tf_op jit(solution)/shard_map/ppermute | solution.py:72
  56.0 3.2 %collective-permute-start.2 = (bf16[8,8,2048]{2,0,1:T(8,128)(2,1)}, bf16[8,8,2048]{2,0,1:T(8,128)(2,1)}, u32[]{:S(2)}, u32[]{:S(2)}) collective-permute-start(bf16[8,8,2048]{2,0,1:T(8,128)(2,1)} %collective-permute-done), channel_id=1, source_target_pairs={{0,1},{1,0},{2,3},{3,2},{4,5},{5,4},{6,7},{7,6},{8,9},{9,8},{10,11... | collective-permute-start | bytes 786440 | tf_op jit(solution)/shard_map/ppermute | solution.py:72

commit v4 on v3

--- a/solution.py
+++ b/solution.py
@@ -1,12 +1,58 @@
 import jax
 import jax.numpy as jnp
 from jax import lax
+from jax.experimental import pallas as pl
+from jax.experimental.pallas import tpu as pltpu
 from jax.sharding import PartitionSpec as P
 
 TILE = 64
 NVT = 8
 AS = 32
 N_CHUNK = 1
+TK = 512
+
+
+def _ladder_kernel(mask_ref, a_ref, w_ref, o_ref, acc_ref):
+    k = pl.program_id(0)
+
+    @pl.when(k == 0)
+    def _():
+        acc_ref[...] = jnp.zeros_like(acc_ref)
+
+    start = pl.multiple_of(k * TK, TK)
+    acc_ref[...] += jnp.dot(
+        a_ref[:, pl.ds(start, TK)], w_ref[0], preferred_element_type=jnp.float32
+    )
+
+    @pl.when(k == pl.num_programs(0) - 1)
+    def _():
+        scale = mask_ref[0].astype(jnp.float32)
+        o_ref[...] = (acc_ref[...] * scale).astype(o_ref.dtype)
+
+
+def ladder_matmul(mask, a, w):
+    m, kdim = a.shape
+    n = w.shape[2]
+    return pl.pallas_call(
+        _ladder_kernel,
+        out_shape=jax.ShapeDtypeStruct((m, n), jnp.bfloat16),
+        grid_spec=pltpu.PrefetchScalarGridSpec(
+            num_scalar_prefetch=1,
+            grid=(kdim // TK,),
+            in_specs=[
+                pl.BlockSpec((m, kdim), lambda k, s: (0, 0)),
+                pl.BlockSpec((1, TK, n), lambda k, s: (0, k, 0)),
+            ],
+            out_specs=pl.BlockSpec((m, n), lambda k, s: (0, 0)),
+            scratch_shapes=[pltpu.VMEM((m, n), jnp.float32)],
+        ),
+        compiler_params=pltpu.CompilerParams(dimension_semantics=("arbitrary",)),
+        cost_estimate=pl.CostEstimate(
+            flops=2 * m * kdim * n,
+            transcendentals=0,
+            bytes_accessed=kdim * n * 2 + m * kdim * 2 + m * n * 2,
+        ),
+    )(mask, a, w)
 
 
 def per_device(amps_pm, integrals, fock_vv, blk_tiles, blk_mask):
@@ -38,15 +84,18 @@
         got.append(lax.ppermute(part, "virt", perm))
     stacked = jnp.stack(got)
     order = (virt_idx - jnp.arange(n_virt, dtype=jnp.int32)) % n_virt
-    sub = jnp.take(stacked, order, axis=0)
+    reorder = (order[:, None] == jnp.arange(n_virt, dtype=jnp.int32)[None, :])
+    sub = jnp.einsum(
+        "uk,kptc->uptc", reorder.astype(stacked.dtype), stacked,
+        preferred_element_type=jnp.float32,
+    ).astype(stacked.dtype)
     sub = sub.reshape(p_grp, slab // NVT, NVT, AS, TILE)
     fock_four = fock_vv.reshape(NVT, TILE, NVT, TILE)
     onebody = jnp.einsum(
         "pkqsd,bjqd->pkbsj", sub, fock_four, preferred_element_type=jnp.float32
     ).reshape(p_grp, slab, out_cols)
 
-    own_mask = lax.dynamic_index_in_dim(blk_mask, device, 0, keepdims=False)
-    own_mask = own_mask.astype(jnp.float32)
+    own_mask = lax.dynamic_slice_in_dim(blk_mask, device, 1, 0)
 
     tout = blk_tiles[:, 1].reshape(n_pair, n_virt)
     my_tiles = virt_idx * slab + jnp.arange(slab, dtype=jnp.int32)
@@ -59,9 +108,8 @@
     width = out_cols // N_CHUNK
     pieces = []
     for c in range(N_CHUNK):
-        cols = integrals[0, :, c * width:(c + 1) * width]
-        product = jnp.dot(chosen, cols, preferred_element_type=jnp.float32)
-        product = (product * own_mask).astype(jnp.bfloat16)
+        cols = integrals[:, :, c * width:(c + 1) * width]
+        product = ladder_matmul(own_mask, chosen, cols)
         held = lax.all_to_all(
             product.reshape(n_pair, p_grp, width), "pair", 0, 0, tiled=True
         )

time: 61.9 us -> 64.6 us (1.044)
  Pallas kernels: 0 us -> 11.1 us
  matrix products: 15.9 us -> 7.65 us
  waiting for transfers between devices: 23.2 us -> 21.3 us
  starting transfers between devices: 13.9 us -> 15.2 us
  local copies, waits for them, and re-layouts: 7.22 us -> 8.38 us
    pallas_call x0 -> x1, Pallas kernels: none -> 11.1 us  [ladder_matmul(): pl.pallas_call(_ladder_kernel, out_shape=jax.ShapeDtypeStruct((m, n), jnp...]
    dot_general x1, matrix products: 9.56 us -> 1.33 us  [per_device(): jnp.einsum('uk,kptc->uptc', reorder.astype(stacked.dtype), stacked, prefe...]
    gather x2 -> x0, local copies, waits for them, and re-layouts: 2.62 us -> none  [per_device(): sub = jnp.take(stacked, order, axis=0)]
    reshape x0 -> x1, local copies, waits for them, and re-layouts: none -> 2.04 us  [per_device(): sub = sub.reshape(p_grp, slab // NVT, NVT, AS, TILE)]
    ppermute x3, waiting for transfers between devices: 1.8 us -> 0.14 us  [per_device(): got = [lax.ppermute(x, 'virt', perm) for x in blocks]]
    all_to_all x1, waiting for transfers between devices: 7.1 us -> 6.19 us  [per_device(): lax.all_to_all(product.reshape(n_pair, p_grp, width), 'pair', 0, 0, tiled...]
    ppermute x3, starting transfers between devices: 1.58 us -> 2.49 us  [per_device(): got.append(lax.ppermute(part, 'virt', perm))]
    another operation x1 -> x5, local copies, waits for them, and re-layouts: 0.05 us -> 0.87 us  [per_device(): stacked = jnp.stack(got)]
  transfers between devices with their start and end apart: 8 -> 8, of which waited for: 3 -> 3; matrix products, arithmetic and copies ran while one was open for 13% -> 15% of each run, Pallas kernels for 0% -> 0%
where the time goes in v4:
time: 64.6 us; the launch traced here: 64.1 us
  waiting for transfers between devices  21.3 us (33%)
  starting transfers between devices  15.2 us (24%)
  Pallas kernels  11.1 us (17%)
  local copies, waits for them, and re-layouts  8.38 us (13%)
  matrix products  7.65 us (12%)
    all_to_all x1, waiting for transfers between devices, per_device(): chosen = lax.all_to_all(picked, ('pair', 'virt'), 0, 0, tiled=True)  14.9 us
    pallas_call x1, Pallas kernels, ladder_matmul(): pl.pallas_call(_ladder_kernel, out_shape=jax.ShapeDtypeStruct((m, n), jnp...  11.1 us
    all_to_all x1, starting transfers between devices, per_device(): chosen = lax.all_to_all(picked, ('pair', 'virt'), 0, 0, tiled=True)  7.32 us
    all_to_all x1, waiting for transfers between devices, per_device(): lax.all_to_all(product.reshape(n_pair, p_grp, width), 'pair', 0, 0, tiled...  6.19 us
    all_to_all x1, starting transfers between devices, per_device(): lax.all_to_all(product.reshape(n_pair, p_grp, width), 'pair', 0, 0, tiled...  3.54 us
    ppermute x3, starting transfers between devices, per_device(): got.append(lax.ppermute(part, 'virt', perm))  2.49 us
    dot_general x1, matrix products, per_device(): jnp.einsum('pkqsd,bjqd->pkbsj', sub, fock_four, preferred_element_type=jn...  2.49 us
    dot_general x1, matrix products, per_device(): jnp.einsum('rpo,rt->pto', allb, one_hot, preferred_element_type=jnp.float32)  2.26 us
  transfers between devices with their start and end apart: 8, of which 3 were waited for; matrix products, arithmetic and copies ran while one was open for 15% of the time, Pallas kernels for 0%

profile of v4, /device:TPU:0, one launch (start us, length us, event | category | flops | bytes accessed | tf_op | source)
XLA Modules:
  0.0 64.1 jit_solution(14378182011624623755)
XLA Ops:
  0.0 0.8 %slice_reduce_fusion = (s32[32]{0:T(128)S(1)}, s32[32]{0:T(128)S(1)}) fusion(s32[32,2]{0,1:T(2,128)} %param.10), kind=kLoop, calls=%fused_computation.47 | loop fusion | bytes 512 | tf_op jit(solution)/shard_map/slice | solution.py:100
  0.8 1.6 %convolution_convert_fusion = bf16[32,2,4096]{2,0,1:T(8,128)(2,1)S(1)} fusion(bf16[2,64,4096]{2,1,0:T(8,128)(2,1)} %param.7, s32[32]{0:T(128)S(1)} %get-tuple-element.26), kind=kOutput, calls=%fused_computation | convolution fusion | flops 33818624 | bytes 1572992 | tf_op jit(solution)/shard_map/dt,itc->dic/dot_general | solution.py:72
  2.4 1.3 %copy.33 = bf16[32,2,4096]{2,1,0:T(2,128)(2,1)} copy(bf16[32,2,4096]{2,0,1:T(8,128)(2,1)S(1)} %convolution_convert_fusion) | data formatting | bytes 1048576 | tf_op jit(solution)/shard_map/convert_element_type | solution.py:74
  3.7 7.3 %all-to-all-start = ((bf16[32,2,4096]{2,1,0:T(2,128)(2,1)}), bf16[32,2,4096]{2,1,0:T(2,128)(2,1)S(1)}, u32[]{:S(2)}, u32[]{:S(2)}) async-start(bf16[32,2,4096]{2,1,0:T(2,128)(2,1)} %copy.33), calls=%async_computation | async-start | bytes 1048576 | tf_op jit(solution)/shard_map/all_to_all | solution.py:75
  11.0 0.7 %dynamic_slice.15.mask_ref = s32[1]{0:T(128)} dynamic-slice(s32[32]{0:T(128)S(1)} %copy-done.1, s32[]{:T(128)S(6)} %select_n.46), dynamic_slice_sizes={1} | dynamic-slice | bytes 12 | tf_op jit(solution)/shard_map/dynamic_slice | solution.py:98
  11.7 14.9 %all-to-all-done = bf16[32,2,4096]{2,1,0:T(2,128)(2,1)S(1)} async-done(((bf16[32,2,4096]{2,1,0:T(2,128)(2,1)}), bf16[32,2,4096]{2,1,0:T(2,128)(2,1)S(1)}, u32[]{:S(2)}, u32[]{:S(2)}) %all-to-all-start) | async-done | bytes 524320 | tf_op jit(solution)/shard_map/all_to_all | solution.py:75
  26.6 1.0 %reshape.36.a_ref = bf16[64,4096]{1,0:T(8,128)(2,1)} reshape(bf16[32,2,4096]{2,1,0:T(2,128)(2,1)S(1)} %all-to-all-done) | data formatting | bytes 1048576 | tf_op jit(solution)/shard_map/reshape | solution.py:76
  27.6 11.1 %shard_map.55 = bf16[64,2048]{1,0:T(8,128)(2,1)} custom-call(s32[1]{0:T(128)} %dynamic_slice.15.mask_ref, bf16[64,4096]{1,0:T(8,128)(2,1)} %reshape.36.a_ref, bf16[1,4096,2048]{2,1,0:T(8,128)(2,1)} %w_ref.1), custom_call_target="tpu_custom_call" | custom-call | flops 1073741824 | bytes 17563648 | tf_op jit(solution)/shard_map/pallas_call | solution.py:36
  38.7 3.5 %all-to-all-start.1 = ((bf16[8,8,2048]{2,1,0:T(8,128)(2,1)}), bf16[8,8,2048]{2,1,0:T(8,128)(2,1)S(1)}, u32[]{:S(2)}, u32[]{:S(2)}) async-start(bf16[8,8,2048]{2,1,0:T(8,128)(2,1)} %bitcast.39), calls=%async_computation.1 | async-start | bytes 524288 | tf_op jit(solution)/shard_map/all_to_all | solution.py:113
  42.3 0.1 dynamic-slice_bitcast_fusion
  42.3 0.1 collective-permute-start.3
  42.4 1.2 %collective-permute-start.4 = (bf16[2,16,2048]{2,1,0:T(8,128)(2,1)S(1)}, bf16[2,16,2048]{2,1,0:T(8,128)(2,1)S(1)}, u32[]{:S(2)}, u32[]{:S(2)}) collective-permute-start(bf16[2,16,2048]{2,1,0:T(8,128)(2,1)S(1)} %get-tuple-element.23), channel_id=1, source_target_pairs={{0,2},{1,3},{2,0},{3,1},{4,6},{5,7},{6,4},{7,5},{8,10},{9,11},{10,... | collective-permute-start | bytes 393224 | tf_op jit(solution)/shard_map/ppermute | solution.py:84
  43.6 1.2 %collective-permute-start.5 = (bf16[2,16,2048]{2,1,0:T(8,128)(2,1)S(1)}, bf16[2,16,2048]{2,1,0:T(8,128)(2,1)S(1)}, u32[]{:S(2)}, u32[]{:S(2)}) collective-permute-start(bf16[2,16,2048]{2,1,0:T(8,128)(2,1)S(1)} %get-tuple-element.22), channel_id=1, source_target_pairs={{0,3},{1,0},{2,1},{3,2},{4,7},{5,4},{6,5},{7,6},{8,11},{9,8},{10,9... | collective-permute-start | bytes 393224 | tf_op jit(solution)/shard_map/ppermute | solution.py:84
  44.9 0.1 reshape_squeeze.3
  45.0 0.2 select_reduce_fusion.3
  45.2 6.2 %all-to-all-done.1 = bf16[8,8,2048]{2,1,0:T(8,128)(2,1)S(1)} async-done(((bf16[8,8,2048]{2,1,0:T(8,128)(2,1)}), bf16[8,8,2048]{2,1,0:T(8,128)(2,1)S(1)}, u32[]{:S(2)}, u32[]{:S(2)}) %all-to-all-start.1) | async-done | bytes 262176 | tf_op jit(solution)/shard_map/all_to_all | solution.py:113
  51.4 0.1 copy.36
  51.5 1.4 %collective-permute-start = (bf16[8,8,2048]{2,0,1:T(8,128)(2,1)S(1)}, bf16[8,8,2048]{2,0,1:T(8,128)(2,1)}, u32[]{:S(2)}, u32[]{:S(2)}) collective-permute-start(bf16[8,8,2048]{2,0,1:T(8,128)(2,1)S(1)} %copy.36), channel_id=1, source_target_pairs={{0,2},{1,3},{2,0},{3,1},{4,6},{5,7},{6,4},{7,5},{8,10},{9,11},{10,... | collective-permute-start | bytes 786440 | tf_op jit(solution)/shard_map/ppermute | solution.py:120
  53.0 0.1 pad_add_fusion
  53.0 0.2 copy.37
  53.3 0.5 reshape.39
  53.8 0.2 copy.38
  54.0 0.2 copy.39
  54.3 0.2 copy.40
  54.5 1.3 %convolution_convert_fusion.1 = bf16[4,2,16,2048]{3,0,2,1:T(4,128)(2,1)S(1)} fusion(bf16[1,2,16,2048]{3,0,2,1:T(2,128)(2,1)S(1)} %copy.40, bf16[1,2,16,2048]{3,0,2,1:T(2,128)(2,1)S(1)} %copy.39, bf16[1,2,16,2048]{3,0,2,1:T(2,128)(2,1)S(1)} %copy.38, bf16[1,2,16,2048]{3,0,2,1:T(2,128)(2,1)S(1)} %copy.37, s32[4]{0:T(128)S(1)} %and_select_fusion), kind=kOutput, calls=%fused_computation.4 | convolution fusion | flops 4456464 | bytes 1048592 | tf_op jit(solution)/shard_map/uk,kptc->uptc/dot_general | solution.py:88
  55.8 0.3 copy.41
  56.1 2.0 %reshape.137 = bf16[8,2,8,32,64,1]{4,3,2,1,0,5:T(8,128)(2,1)} reshape(bf16[4,2,16,2048]{3,2,1,0:T(8,128)(2,1)S(1)} %copy.41) | data formatting | bytes 1048576 | tf_op jit(solution)/shard_map/reshape | solution.py:92
  58.2 0.1 collective-permute-done
  58.3 0.4 collective-permute-start.2
  58.7 2.5 %convolution_bitcast_fusion.1 = f32[8,2,8,32,64]{4,3,2,1,0:T(8,128)S(1)} fusion(bf16[8,64,8,64,1,1]{3,2,1,0,5,4:T(8,128)(2,1)S(1)} %bitcast.40, bf16[8,2,8,32,64,1]{4,3,2,1,0,5:T(8,128)(2,1)} %reshape.137), kind=kOutput, calls=%fused_computation.5 | convolution fusion | flops 268435456 | bytes 2097152 | tf_op jit(solution)/shard_map/pkqsd,bjqd->pkbsj/dot_general | solution.py:94
  61.2 0.7 %reshape.40 = f32[8,16,2048]{2,1,0:T(8,128)S(1)} reshape(f32[8,2,8,32,64]{4,3,2,1,0:T(8,128)S(1)} %convolution_bitcast_fusion.1) | data formatting | bytes 2097152 | tf_op jit(solution)/shard_map/reshape | solution.py:96
  61.8 2.3 %fusion.1 = bf16[8,16,2048]{2,1,0:T(8,128)(2,1)} fusion(f32[8,16,2048]{2,1,0:T(8,128)S(1)} %reshape.40, bf16[8,8,2048]{2,0,1:T(8,128)(2,1)} %collective-permute-done.2, bf16[8,8,2048]{2,0,1:T(8,128)(2,1)} %collective-permute-done.1, bf16[8,8,2048]{2,0,1:T(8,128)(2,1)} %collective-permute-done, bf16[8,8,2048]{2,0,1:T(8,128)(2,1)S(1)} %copy.36, ...), kind=kOutput, calls=%fused_computation.3 | convolution fusion | flops 21496320 | bytes 2621632 | tf_op jit(solution)/shard_map/rpo,rt->pto/dot_general | solution.py:127
  (14 shorter events, 0.0 us)
Async XLA Ops:
  0.0 11.0 %copy-start.1 = (s32[32]{0:T(128)S(1)}, s32[32]{0:T(128)}, u32[]{:S(2)}) copy-start(s32[32]{0:T(128)} %param.11) | copy-start | bytes 388
  3.7 22.9 %all-to-all-start = ((bf16[32,2,4096]{2,1,0:T(2,128)(2,1)}), bf16[32,2,4096]{2,1,0:T(2,128)(2,1)S(1)}, u32[]{:S(2)}, u32[]{:S(2)}) async-start(bf16[32,2,4096]{2,1,0:T(2,128)(2,1)} %copy.33), calls=%async_computation | async-start | bytes 1048576 | tf_op jit(solution)/shard_map/all_to_all | solution.py:75
  27.6 14.7 %slice-start = ((bf16[2,64,4096]{2,1,0:T(8,128)(2,1)}), bf16[2,64,2048]{2,1,0:T(8,128)(2,1)S(1)}, s32[]{:S(2)}) async-start(bf16[2,64,4096]{2,1,0:T(8,128)(2,1)} %param.7), calls=%async_computation.2 | async-start | bytes 1048576 | tf_op jit(solution)/shard_map/slice | solution.py:78
  38.7 14.6 %copy-start = (bf16[512,512]{1,0:T(8,128)(2,1)S(1)}, bf16[512,512]{1,0:T(8,128)(2,1)}, u32[]{:S(2)}) copy-start(bf16[512,512]{1,0:T(8,128)(2,1)} %param.9) | copy-start | bytes 1572868
  38.7 12.7 %all-to-all-start.1 = ((bf16[8,8,2048]{2,1,0:T(8,128)(2,1)}), bf16[8,8,2048]{2,1,0:T(8,128)(2,1)S(1)}, u32[]{:S(2)}, u32[]{:S(2)}) async-start(bf16[8,8,2048]{2,1,0:T(8,128)(2,1)} %bitcast.39), calls=%async_computation.1 | async-start | bytes 524288 | tf_op jit(solution)/shard_map/all_to_all | solution.py:113
  42.3 11.5 %collective-permute-start.3 = (bf16[2,16,2048]{2,1,0:T(8,128)(2,1)S(1)}, bf16[2,16,2048]{2,1,0:T(8,128)(2,1)S(1)}, u32[]{:S(2)}, u32[]{:S(2)}) collective-permute-start(bf16[2,16,2048]{2,1,0:T(8,128)(2,1)S(1)} %get-tuple-element.24), channel_id=1, source_target_pairs={{0,1},{1,2},{2,3},{3,0},{4,5},{5,6},{6,7},{7,4},{8,9},{9,10},{10,1... | collective-permute-start | bytes 393224 | tf_op jit(solution)/shard_map/ppermute | solution.py:84
  42.4 11.6 %collective-permute-start.4 = (bf16[2,16,2048]{2,1,0:T(8,128)(2,1)S(1)}, bf16[2,16,2048]{2,1,0:T(8,128)(2,1)S(1)}, u32[]{:S(2)}, u32[]{:S(2)}) collective-permute-start(bf16[2,16,2048]{2,1,0:T(8,128)(2,1)S(1)} %get-tuple-element.23), channel_id=1, source_target_pairs={{0,2},{1,3},{2,0},{3,1},{4,6},{5,7},{6,4},{7,5},{8,10},{9,11},{10,... | collective-permute-start | bytes 393224 | tf_op jit(solution)/shard_map/ppermute | solution.py:84
  43.6 10.6 %collective-permute-start.5 = (bf16[2,16,2048]{2,1,0:T(8,128)(2,1)S(1)}, bf16[2,16,2048]{2,1,0:T(8,128)(2,1)S(1)}, u32[]{:S(2)}, u32[]{:S(2)}) collective-permute-start(bf16[2,16,2048]{2,1,0:T(8,128)(2,1)S(1)} %get-tuple-element.22), channel_id=1, source_target_pairs={{0,3},{1,0},{2,1},{3,2},{4,7},{5,4},{6,5},{7,6},{8,11},{9,8},{10,9... | collective-permute-start | bytes 393224 | tf_op jit(solution)/shard_map/ppermute | solution.py:84
  51.5 6.7 %collective-permute-start = (bf16[8,8,2048]{2,0,1:T(8,128)(2,1)S(1)}, bf16[8,8,2048]{2,0,1:T(8,128)(2,1)}, u32[]{:S(2)}, u32[]{:S(2)}) collective-permute-start(bf16[8,8,2048]{2,0,1:T(8,128)(2,1)S(1)} %copy.36), channel_id=1, source_target_pairs={{0,2},{1,3},{2,0},{3,1},{4,6},{5,7},{6,4},{7,5},{8,10},{9,11},{10,... | collective-permute-start | bytes 786440 | tf_op jit(solution)/shard_map/ppermute | solution.py:120
  58.1 3.7 %collective-permute-start.1 = (bf16[8,8,2048]{2,0,1:T(8,128)(2,1)S(1)}, bf16[8,8,2048]{2,0,1:T(8,128)(2,1)}, u32[]{:S(2)}, u32[]{:S(2)}) collective-permute-start(bf16[8,8,2048]{2,0,1:T(8,128)(2,1)S(1)} %copy.36), channel_id=1, source_target_pairs={{0,1},{1,0},{2,3},{3,2},{4,5},{5,4},{6,7},{7,6},{8,9},{9,8},{10,11... | collective-permute-start | bytes 786440 | tf_op jit(solution)/shard_map/ppermute | solution.py:120
  58.3 3.5 %collective-permute-start.2 = (bf16[8,8,2048]{2,0,1:T(8,128)(2,1)}, bf16[8,8,2048]{2,0,1:T(8,128)(2,1)}, u32[]{:S(2)}, u32[]{:S(2)}) collective-permute-start(bf16[8,8,2048]{2,0,1:T(8,128)(2,1)} %collective-permute-done), channel_id=1, source_target_pairs={{0,1},{1,0},{2,3},{3,2},{4,5},{5,4},{6,7},{7,6},{8,9},{9,8},{10,11... | collective-permute-start | bytes 786440 | tf_op jit(solution)/shard_map/ppermute | solution.py:120

commit v5 on v4

--- a/solution.py
+++ b/solution.py
@@ -64,6 +64,7 @@
     slab = n_tiles // n_virt
     device = lax.axis_index(("pair", "virt"))
     virt_idx = lax.axis_index("virt")
+    pair_idx = lax.axis_index("pair")
     p_grp = pm_rows * n_virt
 
     tin_all = blk_tiles[:, 0]
@@ -108,11 +109,19 @@
     width = out_cols // N_CHUNK
     pieces = []
     for c in range(N_CHUNK):
-        cols = integrals[:, :, c * width:(c + 1) * width]
-        product = ladder_matmul(own_mask, chosen, cols)
-        held = lax.all_to_all(
-            product.reshape(n_pair, p_grp, width), "pair", 0, 0, tiled=True
-        )
+        cols = integrals[0, :, c * width:(c + 1) * width]
+        product = jnp.dot(chosen, cols, preferred_element_type=jnp.float32)
+        product = (product * own_mask.astype(jnp.float32)).astype(jnp.bfloat16)
+        product = product.reshape(n_pair, p_grp, width)
+        pieces_a = [lax.dynamic_index_in_dim(product, pair_idx, 0)]
+        src_pair = [pair_idx]
+        for k in range(1, n_pair):
+            part = lax.dynamic_index_in_dim(product, (pair_idx + k) % n_pair, 0)
+            perm = [(g, (g + k) % n_pair) for g in range(n_pair)]
+            pieces_a.append(lax.ppermute(part, "pair", perm))
+            src_pair.append((pair_idx - k) % n_pair)
+        held = jnp.concatenate(pieces_a, axis=0)
+        src_pair = jnp.stack(src_pair)
         blocks = [held]
         srcs = [virt_idx]
         for bit in bits:
@@ -121,7 +130,7 @@
             blocks = blocks + got
             srcs = srcs + [s ^ bit for s in srcs]
         allb = jnp.concatenate(blocks, axis=0)
-        src_tiles = jnp.concatenate([jnp.take(tout, s, axis=1) for s in srcs])
+        src_tiles = jnp.concatenate([tout[src_pair, s] for s in srcs])
         one_hot = (src_tiles[:, None] == my_tiles[None, :]).astype(jnp.bfloat16)
         pieces.append(
             jnp.einsum("rpo,rt->pto", allb, one_hot, preferred_element_type=jnp.float32)

time: 64.6 us -> 73.3 us (1.13)
  Pallas kernels: 11.1 us -> 0 us
  local copies, waits for them, and re-layouts: 8.38 us -> 18.4 us
  matrix products: 7.65 us -> 15.7 us
  starting transfers between devices: 15.2 us -> 19.7 us
  waiting for transfers between devices: 21.3 us -> 17.7 us
  between operations: 0.26 us -> 1.27 us
    pallas_call x1 -> x0, Pallas kernels: 11.1 us -> none  [ladder_matmul(): pl.pallas_call(_ladder_kernel, out_shape=jax.ShapeDtypeStruct((m, n), jnp...]
    ppermute x0 -> x7, starting transfers between devices: none -> 10.7 us  [per_device(): pieces_a.append(lax.ppermute(part, 'pair', perm))]
    dot_general x0 -> x1, matrix products: none -> 8.79 us  [per_device(): product = jnp.dot(chosen, cols, preferred_element_type=jnp.float32)]
    all_to_all x1 -> x0, waiting for transfers between devices: 6.19 us -> none  [per_device(): lax.all_to_all(product.reshape(n_pair, p_grp, width), 'pair', 0, 0, tiled...]
    concatenate x0 -> x2, local copies, waits for them, and re-layouts: none -> 5.17 us  [the longest x1 3.71 us: per_device(): allb = jnp.concatenate(blocks, axis=0)]
    ppermute x0 -> x7, waiting for transfers between devices: none -> 4.95 us  [per_device(): pieces_a.append(lax.ppermute(part, 'pair', perm))]
    all_to_all x1 -> x0, starting transfers between devices: 3.54 us -> none  [per_device(): lax.all_to_all(product.reshape(n_pair, p_grp, width), 'pair', 0, 0, tiled...]
    all_to_all x1, waiting for transfers between devices: 14.9 us -> 12 us  [per_device(): chosen = lax.all_to_all(picked, ('pair', 'virt'), 0, 0, tiled=True)]
  transfers between devices with their start and end apart: 8 -> 14, of which waited for: 3 -> 6; matrix products, arithmetic and copies ran while one was open for 15% -> 23% of each run, Pallas kernels for 0% -> 0%
where the time goes in v5:
time: 73.3 us; the launch traced here: 72.8 us
  starting transfers between devices  19.7 us (27%)
  local copies, waits for them, and re-layouts  18.4 us (25%)
  waiting for transfers between devices  17.7 us (24%)
  matrix products  15.7 us (21%)
  between operations  1.27 us (2%)
    all_to_all x1, waiting for transfers between devices, per_device(): chosen = lax.all_to_all(picked, ('pair', 'virt'), 0, 0, tiled=True)  12 us
    ppermute x7, starting transfers between devices, per_device(): pieces_a.append(lax.ppermute(part, 'pair', perm))  10.7 us
    dot_general x1, matrix products, per_device(): product = jnp.dot(chosen, cols, preferred_element_type=jnp.float32)  8.79 us
    all_to_all x1, starting transfers between devices, per_device(): chosen = lax.all_to_all(picked, ('pair', 'virt'), 0, 0, tiled=True)  7.32 us
    ppermute x7, waiting for transfers between devices, per_device(): pieces_a.append(lax.ppermute(part, 'pair', perm))  4.95 us
    concatenate x1, local copies, waits for them, and re-layouts, per_device(): allb = jnp.concatenate(blocks, axis=0)  3.71 us
    dot_general x1, matrix products, per_device(): jnp.einsum('pkqsd,bjqd->pkbsj', sub, fock_four, preferred_element_type=jn...  2.81 us
    gather x4, local copies, waits for them, and re-layouts, per_device(): src_tiles = jnp.concatenate([tout[src_pair, s] for s in srcs])  2.54 us
  transfers between devices with their start and end apart: 14, of which 6 were waited for; matrix products, arithmetic and copies ran while one was open for 23% of the time, Pallas kernels for 0%

profile of v5, /device:TPU:0, one launch (start us, length us, event | category | flops | bytes accessed | tf_op | source)
XLA Modules:
  0.0 72.8 jit_solution(16245107411455731859)
XLA Ops:
  0.0 0.8 %slice_reduce_fusion = (s32[32]{0:T(128)S(1)}, s32[32]{0:T(128)S(1)}) fusion(s32[32,2]{0,1:T(2,128)} %param.8), kind=kLoop, calls=%fused_computation.60 | loop fusion | bytes 512 | tf_op jit(solution)/shard_map/slice | solution.py:101
  0.8 1.6 %convolution_convert_fusion = bf16[32,2,4096]{2,0,1:T(8,128)(2,1)S(1)} fusion(bf16[2,64,4096]{2,1,0:T(8,128)(2,1)} %param.5, s32[32]{0:T(128)S(1)} %get-tuple-element.20), kind=kOutput, calls=%fused_computation.6 | convolution fusion | flops 33818624 | bytes 1572992 | tf_op jit(solution)/shard_map/dt,itc->dic/dot_general | solution.py:73
  2.4 1.3 %copy.60 = bf16[32,2,4096]{2,1,0:T(2,128)(2,1)} copy(bf16[32,2,4096]{2,0,1:T(8,128)(2,1)S(1)} %convolution_convert_fusion) | data formatting | bytes 1048576 | tf_op jit(solution)/shard_map/convert_element_type | solution.py:75
  3.7 7.3 %all-to-all-start = ((bf16[32,2,4096]{2,1,0:T(2,128)(2,1)}), bf16[32,2,4096]{2,1,0:T(2,128)(2,1)S(1)}, u32[]{:S(2)}, u32[]{:S(2)}) async-start(bf16[32,2,4096]{2,1,0:T(2,128)(2,1)} %copy.60), calls=%async_computation | async-start | bytes 1048576 | tf_op jit(solution)/shard_map/all_to_all | solution.py:76
  11.0 1.1 %slice.14 = bf16[2,64,2048]{2,1,0:T(8,128)(2,1)S(1)} slice(bf16[2,64,4096]{2,1,0:T(8,128)(2,1)} %param.5), slice={[0:2], [0:64], [0:2048]} | slice | bytes 1048576 | tf_op jit(solution)/shard_map/slice | solution.py:79
  12.4 1.2 %dynamic_slice.40 = s32[1]{0:T(128)} dynamic-slice(s32[32]{0:T(128)} %param.9, s32[]{:T(128)S(6)} %select_n.158), dynamic_slice_sizes={1} | dynamic-slice | bytes 12 | tf_op jit(solution)/shard_map/dynamic_slice | solution.py:99
  14.6 12.0 %all-to-all-done = bf16[32,2,4096]{2,1,0:T(2,128)(2,1)S(1)} async-done(((bf16[32,2,4096]{2,1,0:T(2,128)(2,1)}), bf16[32,2,4096]{2,1,0:T(2,128)(2,1)S(1)}, u32[]{:S(2)}, u32[]{:S(2)}) %all-to-all-start) | async-done | bytes 524320 | tf_op jit(solution)/shard_map/all_to_all | solution.py:76
  26.8 8.8 %fusion.10 = bf16[8,8,2048]{2,1,0:T(8,128)(2,1)S(1)} fusion(bf16[64,4096]{1,0:T(8,128)(2,1)S(1)} %reshape.349, bf16[1,4096,2048]{2,1,0:T(8,128)(2,1)} %param.6, f32[]{:T(128)} %bitcast.16), kind=kOutput, calls=%fused_computation.13 | convolution fusion | flops 1074003968 | bytes 17563652 | tf_op jit(solution)/shard_map/dot_general | solution.py:113
  35.7 1.2 %collective-permute-start = (bf16[1,8,2048]{2,0,1:T(2,128)(2,1)S(1)}, bf16[1,8,2048]{2,0,1:T(2,128)(2,1)S(1)}, u32[]{:S(2)}, u32[]{:S(2)}) collective-permute-start(bf16[1,8,2048]{2,0,1:T(2,128)(2,1)S(1)} %copy.82), channel_id=1, source_target_pairs={{0,4},{4,8},{8,12},{12,16},{16,20},{20,24},{24,28},{28,0},{1,5},{5... | collective-permute-start | bytes 98312 | tf_op jit(solution)/shard_map/ppermute | solution.py:121
  37.0 0.8 %collective-permute-start.1 = (bf16[1,8,2048]{2,0,1:T(2,128)(2,1)S(1)}, bf16[1,8,2048]{2,0,1:T(2,128)(2,1)S(1)}, u32[]{:S(2)}, u32[]{:S(2)}) collective-permute-start(bf16[1,8,2048]{2,0,1:T(2,128)(2,1)S(1)} %copy.83), channel_id=1, source_target_pairs={{0,8},{4,12},{8,16},{12,20},{16,24},{20,28},{24,0},{28,4},{1,9},{5... | collective-permute-start | bytes 98312 | tf_op jit(solution)/shard_map/ppermute | solution.py:121
  37.9 1.2 %collective-permute-start.2 = (bf16[1,8,2048]{2,0,1:T(2,128)(2,1)S(1)}, bf16[1,8,2048]{2,0,1:T(2,128)(2,1)S(1)}, u32[]{:S(2)}, u32[]{:S(2)}) collective-permute-start(bf16[1,8,2048]{2,0,1:T(2,128)(2,1)S(1)} %copy.84), channel_id=1, source_target_pairs={{0,12},{4,16},{8,20},{12,24},{16,28},{20,0},{24,4},{28,8},{1,13},{... | collective-permute-start | bytes 98312 | tf_op jit(solution)/shard_map/ppermute | solution.py:121
  39.1 3.5 %collective-permute-start.3 = (bf16[1,8,2048]{2,0,1:T(2,128)(2,1)S(1)}, bf16[1,8,2048]{2,0,1:T(2,128)(2,1)S(1)}, u32[]{:S(2)}, u32[]{:S(2)}) collective-permute-start(bf16[1,8,2048]{2,0,1:T(2,128)(2,1)S(1)} %copy.85), channel_id=1, source_target_pairs={{0,16},{4,20},{8,24},{12,28},{16,0},{20,4},{24,8},{28,12},{1,17},{... | collective-permute-start | bytes 98312 | tf_op jit(solution)/shard_map/ppermute | solution.py:121
  43.0 0.5 collective-permute-done
  43.8 0.9 %collective-permute-start.11 = (bf16[2,16,2048]{2,1,0:T(8,128)(2,1)S(1)}, bf16[2,16,2048]{2,1,0:T(8,128)(2,1)S(1)}, u32[]{:S(2)}, u32[]{:S(2)}) collective-permute-start(bf16[2,16,2048]{2,1,0:T(8,128)(2,1)S(1)} %get-tuple-element.9), channel_id=1, source_target_pairs={{0,2},{1,3},{2,0},{3,1},{4,6},{5,7},{6,4},{7,5},{8,10},{9,11},{10,... | collective-permute-start | bytes 393224 | tf_op jit(solution)/shard_map/ppermute | solution.py:85
  44.6 3.5 %collective-permute-done.2 = bf16[1,8,2048]{2,0,1:T(2,128)(2,1)S(1)} collective-permute-done((bf16[1,8,2048]{2,0,1:T(2,128)(2,1)S(1)}, bf16[1,8,2048]{2,0,1:T(2,128)(2,1)S(1)}, u32[]{:S(2)}, u32[]{:S(2)}) %collective-permute-start.2) | collective-permute-done | bytes 32800 | tf_op jit(solution)/shard_map/ppermute | solution.py:121
  48.2 0.7 collective-permute-done.3
  48.9 2.2 %collective-permute-start.5 = (bf16[1,8,2048]{2,0,1:T(2,128)(2,1)S(1)}, bf16[1,8,2048]{2,0,1:T(2,128)(2,1)S(1)}, u32[]{:S(2)}, u32[]{:S(2)}) collective-permute-start(bf16[1,8,2048]{2,0,1:T(2,128)(2,1)S(1)} %copy.87), channel_id=1, source_target_pairs={{0,24},{4,28},{8,0},{12,4},{16,8},{20,12},{24,16},{28,20},{1,25},{... | collective-permute-start | bytes 98312 | tf_op jit(solution)/shard_map/ppermute | solution.py:121
  51.0 1.6 %collective-permute-start.6 = (bf16[1,8,2048]{2,0,1:T(2,128)(2,1)S(1)}, bf16[1,8,2048]{2,0,1:T(2,128)(2,1)S(1)}, u32[]{:S(2)}, u32[]{:S(2)}) collective-permute-start(bf16[1,8,2048]{2,0,1:T(2,128)(2,1)S(1)} %copy.88), channel_id=1, source_target_pairs={{0,28},{4,0},{8,4},{12,8},{16,12},{20,16},{24,20},{28,24},{1,29},{... | collective-permute-start | bytes 98312 | tf_op jit(solution)/shard_map/ppermute | solution.py:121
  52.7 0.6 gather_fusion.3
  53.4 0.6 gather_fusion.2
  54.0 0.6 gather_fusion.1
  54.6 0.6 gather_fusion
  55.4 1.5 %concatenate.46 = bf16[8,8,2048]{2,0,1:T(8,128)(2,1)} concatenate(bf16[1,8,2048]{2,0,1:T(2,128)(2,1)S(1)} %copy.81, bf16[1,8,2048]{2,0,1:T(2,128)(2,1)S(1)} %collective-permute-done, bf16[1,8,2048]{2,0,1:T(2,128)(2,1)S(1)} %collective-permute-done.1, bf16[1,8,2048]{2,0,1:T(2,128)(2,1)S(1)} %collective-permute-done.2, bf16[1,8,2048]{2,0,1:T(2,128)(2,1)S(1)} %collective-permute-done.3, ...), dimensions={0} | concatenate | bytes 524288 | tf_op jit(solution)/shard_map/concatenate | solution.py:123
  56.9 0.7 %collective-permute-start.7 = (bf16[8,8,2048]{2,0,1:T(8,128)(2,1)}, bf16[8,8,2048]{2,0,1:T(8,128)(2,1)S(1)}, u32[]{:S(2)}, u32[]{:S(2)}) collective-permute-start(bf16[8,8,2048]{2,0,1:T(8,128)(2,1)} %concatenate.46), channel_id=1, source_target_pairs={{0,2},{1,3},{2,0},{3,1},{4,6},{5,7},{6,4},{7,5},{8,10},{9,11},{10,... | collective-permute-start | bytes 786440 | tf_op jit(solution)/shard_map/ppermute | solution.py:129
  57.7 1.5 %reshape.352 = bf16[8,64,8,64]{3,2,1,0:T(8,128)(2,1)} reshape(bf16[512,512]{1,0:T(8,128)(2,1)S(1)} %copy-done) | data formatting | bytes 1048576 | tf_op jit(solution)/shard_map/reshape | solution.py:94
  60.1 1.3 %convolution_convert_fusion.1 = bf16[4,2,16,2048]{3,0,2,1:T(4,128)(2,1)S(1)} fusion(bf16[1,2,16,2048]{3,0,2,1:T(2,128)(2,1)S(1)} %copy.72, bf16[1,2,16,2048]{3,0,2,1:T(2,128)(2,1)S(1)} %copy.71, bf16[1,2,16,2048]{3,0,2,1:T(2,128)(2,1)S(1)} %copy.70, bf16[1,2,16,2048]{3,0,2,1:T(2,128)(2,1)S(1)} %copy.69, s32[4]{0:T(128)S(1)} %and_select_fusion), kind=kOutput, calls=%fused_computation.10 | convolution fusion | flops 4456464 | bytes 1048592 | tf_op jit(solution)/shard_map/uk,kptc->uptc/dot_general | solution.py:89
  61.8 2.0 %reshape.381 = bf16[8,2,8,32,64,1]{4,3,2,1,0,5:T(8,128)(2,1)} reshape(bf16[4,2,16,2048]{3,2,1,0:T(8,128)(2,1)S(1)} %copy.73) | data formatting | bytes 1048576 | tf_op jit(solution)/shard_map/reshape | solution.py:93
  63.8 0.7 collective-permute-done.7
  64.5 2.8 %convolution_bitcast_fusion.1 = f32[8,2,8,32,64]{4,3,2,1,0:T(8,128)S(1)} fusion(bf16[8,64,8,64,1,1]{3,2,1,0,5,4:T(8,128)(2,1)} %bitcast.68, bf16[8,2,8,32,64,1]{4,3,2,1,0,5:T(8,128)(2,1)} %reshape.381), kind=kOutput, calls=%fused_computation.14 | convolution fusion | flops 268435456 | bytes 2097152 | tf_op jit(solution)/shard_map/pkqsd,bjqd->pkbsj/dot_general | solution.py:95
  67.3 0.7 reshape.353
  68.0 3.7 %concatenate.47 = bf16[32,8,2048]{2,0,1:T(8,128)(2,1)S(1)} concatenate(bf16[1,8,2048]{2,0,1:T(2,128)(2,1)S(1)} %copy.81, bf16[1,8,2048]{2,0,1:T(2,128)(2,1)S(1)} %collective-permute-done, bf16[1,8,2048]{2,0,1:T(2,128)(2,1)} %copy-done.1, bf16[1,8,2048]{2,0,1:T(2,128)(2,1)} %copy-done.2, bf16[1,8,2048]{2,0,1:T(2,128)(2,1)} %copy-done.3, bf16[1,8,2048]{2,0,1:T(2,128)(2,1)} %copy-done.4, ...), dimensions={0} | concatenate | bytes 2097152 | tf_op jit(solution)/shard_map/concatenate | solution.py:132
  71.7 1.1 %fusion.3 = bf16[8,16,2048]{2,1,0:T(8,128)(2,1)} fusion(f32[8,16,2048]{2,1,0:T(8,128)S(1)} %reshape.353, bf16[32,8,2048]{2,0,1:T(8,128)(2,1)S(1)} %concatenate.47, s32[32]{0:T(128)S(1)} %pad_add_fusion, s32[16]{0:T(128)S(1)} %iota_add_fusion), kind=kOutput, calls=%fused_computation.9 | convolution fusion | flops 17302016 | bytes 2621632 | tf_op jit(solution)/shard_map/rpo,rt->pto/dot_general | solution.py:136
  (51 shorter events, 2.6 us)
Async XLA Ops:
  3.7 22.9 %all-to-all-start = ((bf16[32,2,4096]{2,1,0:T(2,128)(2,1)}), bf16[32,2,4096]{2,1,0:T(2,128)(2,1)S(1)}, u32[]{:S(2)}, u32[]{:S(2)}) async-start(bf16[32,2,4096]{2,1,0:T(2,128)(2,1)} %copy.60), calls=%async_computation | async-start | bytes 1048576 | tf_op jit(solution)/shard_map/all_to_all | solution.py:76
  11.0 46.7 %copy-start = (bf16[512,512]{1,0:T(8,128)(2,1)S(1)}, bf16[512,512]{1,0:T(8,128)(2,1)}, u32[]{:S(2)}) copy-start(bf16[512,512]{1,0:T(8,128)(2,1)} %param.7) | copy-start | bytes 1572868
  35.7 7.8 %collective-permute-start = (bf16[1,8,2048]{2,0,1:T(2,128)(2,1)S(1)}, bf16[1,8,2048]{2,0,1:T(2,128)(2,1)S(1)}, u32[]{:S(2)}, u32[]{:S(2)}) collective-permute-start(bf16[1,8,2048]{2,0,1:T(2,128)(2,1)S(1)} %copy.82), channel_id=1, source_target_pairs={{0,4},{4,8},{8,12},{12,16},{16,20},{20,24},{24,28},{28,0},{1,5},{5... | collective-permute-start | bytes 98312 | tf_op jit(solution)/shard_map/ppermute | solution.py:121
  37.0 6.7 %collective-permute-start.1 = (bf16[1,8,2048]{2,0,1:T(2,128)(2,1)S(1)}, bf16[1,8,2048]{2,0,1:T(2,128)(2,1)S(1)}, u32[]{:S(2)}, u32[]{:S(2)}) collective-permute-start(bf16[1,8,2048]{2,0,1:T(2,128)(2,1)S(1)} %copy.83), channel_id=1, source_target_pairs={{0,8},{4,12},{8,16},{12,20},{16,24},{20,28},{24,0},{28,4},{1,9},{5... | collective-permute-start | bytes 98312 | tf_op jit(solution)/shard_map/ppermute | solution.py:121
  37.9 10.3 %collective-permute-start.2 = (bf16[1,8,2048]{2,0,1:T(2,128)(2,1)S(1)}, bf16[1,8,2048]{2,0,1:T(2,128)(2,1)S(1)}, u32[]{:S(2)}, u32[]{:S(2)}) collective-permute-start(bf16[1,8,2048]{2,0,1:T(2,128)(2,1)S(1)} %copy.84), channel_id=1, source_target_pairs={{0,12},{4,16},{8,20},{12,24},{16,28},{20,0},{24,4},{28,8},{1,13},{... | collective-permute-start | bytes 98312 | tf_op jit(solution)/shard_map/ppermute | solution.py:121
  39.1 9.8 %collective-permute-start.3 = (bf16[1,8,2048]{2,0,1:T(2,128)(2,1)S(1)}, bf16[1,8,2048]{2,0,1:T(2,128)(2,1)S(1)}, u32[]{:S(2)}, u32[]{:S(2)}) collective-permute-start(bf16[1,8,2048]{2,0,1:T(2,128)(2,1)S(1)} %copy.85), channel_id=1, source_target_pairs={{0,16},{4,20},{8,24},{12,28},{16,0},{20,4},{24,8},{28,12},{1,17},{... | collective-permute-start | bytes 98312 | tf_op jit(solution)/shard_map/ppermute | solution.py:121
  42.7 8.3 %collective-permute-start.4 = (bf16[1,8,2048]{2,0,1:T(2,128)(2,1)S(1)}, bf16[1,8,2048]{2,0,1:T(2,128)(2,1)S(1)}, u32[]{:S(2)}, u32[]{:S(2)}) collective-permute-start(bf16[1,8,2048]{2,0,1:T(2,128)(2,1)S(1)} %copy.86), channel_id=1, source_target_pairs={{0,20},{4,24},{8,28},{12,0},{16,4},{20,8},{24,12},{28,16},{1,21},{... | collective-permute-start | bytes 98312 | tf_op jit(solution)/shard_map/ppermute | solution.py:121
  43.6 15.9 %collective-permute-start.12 = (bf16[2,16,2048]{2,1,0:T(8,128)(2,1)S(1)}, bf16[2,16,2048]{2,1,0:T(8,128)(2,1)S(1)}, u32[]{:S(2)}, u32[]{:S(2)}) collective-permute-start(bf16[2,16,2048]{2,1,0:T(8,128)(2,1)S(1)} %get-tuple-element.8), channel_id=1, source_target_pairs={{0,3},{1,0},{2,1},{3,2},{4,7},{5,4},{6,5},{7,6},{8,11},{9,8},{10,9... | collective-permute-start | bytes 393224 | tf_op jit(solution)/shard_map/ppermute | solution.py:85
  43.8 11.6 %copy-start.1 = (bf16[1,8,2048]{2,0,1:T(2,128)(2,1)}, bf16[1,8,2048]{2,0,1:T(2,128)(2,1)S(1)}, u32[]{:S(2)}) copy-start(bf16[1,8,2048]{2,0,1:T(2,128)(2,1)S(1)} %collective-permute-done.1) | copy-start | bytes 98308
  43.8 15.9 %collective-permute-start.11 = (bf16[2,16,2048]{2,1,0:T(8,128)(2,1)S(1)}, bf16[2,16,2048]{2,1,0:T(8,128)(2,1)S(1)}, u32[]{:S(2)}, u32[]{:S(2)}) collective-permute-start(bf16[2,16,2048]{2,1,0:T(8,128)(2,1)S(1)} %get-tuple-element.9), channel_id=1, source_target_pairs={{0,2},{1,3},{2,0},{3,1},{4,6},{5,7},{6,4},{7,5},{8,10},{9,11},{10,... | collective-permute-start | bytes 393224 | tf_op jit(solution)/shard_map/ppermute | solution.py:85
  48.2 7.2 %copy-start.2 = (bf16[1,8,2048]{2,0,1:T(2,128)(2,1)}, bf16[1,8,2048]{2,0,1:T(2,128)(2,1)S(1)}, u32[]{:S(2)}) copy-start(bf16[1,8,2048]{2,0,1:T(2,128)(2,1)S(1)} %collective-permute-done.2) | copy-start | bytes 98308
  48.2 11.7 %collective-permute-start.10 = (bf16[2,16,2048]{2,1,0:T(8,128)(2,1)S(1)}, bf16[2,16,2048]{2,1,0:T(8,128)(2,1)S(1)}, u32[]{:S(2)}, u32[]{:S(2)}) collective-permute-start(bf16[2,16,2048]{2,1,0:T(8,128)(2,1)S(1)} %get-tuple-element.10), channel_id=1, source_target_pairs={{0,1},{1,2},{2,3},{3,0},{4,5},{5,6},{6,7},{7,4},{8,9},{9,10},{10,1... | collective-permute-start | bytes 393224 | tf_op jit(solution)/shard_map/ppermute | solution.py:85
  48.9 6.5 %copy-start.3 = (bf16[1,8,2048]{2,0,1:T(2,128)(2,1)}, bf16[1,8,2048]{2,0,1:T(2,128)(2,1)S(1)}, u32[]{:S(2)}) copy-start(bf16[1,8,2048]{2,0,1:T(2,128)(2,1)S(1)} %collective-permute-done.3) | copy-start | bytes 98308
  48.9 6.5 %collective-permute-start.5 = (bf16[1,8,2048]{2,0,1:T(2,128)(2,1)S(1)}, bf16[1,8,2048]{2,0,1:T(2,128)(2,1)S(1)}, u32[]{:S(2)}, u32[]{:S(2)}) collective-permute-start(bf16[1,8,2048]{2,0,1:T(2,128)(2,1)S(1)} %copy.87), channel_id=1, source_target_pairs={{0,24},{4,28},{8,0},{12,4},{16,8},{20,12},{24,16},{28,20},{1,25},{... | collective-permute-start | bytes 98312 | tf_op jit(solution)/shard_map/ppermute | solution.py:121
  51.0 4.3 %copy-start.4 = (bf16[1,8,2048]{2,0,1:T(2,128)(2,1)}, bf16[1,8,2048]{2,0,1:T(2,128)(2,1)S(1)}, u32[]{:S(2)}) copy-start(bf16[1,8,2048]{2,0,1:T(2,128)(2,1)S(1)} %collective-permute-done.4) | copy-start | bytes 98308
  51.0 4.3 %collective-permute-start.6 = (bf16[1,8,2048]{2,0,1:T(2,128)(2,1)S(1)}, bf16[1,8,2048]{2,0,1:T(2,128)(2,1)S(1)}, u32[]{:S(2)}, u32[]{:S(2)}) collective-permute-start(bf16[1,8,2048]{2,0,1:T(2,128)(2,1)S(1)} %copy.88), channel_id=1, source_target_pairs={{0,28},{4,0},{8,4},{12,8},{16,12},{20,16},{24,20},{28,24},{1,29},{... | collective-permute-start | bytes 98312 | tf_op jit(solution)/shard_map/ppermute | solution.py:121
  55.3 4.8 %copy-start.5 = (bf16[1,8,2048]{2,0,1:T(2,128)(2,1)}, bf16[1,8,2048]{2,0,1:T(2,128)(2,1)S(1)}, u32[]{:S(2)}) copy-start(bf16[1,8,2048]{2,0,1:T(2,128)(2,1)S(1)} %collective-permute-done.5) | copy-start | bytes 98308
  55.4 4.7 %copy-start.6 = (bf16[1,8,2048]{2,0,1:T(2,128)(2,1)}, bf16[1,8,2048]{2,0,1:T(2,128)(2,1)S(1)}, u32[]{:S(2)}) copy-start(bf16[1,8,2048]{2,0,1:T(2,128)(2,1)S(1)} %collective-permute-done.6) | copy-start | bytes 98308
  56.9 7.6 %collective-permute-start.7 = (bf16[8,8,2048]{2,0,1:T(8,128)(2,1)}, bf16[8,8,2048]{2,0,1:T(8,128)(2,1)S(1)}, u32[]{:S(2)}, u32[]{:S(2)}) collective-permute-start(bf16[8,8,2048]{2,0,1:T(8,128)(2,1)} %concatenate.46), channel_id=1, source_target_pairs={{0,2},{1,3},{2,0},{3,1},{4,6},{5,7},{6,4},{7,5},{8,10},{9,11},{10,... | collective-permute-start | bytes 786440 | tf_op jit(solution)/shard_map/ppermute | solution.py:129
  63.8 4.2 %collective-permute-start.8 = (bf16[8,8,2048]{2,0,1:T(8,128)(2,1)}, bf16[8,8,2048]{2,0,1:T(8,128)(2,1)}, u32[]{:S(2)}, u32[]{:S(2)}) collective-permute-start(bf16[8,8,2048]{2,0,1:T(8,128)(2,1)} %concatenate.46), channel_id=1, source_target_pairs={{0,1},{1,0},{2,3},{3,2},{4,5},{5,4},{6,7},{7,6},{8,9},{9,8},{10,11... | collective-permute-start | bytes 786440 | tf_op jit(solution)/shard_map/ppermute | solution.py:129
  64.5 3.5 %collective-permute-start.9 = (bf16[8,8,2048]{2,0,1:T(8,128)(2,1)S(1)}, bf16[8,8,2048]{2,0,1:T(8,128)(2,1)}, u32[]{:S(2)}, u32[]{:S(2)}) collective-permute-start(bf16[8,8,2048]{2,0,1:T(8,128)(2,1)S(1)} %collective-permute-done.7), channel_id=1, source_target_pairs={{0,1},{1,0},{2,3},{3,2},{4,5},{5,4},{6,7},{7,6},{8,9},{9,8},{10,11... | collective-permute-start | bytes 786440 | tf_op jit(solution)/shard_map/ppermute | solution.py:129

commit v6 on v3

--- a/solution.py
+++ b/solution.py
@@ -38,12 +38,18 @@
         got.append(lax.ppermute(part, "virt", perm))
     stacked = jnp.stack(got)
     order = (virt_idx - jnp.arange(n_virt, dtype=jnp.int32)) % n_virt
-    sub = jnp.take(stacked, order, axis=0)
+    reorder = (order[:, None] == jnp.arange(n_virt, dtype=jnp.int32)[None, :])
+    sub = jnp.einsum(
+        "uk,kptc->uptc", reorder.astype(stacked.dtype), stacked,
+        preferred_element_type=jnp.float32,
+    ).astype(stacked.dtype)
     sub = sub.reshape(p_grp, slab // NVT, NVT, AS, TILE)
     fock_four = fock_vv.reshape(NVT, TILE, NVT, TILE)
     onebody = jnp.einsum(
         "pkqsd,bjqd->pkbsj", sub, fock_four, preferred_element_type=jnp.float32
     ).reshape(p_grp, slab, out_cols)
+
+    chosen, onebody = lax.optimization_barrier((chosen, onebody))
 
     own_mask = lax.dynamic_index_in_dim(blk_mask, device, 0, keepdims=False)
     own_mask = own_mask.astype(jnp.float32)

time: 61.9 us -> 67.6 us (1.092)
  blocking collectives: 0 us -> 15.6 us
  waiting for transfers between devices: 23.2 us -> 12.4 us
  local copies, waits for them, and re-layouts: 7.22 us -> 9.56 us
  starting transfers between devices: 13.9 us -> 12.8 us
    all_to_all x0 -> x1, blocking collectives: none -> 15.6 us  [per_device(): lax.all_to_all(product.reshape(n_pair, p_grp, width), 'pair', 0, 0, tiled...]
    all_to_all x1, waiting for transfers between devices: 14.3 us -> 0.01 us  [per_device(): chosen = lax.all_to_all(picked, ('pair', 'virt'), 0, 0, tiled=True)]
    all_to_all x1 -> x0, waiting for transfers between devices: 7.1 us -> none  [per_device(): lax.all_to_all(product.reshape(n_pair, p_grp, width), 'pair', 0, 0, tiled...]
    ppermute x3, waiting for transfers between devices: 1.8 us -> 7.9 us  [per_device(): got = [lax.ppermute(x, 'virt', perm) for x in blocks]]
    ppermute x3, waiting for transfers between devices: 0.01 us -> 4.49 us  [per_device(): got.append(lax.ppermute(part, 'virt', perm))]
    all_to_all x1 -> x0, starting transfers between devices: 3.54 us -> none  [per_device(): lax.all_to_all(product.reshape(n_pair, p_grp, width), 'pair', 0, 0, tiled...]
    gather x2 -> x0, local copies, waits for them, and re-layouts: 2.62 us -> none  [per_device(): sub = jnp.take(stacked, order, axis=0)]
    reshape x0 -> x1, local copies, waits for them, and re-layouts: none -> 2.09 us  [per_device(): sub = sub.reshape(p_grp, slab // NVT, NVT, AS, TILE)]
  transfers between devices with their start and end apart: 8 -> 7, of which waited for: 3 -> 5; matrix products, arithmetic and copies ran while one was open for 13% -> 17% of each run, Pallas kernels for 0% -> 0%
where the time goes in v6:
time: 67.6 us; the launch traced here: 67.3 us
  matrix products  15.8 us (23%)
  blocking collectives  15.6 us (23%)
  starting transfers between devices  12.8 us (19%)
  waiting for transfers between devices  12.4 us (18%)
  local copies, waits for them, and re-layouts  9.56 us (14%)
  between operations  0.82 us (1%)
    all_to_all x1, blocking collectives, per_device(): lax.all_to_all(product.reshape(n_pair, p_grp, width), 'pair', 0, 0, tiled...  15.6 us
    dot_general x1, matrix products, per_device(): product = jnp.dot(chosen, cols, preferred_element_type=jnp.float32)  8.88 us
    ppermute x3, waiting for transfers between devices, per_device(): got = [lax.ppermute(x, 'virt', perm) for x in blocks]  7.9 us
    all_to_all x1, starting transfers between devices, per_device(): chosen = lax.all_to_all(picked, ('pair', 'virt'), 0, 0, tiled=True)  7.33 us
    ppermute x3, waiting for transfers between devices, per_device(): got.append(lax.ppermute(part, 'virt', perm))  4.49 us
    ppermute x3, starting transfers between devices, per_device(): got.append(lax.ppermute(part, 'virt', perm))  3.28 us
    dot_general x1, matrix products, per_device(): jnp.einsum('pkqsd,bjqd->pkbsj', sub, fock_four, preferred_element_type=jn...  2.81 us
    ppermute x3, starting transfers between devices, per_device(): got = [lax.ppermute(x, 'virt', perm) for x in blocks]  2.19 us
  transfers between devices with their start and end apart: 7, of which 5 were waited for; matrix products, arithmetic and copies ran while one was open for 17% of the time, Pallas kernels for 0%

profile of v6, /device:TPU:0, one launch (start us, length us, event | category | flops | bytes accessed | tf_op | source)
XLA Modules:
  0.0 67.3 jit_solution(16273777544052795494)
XLA Ops:
  0.0 0.8 %slice_reduce_fusion = (s32[32]{0:T(128)S(1)}, s32[32]{0:T(128)S(1)}) fusion(s32[32,2]{0,1:T(2,128)} %param.10), kind=kLoop, calls=%fused_computation.52 | loop fusion | bytes 512 | tf_op jit(solution)/shard_map/slice | solution.py:57
  0.8 1.6 %convolution_convert_fusion = bf16[32,2,4096]{2,0,1:T(8,128)(2,1)S(1)} fusion(bf16[2,64,4096]{2,1,0:T(8,128)(2,1)} %param.7, s32[32]{0:T(128)S(1)} %get-tuple-element.30), kind=kOutput, calls=%fused_computation.2 | convolution fusion | flops 33818624 | bytes 1572992 | tf_op jit(solution)/shard_map/dt,itc->dic/dot_general | solution.py:26
  2.4 1.3 %copy.32 = bf16[32,2,4096]{2,1,0:T(2,128)(2,1)} copy(bf16[32,2,4096]{2,0,1:T(8,128)(2,1)S(1)} %convolution_convert_fusion) | data formatting | bytes 1048576 | tf_op jit(solution)/shard_map/convert_element_type | solution.py:28
  3.8 7.3 %all-to-all-start = ((bf16[32,2,4096]{2,1,0:T(2,128)(2,1)}), bf16[32,2,4096]{2,1,0:T(2,128)(2,1)S(1)}, u32[]{:S(2)}, u32[]{:S(2)}) async-start(bf16[32,2,4096]{2,1,0:T(2,128)(2,1)} %copy.32), calls=%async_computation | async-start | bytes 1048576 | tf_op jit(solution)/shard_map/all_to_all | solution.py:29
  11.2 0.3 collective-permute-start
  11.5 1.6 %collective-permute-start.1 = (bf16[2,16,2048]{2,1,0:T(8,128)(2,1)S(1)}, bf16[2,16,2048]{2,1,0:T(8,128)(2,1)S(1)}, u32[]{:S(2)}, u32[]{:S(2)}) collective-permute-start(bf16[2,16,2048]{2,1,0:T(8,128)(2,1)S(1)} %get-tuple-element.27), channel_id=1, source_target_pairs={{0,2},{1,3},{2,0},{3,1},{4,6},{5,7},{6,4},{7,5},{8,10},{9,11},{10,... | collective-permute-start | bytes 393224 | tf_op jit(solution)/shard_map/ppermute | solution.py:38
  13.2 1.4 %collective-permute-start.2 = (bf16[2,16,2048]{2,1,0:T(8,128)(2,1)S(1)}, bf16[2,16,2048]{2,1,0:T(8,128)(2,1)S(1)}, u32[]{:S(2)}, u32[]{:S(2)}) collective-permute-start(bf16[2,16,2048]{2,1,0:T(8,128)(2,1)S(1)} %get-tuple-element.26), channel_id=1, source_target_pairs={{0,3},{1,0},{2,1},{3,2},{4,7},{5,4},{6,5},{7,6},{8,11},{9,8},{10,9... | collective-permute-start | bytes 393224 | tf_op jit(solution)/shard_map/ppermute | solution.py:38
  14.5 0.2 copy.33
  14.7 1.5 %reshape.39 = bf16[8,64,8,64]{3,2,1,0:T(8,128)(2,1)} reshape(bf16[512,512]{1,0:T(8,128)(2,1)S(1)} %copy-done.1) | data formatting | bytes 1048576 | tf_op jit(solution)/shard_map/reshape | solution.py:47
  16.3 0.6 dynamic_slice.20
  17.5 2.8 %collective-permute-done = bf16[2,16,2048]{2,1,0:T(8,128)(2,1)S(1)} collective-permute-done((bf16[2,16,2048]{2,1,0:T(8,128)(2,1)S(1)}, bf16[2,16,2048]{2,1,0:T(8,128)(2,1)S(1)}, u32[]{:S(2)}, u32[]{:S(2)}) %collective-permute-start) | collective-permute-done | bytes 131104 | tf_op jit(solution)/shard_map/ppermute | solution.py:38
  20.4 0.2 copy.34
  20.6 1.0 %collective-permute-done.1 = bf16[2,16,2048]{2,1,0:T(8,128)(2,1)S(1)} collective-permute-done((bf16[2,16,2048]{2,1,0:T(8,128)(2,1)S(1)}, bf16[2,16,2048]{2,1,0:T(8,128)(2,1)S(1)}, u32[]{:S(2)}, u32[]{:S(2)}) %collective-permute-start.1) | collective-permute-done | bytes 131104 | tf_op jit(solution)/shard_map/ppermute | solution.py:38
  21.6 0.2 copy.35
  21.8 0.6 collective-permute-done.2
  22.4 0.2 copy.36
  22.6 1.3 %convolution_convert_fusion.1 = bf16[4,2,16,2048]{3,0,2,1:T(4,128)(2,1)S(1)} fusion(bf16[1,2,16,2048]{3,0,2,1:T(2,128)(2,1)S(1)} %copy.36, bf16[1,2,16,2048]{3,0,2,1:T(2,128)(2,1)S(1)} %copy.35, bf16[1,2,16,2048]{3,0,2,1:T(2,128)(2,1)S(1)} %copy.34, bf16[1,2,16,2048]{3,0,2,1:T(2,128)(2,1)S(1)} %copy.33, s32[4]{0:T(128)S(1)} %and_select_fusion), kind=kOutput, calls=%fused_computation.6 | convolution fusion | flops 4456464 | bytes 1048592 | tf_op jit(solution)/shard_map/uk,kptc->uptc/dot_general | solution.py:42
  24.0 0.3 copy.37
  24.3 2.1 %reshape.137 = bf16[8,2,8,32,64,1]{4,3,2,1,0,5:T(8,128)(2,1)} reshape(bf16[4,2,16,2048]{3,2,1,0:T(8,128)(2,1)S(1)} %copy.37) | data formatting | bytes 1048576 | tf_op jit(solution)/shard_map/reshape | solution.py:46
  26.4 2.8 %convolution_bitcast_fusion.1 = f32[8,2,8,32,64]{4,3,2,1,0:T(8,128)S(1)} fusion(bf16[8,64,8,64,1,1]{3,2,1,0,5,4:T(8,128)(2,1)} %bitcast.51, bf16[8,2,8,32,64,1]{4,3,2,1,0,5:T(8,128)(2,1)} %reshape.137), kind=kOutput, calls=%fused_computation.10 | convolution fusion | flops 268435456 | bytes 2097152 | tf_op jit(solution)/shard_map/pkqsd,bjqd->pkbsj/dot_general | solution.py:48
  29.2 1.6 %reshape.40 = f32[8,16,2048]{2,1,0:T(8,128)} reshape(f32[8,2,8,32,64]{4,3,2,1,0:T(8,128)S(1)} %convolution_bitcast_fusion.1) | data formatting | bytes 2097152 | tf_op jit(solution)/shard_map/reshape | solution.py:50
  30.8 0.2 reshape.37
  31.0 8.9 %fusion.10 = bf16[8,8,2048]{2,1,0:T(8,128)(2,1)S(1)} fusion(bf16[64,4096]{1,0:T(8,128)(2,1)S(1)} %reshape.37, bf16[1,4096,2048]{2,1,0:T(8,128)(2,1)} %param.8, f32[]{:T(128)} %bitcast.15), kind=kOutput, calls=%fused_computation.9 | convolution fusion | flops 1074003968 | bytes 17563652 | tf_op jit(solution)/shard_map/dot_general | solution.py:69
  39.9 15.6 %all_to_all.10 = bf16[8,8,2048]{2,1,0:T(8,128)(2,1)S(1)} all-to-all(bf16[8,8,2048]{2,1,0:T(8,128)(2,1)S(1)} %fusion.10), channel_id=1, replica_groups=mesh['pair'=8,'virt'=4] {'pair'}, dimensions={0} | all-to-all | bytes 524288 | tf_op jit(solution)/shard_map/all_to_all | solution.py:71
  55.5 0.1 copy.41
  55.6 2.2 %collective-permute-start.3 = (bf16[8,8,2048]{2,0,1:T(8,128)(2,1)S(1)}, bf16[8,8,2048]{2,0,1:T(8,128)(2,1)S(1)}, u32[]{:S(2)}, u32[]{:S(2)}) collective-permute-start(bf16[8,8,2048]{2,0,1:T(8,128)(2,1)S(1)} %copy.41), channel_id=1, source_target_pairs={{0,2},{1,3},{2,0},{3,1},{4,6},{5,7},{6,4},{7,5},{8,10},{9,11},{10,... | collective-permute-start | bytes 786440 | tf_op jit(solution)/shard_map/ppermute | solution.py:78
  57.8 6.8 %collective-permute-done.3 = bf16[8,8,2048]{2,0,1:T(8,128)(2,1)S(1)} collective-permute-done((bf16[8,8,2048]{2,0,1:T(8,128)(2,1)S(1)}, bf16[8,8,2048]{2,0,1:T(8,128)(2,1)S(1)}, u32[]{:S(2)}, u32[]{:S(2)}) %collective-permute-start.3) | collective-permute-done | bytes 262176 | tf_op jit(solution)/shard_map/ppermute | solution.py:78
  64.6 0.1 reshape_squeeze.3
  64.7 0.2 select_reduce_fusion.3
  64.9 0.1 pad_add_fusion
  65.0 1.1 %collective-permute-done.5 = bf16[8,8,2048]{2,0,1:T(8,128)(2,1)S(1)} collective-permute-done((bf16[8,8,2048]{2,0,1:T(8,128)(2,1)S(1)}, bf16[8,8,2048]{2,0,1:T(8,128)(2,1)S(1)}, u32[]{:S(2)}, u32[]{:S(2)}) %collective-permute-start.5) | collective-permute-done | bytes 262176 | tf_op jit(solution)/shard_map/ppermute | solution.py:78
  66.1 1.1 %fusion.3 = bf16[8,16,2048]{2,1,0:T(8,128)(2,1)} fusion(f32[8,16,2048]{2,1,0:T(8,128)S(1)} %copy-done, bf16[8,8,2048]{2,0,1:T(8,128)(2,1)S(1)} %collective-permute-done.5, bf16[8,8,2048]{2,0,1:T(8,128)(2,1)S(1)} %collective-permute-done.4, bf16[8,8,2048]{2,0,1:T(8,128)(2,1)S(1)} %collective-permute-done.3, bf16[8,8,2048]{2,0,1:T(8,128)(2,1)S(1)} %copy.41, ...), kind=kOutput, calls=%fused_computation.5 | convolution fusion | flops 21496320 | bytes 2621632 | tf_op jit(solution)/shard_map/rpo,rt->pto/dot_general | solution.py:85
  (15 shorter events, 0.1 us)
Async XLA Ops:
  0.8 10.4 %slice-start = ((bf16[2,64,4096]{2,1,0:T(8,128)(2,1)}), bf16[2,64,2048]{2,1,0:T(8,128)(2,1)S(1)}, s32[]{:S(2)}) async-start(bf16[2,64,4096]{2,1,0:T(8,128)(2,1)} %param.7), calls=%async_computation.2 | async-start | bytes 1048576 | tf_op jit(solution)/shard_map/slice | solution.py:32
  2.4 12.3 %copy-start.1 = (bf16[512,512]{1,0:T(8,128)(2,1)S(1)}, bf16[512,512]{1,0:T(8,128)(2,1)}, u32[]{:S(2)}) copy-start(bf16[512,512]{1,0:T(8,128)(2,1)} %param.9) | copy-start | bytes 1572868
  3.8 27.0 %all-to-all-start = ((bf16[32,2,4096]{2,1,0:T(2,128)(2,1)}), bf16[32,2,4096]{2,1,0:T(2,128)(2,1)S(1)}, u32[]{:S(2)}, u32[]{:S(2)}) async-start(bf16[32,2,4096]{2,1,0:T(2,128)(2,1)} %copy.32), calls=%async_computation | async-start | bytes 1048576 | tf_op jit(solution)/shard_map/all_to_all | solution.py:29
  11.1 5.2 %copy-start.2 = (s32[32]{0:T(128)S(1)}, s32[32]{0:T(128)}, u32[]{:S(2)}) copy-start(s32[32]{0:T(128)} %param.11) | copy-start | bytes 388
  11.2 9.1 %collective-permute-start = (bf16[2,16,2048]{2,1,0:T(8,128)(2,1)S(1)}, bf16[2,16,2048]{2,1,0:T(8,128)(2,1)S(1)}, u32[]{:S(2)}, u32[]{:S(2)}) collective-permute-start(bf16[2,16,2048]{2,1,0:T(8,128)(2,1)S(1)} %get-tuple-element.28), channel_id=1, source_target_pairs={{0,1},{1,2},{2,3},{3,0},{4,5},{5,6},{6,7},{7,4},{8,9},{9,10},{10,1... | collective-permute-start | bytes 393224 | tf_op jit(solution)/shard_map/ppermute | solution.py:38
  11.5 10.0 %collective-permute-start.1 = (bf16[2,16,2048]{2,1,0:T(8,128)(2,1)S(1)}, bf16[2,16,2048]{2,1,0:T(8,128)(2,1)S(1)}, u32[]{:S(2)}, u32[]{:S(2)}) collective-permute-start(bf16[2,16,2048]{2,1,0:T(8,128)(2,1)S(1)} %get-tuple-element.27), channel_id=1, source_target_pairs={{0,2},{1,3},{2,0},{3,1},{4,6},{5,7},{6,4},{7,5},{8,10},{9,11},{10,... | collective-permute-start | bytes 393224 | tf_op jit(solution)/shard_map/ppermute | solution.py:38
  13.2 9.3 %collective-permute-start.2 = (bf16[2,16,2048]{2,1,0:T(8,128)(2,1)S(1)}, bf16[2,16,2048]{2,1,0:T(8,128)(2,1)S(1)}, u32[]{:S(2)}, u32[]{:S(2)}) collective-permute-start(bf16[2,16,2048]{2,1,0:T(8,128)(2,1)S(1)} %get-tuple-element.26), channel_id=1, source_target_pairs={{0,3},{1,0},{2,1},{3,2},{4,7},{5,4},{6,5},{7,6},{8,11},{9,8},{10,9... | collective-permute-start | bytes 393224 | tf_op jit(solution)/shard_map/ppermute | solution.py:38
  31.0 35.1 %copy-start = (f32[8,16,2048]{2,1,0:T(8,128)S(1)}, f32[8,16,2048]{2,1,0:T(8,128)}, u32[]{:S(2)}) copy-start(f32[8,16,2048]{2,1,0:T(8,128)} %reshape.40) | copy-start | bytes 3145732
  55.6 9.0 %collective-permute-start.3 = (bf16[8,8,2048]{2,0,1:T(8,128)(2,1)S(1)}, bf16[8,8,2048]{2,0,1:T(8,128)(2,1)S(1)}, u32[]{:S(2)}, u32[]{:S(2)}) collective-permute-start(bf16[8,8,2048]{2,0,1:T(8,128)(2,1)S(1)} %copy.41), channel_id=1, source_target_pairs={{0,2},{1,3},{2,0},{3,1},{4,6},{5,7},{6,4},{7,5},{8,10},{9,11},{10,... | collective-permute-start | bytes 786440 | tf_op jit(solution)/shard_map/ppermute | solution.py:78
  57.8 7.2 %collective-permute-start.4 = (bf16[8,8,2048]{2,0,1:T(8,128)(2,1)S(1)}, bf16[8,8,2048]{2,0,1:T(8,128)(2,1)S(1)}, u32[]{:S(2)}, u32[]{:S(2)}) collective-permute-start(bf16[8,8,2048]{2,0,1:T(8,128)(2,1)S(1)} %copy.41), channel_id=1, source_target_pairs={{0,1},{1,0},{2,3},{3,2},{4,5},{5,4},{6,7},{7,6},{8,9},{9,8},{10,11... | collective-permute-start | bytes 786440 | tf_op jit(solution)/shard_map/ppermute | solution.py:78
  64.6 1.5 %collective-permute-start.5 = (bf16[8,8,2048]{2,0,1:T(8,128)(2,1)S(1)}, bf16[8,8,2048]{2,0,1:T(8,128)(2,1)S(1)}, u32[]{:S(2)}, u32[]{:S(2)}) collective-permute-start(bf16[8,8,2048]{2,0,1:T(8,128)(2,1)S(1)} %collective-permute-done.3), channel_id=1, source_target_pairs={{0,1},{1,0},{2,3},{3,2},{4,5},{5,4},{6,7},{7,6},{8,9},{9,8},{10,11... | collective-permute-start | bytes 786440 | tf_op jit(solution)/shard_map/ppermute | solution.py:78

commit v7 on v6

--- a/solution.py
+++ b/solution.py
@@ -26,6 +26,7 @@
     picked = jnp.einsum(
         "dt,itc->dic", pick, amps_pm, preferred_element_type=jnp.float32
     ).astype(amps_pm.dtype)
+    picked = picked.reshape(n_dev, pm_rows * tile_len)
     chosen = lax.all_to_all(picked, ("pair", "virt"), 0, 0, tiled=True)
     chosen = chosen.reshape(n_dev * pm_rows, tile_len)
 
@@ -48,8 +49,6 @@
     onebody = jnp.einsum(
         "pkqsd,bjqd->pkbsj", sub, fock_four, preferred_element_type=jnp.float32
     ).reshape(p_grp, slab, out_cols)
-
-    chosen, onebody = lax.optimization_barrier((chosen, onebody))
 
     own_mask = lax.dynamic_index_in_dim(blk_mask, device, 0, keepdims=False)
     own_mask = own_mask.astype(jnp.float32)
@@ -75,8 +74,8 @@
         srcs = [virt_idx]
         for bit in bits:
             perm = [(v, v ^ bit) for v in range(n_virt)]
-            got = [lax.ppermute(x, "virt", perm) for x in blocks]
-            blocks = blocks + got
+            got = lax.ppermute(jnp.concatenate(blocks, axis=0), "virt", perm)
+            blocks = blocks + [got]
             srcs = srcs + [s ^ bit for s in srcs]
         allb = jnp.concatenate(blocks, axis=0)
         src_tiles = jnp.concatenate([jnp.take(tout, s, axis=1) for s in srcs])

time: 67.6 us -> 75.4 us (1.12)
  blocking collectives: 15.6 us -> 0 us
  waiting for transfers between devices: 12.4 us -> 24.1 us
  other arithmetic: 0.32 us -> 8.17 us
  starting transfers between devices: 12.8 us -> 14.8 us
  matrix products: 15.8 us -> 17.2 us
    all_to_all x1 -> x0, blocking collectives: 15.6 us -> none  [per_device(): lax.all_to_all(product.reshape(n_pair, p_grp, width), 'pair', 0, 0, tiled...]
    all_to_all x1, waiting for transfers between devices: 0.01 us -> 14.2 us  [per_device(): chosen = lax.all_to_all(picked, ('pair', 'virt'), 0, 0, tiled=True)]
    all_to_all x0 -> x2, other arithmetic: none -> 6.97 us  [per_device(): chosen = lax.all_to_all(picked, ('pair', 'virt'), 0, 0, tiled=True)]
    all_to_all x0 -> x1, waiting for transfers between devices: none -> 6.55 us  [per_device(): lax.all_to_all(product.reshape(n_pair, p_grp, width), 'pair', 0, 0, tiled...]
    ppermute x3 -> x2, waiting for transfers between devices: 7.9 us -> 3.35 us  [per_device(): got = lax.ppermute(jnp.concatenate(blocks, axis=0), 'virt', perm)]
    ppermute x3, waiting for transfers between devices: 4.49 us -> 0.01 us  [per_device(): got.append(lax.ppermute(part, 'virt', perm))]
    all_to_all x0 -> x1, starting transfers between devices: none -> 3.54 us  [per_device(): lax.all_to_all(product.reshape(n_pair, p_grp, width), 'pair', 0, 0, tiled...]
    unnamed x6 -> x8, local copies, waits for them, and re-layouts: 0.02 us -> 1.71 us
  transfers between devices with their start and end apart: 7 -> 7, of which waited for: 5 -> 3; matrix products, arithmetic and copies ran while one was open for 17% -> 13% of each run, Pallas kernels for 0% -> 0%
where the time goes in v7:
time: 75.4 us; the launch traced here: 74.9 us
  waiting for transfers between devices  24.1 us (32%)
  matrix products  17.2 us (23%)
  starting transfers between devices  14.8 us (20%)
  local copies, waits for them, and re-layouts  9.59 us (13%)
  other arithmetic  8.17 us (11%)
  between operations  1 us (1%)
    all_to_all x1, waiting for transfers between devices, per_device(): chosen = lax.all_to_all(picked, ('pair', 'virt'), 0, 0, tiled=True)  14.2 us
    dot_general x1, matrix products, per_device(): product = jnp.dot(chosen, cols, preferred_element_type=jnp.float32)  9.56 us
    all_to_all x1, starting transfers between devices, per_device(): chosen = lax.all_to_all(picked, ('pair', 'virt'), 0, 0, tiled=True)  7.32 us
    all_to_all x2, other arithmetic, per_device(): chosen = lax.all_to_all(picked, ('pair', 'virt'), 0, 0, tiled=True)  6.97 us
    all_to_all x1, waiting for transfers between devices, per_device(): lax.all_to_all(product.reshape(n_pair, p_grp, width), 'pair', 0, 0, tiled...  6.55 us
    all_to_all x1, starting transfers between devices, per_device(): lax.all_to_all(product.reshape(n_pair, p_grp, width), 'pair', 0, 0, tiled...  3.54 us
    ppermute x2, waiting for transfers between devices, per_device(): got = lax.ppermute(jnp.concatenate(blocks, axis=0), 'virt', perm)  3.35 us
    ppermute x3, starting transfers between devices, per_device(): got.append(lax.ppermute(part, 'virt', perm))  2.49 us
  transfers between devices with their start and end apart: 7, of which 3 were waited for; matrix products, arithmetic and copies ran while one was open for 13% of the time, Pallas kernels for 0%

profile of v7, /device:TPU:0, one launch (start us, length us, event | category | flops | bytes accessed | tf_op | source)
XLA Modules:
  0.0 74.9 jit_solution(6111749797477811093)
XLA Ops:
  0.0 0.8 %slice_reduce_fusion = (s32[32]{0:T(128)S(1)}, s32[32]{0:T(128)S(1)}) fusion(s32[32,2]{0,1:T(2,128)} %param.10), kind=kLoop, calls=%fused_computation.51 | loop fusion | bytes 512 | tf_op jit(solution)/shard_map/slice | solution.py:56
  0.8 1.6 %convolution_convert_fusion = bf16[32,2,4096]{2,0,1:T(8,128)(2,1)S(1)} fusion(bf16[2,64,4096]{2,1,0:T(8,128)(2,1)} %param.7, s32[32]{0:T(128)S(1)} %get-tuple-element.26), kind=kOutput, calls=%fused_computation.2 | convolution fusion | flops 33818624 | bytes 1572992 | tf_op jit(solution)/shard_map/dt,itc->dic/dot_general | solution.py:26
  2.4 0.5 copy.32
  2.9 0.5 all_to_all.12
  3.5 0.5 broadcast.114
  4.0 3.8 %reduce.13 = bf16[32,8192]{1,0:T(8,128)(2,1)S(1)} reduce(bf16[32,1,8192]{2,1,0:T(2,128)(2,1)S(1)} %all_to_all.12, bf16[]{:T(256)} %broadcast.114), dimensions={1}, to_apply=%all_to_all.12.reduce_sub_computation | reduce | bytes 1048578 | tf_op jit(solution)/shard_map/all_to_all | solution.py:30
  7.8 1.2 %reshape.159 = bf16[32,2,4096]{2,1,0:T(2,128)(2,1)} reshape(bf16[32,8192]{1,0:T(8,128)(2,1)S(1)} %reduce.13) | data formatting | bytes 1048576
  9.0 7.3 %all-to-all-start = ((bf16[32,2,4096]{2,1,0:T(2,128)(2,1)}), bf16[32,2,4096]{2,1,0:T(2,128)(2,1)S(1)}, u32[]{:S(2)}, u32[]{:S(2)}) async-start(bf16[32,2,4096]{2,1,0:T(2,128)(2,1)} %reshape.159), calls=%async_computation | async-start | bytes 1048576 | tf_op jit(solution)/shard_map/all_to_all | solution.py:30
  16.3 0.7 dynamic_slice.16
  17.7 14.2 %all-to-all-done = bf16[32,2,4096]{2,1,0:T(2,128)(2,1)S(1)} async-done(((bf16[32,2,4096]{2,1,0:T(2,128)(2,1)}), bf16[32,2,4096]{2,1,0:T(2,128)(2,1)S(1)}, u32[]{:S(2)}, u32[]{:S(2)}) %all-to-all-start) | async-done | bytes 524320 | tf_op jit(solution)/shard_map/all_to_all | solution.py:30
  31.9 0.5 reshape.160
  32.4 3.2 %reduce.5 = bf16[32,8192]{1,0:T(8,128)(2,1)S(1)} reduce(bf16[32,1,8192]{2,1,0:T(2,128)(2,1)S(1)} %reshape.160, bf16[]{:T(256)} %constant.102), dimensions={1}, to_apply=%all_to_all.10.reduce_sub_computation | reduce | bytes 1048578 | tf_op jit(solution)/shard_map/all_to_all | solution.py:30
  35.8 9.6 %fusion.10 = bf16[8,8,2048]{2,1,0:T(8,128)(2,1)} fusion(bf16[64,4096]{1,0:T(8,128)(2,1)S(1)} %reshape.42, bf16[1,4096,2048]{2,1,0:T(8,128)(2,1)} %param.8, f32[]{:T(128)} %bitcast.4), kind=kOutput, calls=%fused_computation.9 | convolution fusion | flops 1074003968 | bytes 17563652 | tf_op jit(solution)/shard_map/dot_general | solution.py:68
  45.4 3.5 %all-to-all-start.1 = ((bf16[8,8,2048]{2,1,0:T(8,128)(2,1)}), bf16[8,8,2048]{2,1,0:T(8,128)(2,1)S(1)}, u32[]{:S(2)}, u32[]{:S(2)}) async-start(bf16[8,8,2048]{2,1,0:T(8,128)(2,1)} %fusion.10), calls=%async_computation.1 | async-start | bytes 524288 | tf_op jit(solution)/shard_map/all_to_all | solution.py:70
  49.1 1.2 %collective-permute-start.3 = (bf16[2,16,2048]{2,1,0:T(8,128)(2,1)S(1)}, bf16[2,16,2048]{2,1,0:T(8,128)(2,1)S(1)}, u32[]{:S(2)}, u32[]{:S(2)}) collective-permute-start(bf16[2,16,2048]{2,1,0:T(8,128)(2,1)S(1)} %get-tuple-element.23), channel_id=1, source_target_pairs={{0,2},{1,3},{2,0},{3,1},{4,6},{5,7},{6,4},{7,5},{8,10},{9,11},{10,... | collective-permute-start | bytes 393224 | tf_op jit(solution)/shard_map/ppermute | solution.py:39
  50.3 1.2 %collective-permute-start.4 = (bf16[2,16,2048]{2,1,0:T(8,128)(2,1)S(1)}, bf16[2,16,2048]{2,1,0:T(8,128)(2,1)S(1)}, u32[]{:S(2)}, u32[]{:S(2)}) collective-permute-start(bf16[2,16,2048]{2,1,0:T(8,128)(2,1)S(1)} %get-tuple-element.22), channel_id=1, source_target_pairs={{0,3},{1,0},{2,1},{3,2},{4,7},{5,4},{6,5},{7,6},{8,11},{9,8},{10,9... | collective-permute-start | bytes 393224 | tf_op jit(solution)/shard_map/ppermute | solution.py:39
  51.6 6.6 %all-to-all-done.1 = bf16[8,8,2048]{2,1,0:T(8,128)(2,1)S(1)} async-done(((bf16[8,8,2048]{2,1,0:T(8,128)(2,1)}), bf16[8,8,2048]{2,1,0:T(8,128)(2,1)S(1)}, u32[]{:S(2)}, u32[]{:S(2)}) %all-to-all-start.1) | async-done | bytes 262176 | tf_op jit(solution)/shard_map/all_to_all | solution.py:70
  58.3 1.4 %collective-permute-start = (bf16[8,8,2048]{2,0,1:T(8,128)(2,1)S(1)}, bf16[8,8,2048]{2,0,1:T(8,128)(2,1)S(1)}, u32[]{:S(2)}, u32[]{:S(2)}) collective-permute-start(bf16[8,8,2048]{2,0,1:T(8,128)(2,1)S(1)} %copy.36), channel_id=1, source_target_pairs={{0,2},{1,3},{2,0},{3,1},{4,6},{5,7},{6,4},{7,5},{8,10},{9,11},{10,... | collective-permute-start | bytes 786440 | tf_op jit(solution)/shard_map/ppermute | solution.py:77
  59.7 0.2 copy.37
  60.0 0.5 reshape.45
  60.6 0.2 select_reduce_fusion.3
  60.9 0.2 copy.38
  61.1 0.2 copy.39
  61.3 0.2 copy.40
  61.6 3.4 %collective-permute-done = bf16[8,8,2048]{2,0,1:T(8,128)(2,1)S(1)} collective-permute-done((bf16[8,8,2048]{2,0,1:T(8,128)(2,1)S(1)}, bf16[8,8,2048]{2,0,1:T(8,128)(2,1)S(1)}, u32[]{:S(2)}, u32[]{:S(2)}) %collective-permute-start) | collective-permute-done | bytes 262176 | tf_op jit(solution)/shard_map/ppermute | solution.py:77
  64.9 0.9 %pad_maximum_fusion = bf16[16,8,2048]{2,0,1:T(8,128)(2,1)} fusion(bf16[8,8,2048]{2,0,1:T(8,128)(2,1)S(1)} %collective-permute-done, bf16[8,8,2048]{2,0,1:T(8,128)(2,1)S(1)} %copy.36), kind=kLoop, calls=%fused_computation.18 | loop fusion | flops 1048576 | bytes 1048576 | tf_op jit(solution)/shard_map/concatenate | solution.py:77
  65.8 1.3 %convolution_convert_fusion.1 = bf16[4,2,16,2048]{3,0,2,1:T(4,128)(2,1)S(1)} fusion(bf16[1,2,16,2048]{3,0,2,1:T(2,128)(2,1)S(1)} %copy.40, bf16[1,2,16,2048]{3,0,2,1:T(2,128)(2,1)S(1)} %copy.39, bf16[1,2,16,2048]{3,0,2,1:T(2,128)(2,1)S(1)} %copy.38, bf16[1,2,16,2048]{3,0,2,1:T(2,128)(2,1)S(1)} %copy.37, s32[4]{0:T(128)S(1)} %and_select_fusion), kind=kOutput, calls=%fused_computation.6 | convolution fusion | flops 4456464 | bytes 1048592 | tf_op jit(solution)/shard_map/uk,kptc->uptc/dot_general | solution.py:43
  67.1 0.3 copy.41
  67.4 2.1 %reshape.143 = bf16[8,2,8,32,64,1]{4,3,2,1,0,5:T(8,128)(2,1)} reshape(bf16[4,2,16,2048]{3,2,1,0:T(8,128)(2,1)S(1)} %copy.41) | data formatting | bytes 1048576 | tf_op jit(solution)/shard_map/reshape | solution.py:47
  69.5 2.5 %convolution_bitcast_fusion.1 = f32[8,2,8,32,64]{4,3,2,1,0:T(8,128)S(1)} fusion(bf16[8,64,8,64,1,1]{3,2,1,0,5,4:T(8,128)(2,1)S(1)} %bitcast.51, bf16[8,2,8,32,64,1]{4,3,2,1,0,5:T(8,128)(2,1)} %reshape.143), kind=kOutput, calls=%fused_computation.10 | convolution fusion | flops 268435456 | bytes 2097152 | tf_op jit(solution)/shard_map/pkqsd,bjqd->pkbsj/dot_general | solution.py:49
  72.0 0.7 reshape.46
  72.6 2.3 %fusion.3 = bf16[8,16,2048]{2,1,0:T(8,128)(2,1)} fusion(f32[8,16,2048]{2,1,0:T(8,128)S(1)} %reshape.46, bf16[16,8,2048]{2,0,1:T(8,128)(2,1)} %collective-permute-done.1, bf16[8,8,2048]{2,0,1:T(8,128)(2,1)} %copy-done.1, bf16[8,8,2048]{2,0,1:T(8,128)(2,1)S(1)} %copy.36, s32[32]{0:T(128)S(1)} %pad_add_fusion, s32[16]{0:T(128)S(1)} %iota_add_fusion), kind=kOutput, calls=%fused_computation.5 | convolution fusion | flops 20447744 | bytes 2621632 | tf_op jit(solution)/shard_map/rpo,rt->pto/dot_general | solution.py:84
  (21 shorter events, 0.7 us)
Async XLA Ops:
  3.5 12.9 %copy-start.2 = (s32[32]{0:T(128)S(1)}, s32[32]{0:T(128)}, u32[]{:S(2)}) copy-start(s32[32]{0:T(128)} %param.11) | copy-start | bytes 388
  9.0 22.9 %all-to-all-start = ((bf16[32,2,4096]{2,1,0:T(2,128)(2,1)}), bf16[32,2,4096]{2,1,0:T(2,128)(2,1)S(1)}, u32[]{:S(2)}, u32[]{:S(2)}) async-start(bf16[32,2,4096]{2,1,0:T(2,128)(2,1)} %reshape.159), calls=%async_computation | async-start | bytes 1048576 | tf_op jit(solution)/shard_map/all_to_all | solution.py:30
  35.8 13.2 %slice-start = ((bf16[2,64,4096]{2,1,0:T(8,128)(2,1)}), bf16[2,64,2048]{2,1,0:T(8,128)(2,1)S(1)}, s32[]{:S(2)}) async-start(bf16[2,64,4096]{2,1,0:T(8,128)(2,1)} %param.7), calls=%async_computation.2 | async-start | bytes 1048576 | tf_op jit(solution)/shard_map/slice | solution.py:33
  45.4 14.6 %copy-start = (bf16[512,512]{1,0:T(8,128)(2,1)S(1)}, bf16[512,512]{1,0:T(8,128)(2,1)}, u32[]{:S(2)}) copy-start(bf16[512,512]{1,0:T(8,128)(2,1)} %param.9) | copy-start | bytes 1572868
  45.4 12.7 %all-to-all-start.1 = ((bf16[8,8,2048]{2,1,0:T(8,128)(2,1)}), bf16[8,8,2048]{2,1,0:T(8,128)(2,1)S(1)}, u32[]{:S(2)}, u32[]{:S(2)}) async-start(bf16[8,8,2048]{2,1,0:T(8,128)(2,1)} %fusion.10), calls=%async_computation.1 | async-start | bytes 524288 | tf_op jit(solution)/shard_map/all_to_all | solution.py:70
  49.1 11.8 %collective-permute-start.2 = (bf16[2,16,2048]{2,1,0:T(8,128)(2,1)S(1)}, bf16[2,16,2048]{2,1,0:T(8,128)(2,1)S(1)}, u32[]{:S(2)}, u32[]{:S(2)}) collective-permute-start(bf16[2,16,2048]{2,1,0:T(8,128)(2,1)S(1)} %get-tuple-element.24), channel_id=1, source_target_pairs={{0,1},{1,2},{2,3},{3,0},{4,5},{5,6},{6,7},{7,4},{8,9},{9,10},{10,1... | collective-permute-start | bytes 393224 | tf_op jit(solution)/shard_map/ppermute | solution.py:39
  49.1 12.0 %collective-permute-start.3 = (bf16[2,16,2048]{2,1,0:T(8,128)(2,1)S(1)}, bf16[2,16,2048]{2,1,0:T(8,128)(2,1)S(1)}, u32[]{:S(2)}, u32[]{:S(2)}) collective-permute-start(bf16[2,16,2048]{2,1,0:T(8,128)(2,1)S(1)} %get-tuple-element.23), channel_id=1, source_target_pairs={{0,2},{1,3},{2,0},{3,1},{4,6},{5,7},{6,4},{7,5},{8,10},{9,11},{10,... | collective-permute-start | bytes 393224 | tf_op jit(solution)/shard_map/ppermute | solution.py:39
  50.3 11.0 %collective-permute-start.4 = (bf16[2,16,2048]{2,1,0:T(8,128)(2,1)S(1)}, bf16[2,16,2048]{2,1,0:T(8,128)(2,1)S(1)}, u32[]{:S(2)}, u32[]{:S(2)}) collective-permute-start(bf16[2,16,2048]{2,1,0:T(8,128)(2,1)S(1)} %get-tuple-element.22), channel_id=1, source_target_pairs={{0,3},{1,0},{2,1},{3,2},{4,7},{5,4},{6,5},{7,6},{8,11},{9,8},{10,9... | collective-permute-start | bytes 393224 | tf_op jit(solution)/shard_map/ppermute | solution.py:39
  58.3 6.6 %collective-permute-start = (bf16[8,8,2048]{2,0,1:T(8,128)(2,1)S(1)}, bf16[8,8,2048]{2,0,1:T(8,128)(2,1)S(1)}, u32[]{:S(2)}, u32[]{:S(2)}) collective-permute-start(bf16[8,8,2048]{2,0,1:T(8,128)(2,1)S(1)} %copy.36), channel_id=1, source_target_pairs={{0,2},{1,3},{2,0},{3,1},{4,6},{5,7},{6,4},{7,5},{8,10},{9,11},{10,... | collective-permute-start | bytes 786440 | tf_op jit(solution)/shard_map/ppermute | solution.py:77
  64.9 0.9 %copy-start.1 = (bf16[8,8,2048]{2,0,1:T(8,128)(2,1)}, bf16[8,8,2048]{2,0,1:T(8,128)(2,1)S(1)}, u32[]{:S(2)}) copy-start(bf16[8,8,2048]{2,0,1:T(8,128)(2,1)S(1)} %collective-permute-done) | copy-start | bytes 786436
  65.8 6.9 %collective-permute-start.1 = (bf16[16,8,2048]{2,0,1:T(8,128)(2,1)}, bf16[16,8,2048]{2,0,1:T(8,128)(2,1)}, u32[]{:S(2)}, u32[]{:S(2)}) collective-permute-start(bf16[16,8,2048]{2,0,1:T(8,128)(2,1)} %pad_maximum_fusion), channel_id=1, source_target_pairs={{0,1},{1,0},{2,3},{3,2},{4,5},{5,4},{6,7},{7,6},{8,9},{9,8},{10,11... | collective-permute-start | bytes 1572872 | tf_op jit(solution)/shard_map/ppermute | solution.py:77

commit v8 on v7

--- a/solution.py
+++ b/solution.py
@@ -26,7 +26,6 @@
     picked = jnp.einsum(
         "dt,itc->dic", pick, amps_pm, preferred_element_type=jnp.float32
     ).astype(amps_pm.dtype)
-    picked = picked.reshape(n_dev, pm_rows * tile_len)
     chosen = lax.all_to_all(picked, ("pair", "virt"), 0, 0, tiled=True)
     chosen = chosen.reshape(n_dev * pm_rows, tile_len)
 

time: 75.4 us -> 66.3 us (0.88)
  other arithmetic: 8.17 us -> 1.2 us
  local copies, waits for them, and re-layouts: 9.59 us -> 7.59 us
    all_to_all x2 -> x0, other arithmetic: 6.97 us -> none  [per_device(): chosen = lax.all_to_all(picked, ('pair', 'virt'), 0, 0, tiled=True)]
    unnamed x8 -> x6, local copies, waits for them, and re-layouts: 1.71 us -> 0.01 us
    all_to_all x2 -> x0, local copies, waits for them, and re-layouts: 1.06 us -> none  [per_device(): chosen = lax.all_to_all(picked, ('pair', 'virt'), 0, 0, tiled=True)]
    convert_element_type x1, local copies, waits for them, and re-layouts: 0.54 us -> 1.34 us  [per_device(): picked = jnp.einsum('dt,itc->dic', pick, amps_pm, preferred_element_type=...]
  transfers between devices with their start and end apart: 7 -> 7, of which waited for: 3 -> 3; matrix products, arithmetic and copies ran while one was open for 13% -> 14% of each run, Pallas kernels for 0% -> 0%
where the time goes in v8:
time: 66.3 us; the launch traced here: 65.9 us
  waiting for transfers between devices  24.2 us (37%)
  matrix products  17.2 us (26%)
  starting transfers between devices  14.8 us (22%)
  local copies, waits for them, and re-layouts  7.59 us (11%)
  other arithmetic  1.2 us (2%)
  between operations  0.89 us (1%)
    all_to_all x1, waiting for transfers between devices, per_device(): chosen = lax.all_to_all(picked, ('pair', 'virt'), 0, 0, tiled=True)  14.3 us
    dot_general x1, matrix products, per_device(): product = jnp.dot(chosen, cols, preferred_element_type=jnp.float32)  9.56 us
    all_to_all x1, starting transfers between devices, per_device(): chosen = lax.all_to_all(picked, ('pair', 'virt'), 0, 0, tiled=True)  7.32 us
    all_to_all x1, waiting for transfers between devices, per_device(): lax.all_to_all(product.reshape(n_pair, p_grp, width), 'pair', 0, 0, tiled...  6.55 us
    all_to_all x1, starting transfers between devices, per_device(): lax.all_to_all(product.reshape(n_pair, p_grp, width), 'pair', 0, 0, tiled...  3.54 us
    ppermute x2, waiting for transfers between devices, per_device(): got = lax.ppermute(jnp.concatenate(blocks, axis=0), 'virt', perm)  3.35 us
    ppermute x3, starting transfers between devices, per_device(): got.append(lax.ppermute(part, 'virt', perm))  2.49 us
    dot_general x1, matrix products, per_device(): jnp.einsum('pkqsd,bjqd->pkbsj', sub, fock_four, preferred_element_type=jn...  2.49 us
  transfers between devices with their start and end apart: 7, of which 3 were waited for; matrix products, arithmetic and copies ran while one was open for 14% of the time, Pallas kernels for 0%

profile of v8, /device:TPU:0, one launch (start us, length us, event | category | flops | bytes accessed | tf_op | source)
XLA Modules:
  0.0 65.9 jit_solution(7799369057186528068)
XLA Ops:
  0.0 0.8 %slice_reduce_fusion = (s32[32]{0:T(128)S(1)}, s32[32]{0:T(128)S(1)}) fusion(s32[32,2]{0,1:T(2,128)} %param.10), kind=kLoop, calls=%fused_computation.51 | loop fusion | bytes 512 | tf_op jit(solution)/shard_map/slice | solution.py:55
  0.8 1.6 %convolution_convert_fusion = bf16[32,2,4096]{2,0,1:T(8,128)(2,1)S(1)} fusion(bf16[2,64,4096]{2,1,0:T(8,128)(2,1)} %param.7, s32[32]{0:T(128)S(1)} %get-tuple-element.26), kind=kOutput, calls=%fused_computation.2 | convolution fusion | flops 33818624 | bytes 1572992 | tf_op jit(solution)/shard_map/dt,itc->dic/dot_general | solution.py:26
  2.4 1.3 %copy.32 = bf16[32,2,4096]{2,1,0:T(2,128)(2,1)} copy(bf16[32,2,4096]{2,0,1:T(8,128)(2,1)S(1)} %convolution_convert_fusion) | data formatting | bytes 1048576 | tf_op jit(solution)/shard_map/convert_element_type | solution.py:28
  3.7 7.3 %all-to-all-start = ((bf16[32,2,4096]{2,1,0:T(2,128)(2,1)}), bf16[32,2,4096]{2,1,0:T(2,128)(2,1)S(1)}, u32[]{:S(2)}, u32[]{:S(2)}) async-start(bf16[32,2,4096]{2,1,0:T(2,128)(2,1)} %copy.32), calls=%async_computation | async-start | bytes 1048576 | tf_op jit(solution)/shard_map/all_to_all | solution.py:29
  11.0 0.7 dynamic_slice.16
  12.3 14.3 %all-to-all-done = bf16[32,2,4096]{2,1,0:T(2,128)(2,1)S(1)} async-done(((bf16[32,2,4096]{2,1,0:T(2,128)(2,1)}), bf16[32,2,4096]{2,1,0:T(2,128)(2,1)S(1)}, u32[]{:S(2)}, u32[]{:S(2)}) %all-to-all-start) | async-done | bytes 524320 | tf_op jit(solution)/shard_map/all_to_all | solution.py:29
  26.6 0.2 reshape.37
  26.9 9.6 %fusion.10 = bf16[8,8,2048]{2,1,0:T(8,128)(2,1)} fusion(bf16[64,4096]{1,0:T(8,128)(2,1)S(1)} %reshape.37, bf16[1,4096,2048]{2,1,0:T(8,128)(2,1)} %param.8, f32[]{:T(128)} %bitcast.4), kind=kOutput, calls=%fused_computation.9 | convolution fusion | flops 1074003968 | bytes 17563652 | tf_op jit(solution)/shard_map/dot_general | solution.py:67
  36.4 3.5 %all-to-all-start.1 = ((bf16[8,8,2048]{2,1,0:T(8,128)(2,1)}), bf16[8,8,2048]{2,1,0:T(8,128)(2,1)S(1)}, u32[]{:S(2)}, u32[]{:S(2)}) async-start(bf16[8,8,2048]{2,1,0:T(8,128)(2,1)} %fusion.10), calls=%async_computation.1 | async-start | bytes 524288 | tf_op jit(solution)/shard_map/all_to_all | solution.py:69
  40.0 0.1 dynamic-slice_bitcast_fusion
  40.1 0.1 collective-permute-start.2
  40.1 1.2 %collective-permute-start.3 = (bf16[2,16,2048]{2,1,0:T(8,128)(2,1)S(1)}, bf16[2,16,2048]{2,1,0:T(8,128)(2,1)S(1)}, u32[]{:S(2)}, u32[]{:S(2)}) collective-permute-start(bf16[2,16,2048]{2,1,0:T(8,128)(2,1)S(1)} %get-tuple-element.23), channel_id=1, source_target_pairs={{0,2},{1,3},{2,0},{3,1},{4,6},{5,7},{6,4},{7,5},{8,10},{9,11},{10,... | collective-permute-start | bytes 393224 | tf_op jit(solution)/shard_map/ppermute | solution.py:38
  41.3 1.2 %collective-permute-start.4 = (bf16[2,16,2048]{2,1,0:T(8,128)(2,1)S(1)}, bf16[2,16,2048]{2,1,0:T(8,128)(2,1)S(1)}, u32[]{:S(2)}, u32[]{:S(2)}) collective-permute-start(bf16[2,16,2048]{2,1,0:T(8,128)(2,1)S(1)} %get-tuple-element.22), channel_id=1, source_target_pairs={{0,3},{1,0},{2,1},{3,2},{4,7},{5,4},{6,5},{7,6},{8,11},{9,8},{10,9... | collective-permute-start | bytes 393224 | tf_op jit(solution)/shard_map/ppermute | solution.py:38
  42.6 6.5 %all-to-all-done.1 = bf16[8,8,2048]{2,1,0:T(8,128)(2,1)S(1)} async-done(((bf16[8,8,2048]{2,1,0:T(8,128)(2,1)}), bf16[8,8,2048]{2,1,0:T(8,128)(2,1)S(1)}, u32[]{:S(2)}, u32[]{:S(2)}) %all-to-all-start.1) | async-done | bytes 262176 | tf_op jit(solution)/shard_map/all_to_all | solution.py:69
  49.1 0.1 copy.35
  49.3 1.4 %collective-permute-start = (bf16[8,8,2048]{2,0,1:T(8,128)(2,1)S(1)}, bf16[8,8,2048]{2,0,1:T(8,128)(2,1)S(1)}, u32[]{:S(2)}, u32[]{:S(2)}) collective-permute-start(bf16[8,8,2048]{2,0,1:T(8,128)(2,1)S(1)} %copy.35), channel_id=1, source_target_pairs={{0,2},{1,3},{2,0},{3,1},{4,6},{5,7},{6,4},{7,5},{8,10},{9,11},{10,... | collective-permute-start | bytes 786440 | tf_op jit(solution)/shard_map/ppermute | solution.py:76
  50.8 0.2 copy.36
  51.0 0.5 reshape.40
  51.5 0.1 reshape_squeeze.3
  51.6 0.2 select_reduce_fusion.3
  51.8 0.1 pad_add_fusion
  51.9 0.2 copy.37
  52.1 0.2 copy.38
  52.4 0.2 copy.39
  52.6 3.4 %collective-permute-done = bf16[8,8,2048]{2,0,1:T(8,128)(2,1)S(1)} collective-permute-done((bf16[8,8,2048]{2,0,1:T(8,128)(2,1)S(1)}, bf16[8,8,2048]{2,0,1:T(8,128)(2,1)S(1)}, u32[]{:S(2)}, u32[]{:S(2)}) %collective-permute-start) | collective-permute-done | bytes 262176 | tf_op jit(solution)/shard_map/ppermute | solution.py:76
  55.9 0.9 %pad_maximum_fusion = bf16[16,8,2048]{2,0,1:T(8,128)(2,1)} fusion(bf16[8,8,2048]{2,0,1:T(8,128)(2,1)S(1)} %collective-permute-done, bf16[8,8,2048]{2,0,1:T(8,128)(2,1)S(1)} %copy.35), kind=kLoop, calls=%fused_computation.18 | loop fusion | flops 1048576 | bytes 1048576 | tf_op jit(solution)/shard_map/concatenate | solution.py:76
  56.8 1.3 %convolution_convert_fusion.1 = bf16[4,2,16,2048]{3,0,2,1:T(4,128)(2,1)S(1)} fusion(bf16[1,2,16,2048]{3,0,2,1:T(2,128)(2,1)S(1)} %copy.39, bf16[1,2,16,2048]{3,0,2,1:T(2,128)(2,1)S(1)} %copy.38, bf16[1,2,16,2048]{3,0,2,1:T(2,128)(2,1)S(1)} %copy.37, bf16[1,2,16,2048]{3,0,2,1:T(2,128)(2,1)S(1)} %copy.36, s32[4]{0:T(128)S(1)} %and_select_fusion), kind=kOutput, calls=%fused_computation.6 | convolution fusion | flops 4456464 | bytes 1048592 | tf_op jit(solution)/shard_map/uk,kptc->uptc/dot_general | solution.py:42
  58.1 0.3 copy.40
  58.4 2.0 %reshape.138 = bf16[8,2,8,32,64,1]{4,3,2,1,0,5:T(8,128)(2,1)} reshape(bf16[4,2,16,2048]{3,2,1,0:T(8,128)(2,1)S(1)} %copy.40) | data formatting | bytes 1048576 | tf_op jit(solution)/shard_map/reshape | solution.py:46
  60.5 2.5 %convolution_bitcast_fusion.1 = f32[8,2,8,32,64]{4,3,2,1,0:T(8,128)S(1)} fusion(bf16[8,64,8,64,1,1]{3,2,1,0,5,4:T(8,128)(2,1)S(1)} %bitcast.51, bf16[8,2,8,32,64,1]{4,3,2,1,0,5:T(8,128)(2,1)} %reshape.138), kind=kOutput, calls=%fused_computation.10 | convolution fusion | flops 268435456 | bytes 2097152 | tf_op jit(solution)/shard_map/pkqsd,bjqd->pkbsj/dot_general | solution.py:48
  63.0 0.7 reshape.41
  63.6 2.3 %fusion.3 = bf16[8,16,2048]{2,1,0:T(8,128)(2,1)} fusion(f32[8,16,2048]{2,1,0:T(8,128)S(1)} %reshape.41, bf16[16,8,2048]{2,0,1:T(8,128)(2,1)} %collective-permute-done.1, bf16[8,8,2048]{2,0,1:T(8,128)(2,1)} %copy-done.1, bf16[8,8,2048]{2,0,1:T(8,128)(2,1)S(1)} %copy.35, s32[32]{0:T(128)S(1)} %pad_add_fusion, s32[16]{0:T(128)S(1)} %iota_add_fusion), kind=kOutput, calls=%fused_computation.5 | convolution fusion | flops 20447744 | bytes 2621632 | tf_op jit(solution)/shard_map/rpo,rt->pto/dot_general | solution.py:83
  (15 shorter events, 0.0 us)
Async XLA Ops:
  0.0 11.0 %copy-start.2 = (s32[32]{0:T(128)S(1)}, s32[32]{0:T(128)}, u32[]{:S(2)}) copy-start(s32[32]{0:T(128)} %param.11) | copy-start | bytes 388
  3.7 22.9 %all-to-all-start = ((bf16[32,2,4096]{2,1,0:T(2,128)(2,1)}), bf16[32,2,4096]{2,1,0:T(2,128)(2,1)S(1)}, u32[]{:S(2)}, u32[]{:S(2)}) async-start(bf16[32,2,4096]{2,1,0:T(2,128)(2,1)} %copy.32), calls=%async_computation | async-start | bytes 1048576 | tf_op jit(solution)/shard_map/all_to_all | solution.py:29
  26.8 13.2 %slice-start = ((bf16[2,64,4096]{2,1,0:T(8,128)(2,1)}), bf16[2,64,2048]{2,1,0:T(8,128)(2,1)S(1)}, s32[]{:S(2)}) async-start(bf16[2,64,4096]{2,1,0:T(8,128)(2,1)} %param.7), calls=%async_computation.2 | async-start | bytes 1048576 | tf_op jit(solution)/shard_map/slice | solution.py:32
  36.4 14.6 %copy-start = (bf16[512,512]{1,0:T(8,128)(2,1)S(1)}, bf16[512,512]{1,0:T(8,128)(2,1)}, u32[]{:S(2)}) copy-start(bf16[512,512]{1,0:T(8,128)(2,1)} %param.9) | copy-start | bytes 1572868
  36.4 12.7 %all-to-all-start.1 = ((bf16[8,8,2048]{2,1,0:T(8,128)(2,1)}), bf16[8,8,2048]{2,1,0:T(8,128)(2,1)S(1)}, u32[]{:S(2)}, u32[]{:S(2)}) async-start(bf16[8,8,2048]{2,1,0:T(8,128)(2,1)} %fusion.10), calls=%async_computation.1 | async-start | bytes 524288 | tf_op jit(solution)/shard_map/all_to_all | solution.py:69
  40.1 11.8 %collective-permute-start.2 = (bf16[2,16,2048]{2,1,0:T(8,128)(2,1)S(1)}, bf16[2,16,2048]{2,1,0:T(8,128)(2,1)S(1)}, u32[]{:S(2)}, u32[]{:S(2)}) collective-permute-start(bf16[2,16,2048]{2,1,0:T(8,128)(2,1)S(1)} %get-tuple-element.24), channel_id=1, source_target_pairs={{0,1},{1,2},{2,3},{3,0},{4,5},{5,6},{6,7},{7,4},{8,9},{9,10},{10,1... | collective-permute-start | bytes 393224 | tf_op jit(solution)/shard_map/ppermute | solution.py:38
  40.1 12.0 %collective-permute-start.3 = (bf16[2,16,2048]{2,1,0:T(8,128)(2,1)S(1)}, bf16[2,16,2048]{2,1,0:T(8,128)(2,1)S(1)}, u32[]{:S(2)}, u32[]{:S(2)}) collective-permute-start(bf16[2,16,2048]{2,1,0:T(8,128)(2,1)S(1)} %get-tuple-element.23), channel_id=1, source_target_pairs={{0,2},{1,3},{2,0},{3,1},{4,6},{5,7},{6,4},{7,5},{8,10},{9,11},{10,... | collective-permute-start | bytes 393224 | tf_op jit(solution)/shard_map/ppermute | solution.py:38
  41.3 11.0 %collective-permute-start.4 = (bf16[2,16,2048]{2,1,0:T(8,128)(2,1)S(1)}, bf16[2,16,2048]{2,1,0:T(8,128)(2,1)S(1)}, u32[]{:S(2)}, u32[]{:S(2)}) collective-permute-start(bf16[2,16,2048]{2,1,0:T(8,128)(2,1)S(1)} %get-tuple-element.22), channel_id=1, source_target_pairs={{0,3},{1,0},{2,1},{3,2},{4,7},{5,4},{6,5},{7,6},{8,11},{9,8},{10,9... | collective-permute-start | bytes 393224 | tf_op jit(solution)/shard_map/ppermute | solution.py:38
  49.3 6.6 %collective-permute-start = (bf16[8,8,2048]{2,0,1:T(8,128)(2,1)S(1)}, bf16[8,8,2048]{2,0,1:T(8,128)(2,1)S(1)}, u32[]{:S(2)}, u32[]{:S(2)}) collective-permute-start(bf16[8,8,2048]{2,0,1:T(8,128)(2,1)S(1)} %copy.35), channel_id=1, source_target_pairs={{0,2},{1,3},{2,0},{3,1},{4,6},{5,7},{6,4},{7,5},{8,10},{9,11},{10,... | collective-permute-start | bytes 786440 | tf_op jit(solution)/shard_map/ppermute | solution.py:76
  55.9 0.9 %copy-start.1 = (bf16[8,8,2048]{2,0,1:T(8,128)(2,1)}, bf16[8,8,2048]{2,0,1:T(8,128)(2,1)S(1)}, u32[]{:S(2)}) copy-start(bf16[8,8,2048]{2,0,1:T(8,128)(2,1)S(1)} %collective-permute-done) | copy-start | bytes 786436
  56.8 6.8 %collective-permute-start.1 = (bf16[16,8,2048]{2,0,1:T(8,128)(2,1)}, bf16[16,8,2048]{2,0,1:T(8,128)(2,1)}, u32[]{:S(2)}, u32[]{:S(2)}) collective-permute-start(bf16[16,8,2048]{2,0,1:T(8,128)(2,1)} %pad_maximum_fusion), channel_id=1, source_target_pairs={{0,1},{1,0},{2,3},{3,2},{4,5},{5,4},{6,7},{7,6},{8,9},{9,8},{10,11... | collective-permute-start | bytes 1572872 | tf_op jit(solution)/shard_map/ppermute | solution.py:76

commit v9 on v3

--- a/solution.py
+++ b/solution.py
@@ -38,12 +38,18 @@
         got.append(lax.ppermute(part, "virt", perm))
     stacked = jnp.stack(got)
     order = (virt_idx - jnp.arange(n_virt, dtype=jnp.int32)) % n_virt
-    sub = jnp.take(stacked, order, axis=0)
-    sub = sub.reshape(p_grp, slab // NVT, NVT, AS, TILE)
+    reorder = (order[:, None] == jnp.arange(n_virt, dtype=jnp.int32)[None, :])
     fock_four = fock_vv.reshape(NVT, TILE, NVT, TILE)
-    onebody = jnp.einsum(
-        "pkqsd,bjqd->pkbsj", sub, fock_four, preferred_element_type=jnp.float32
-    ).reshape(p_grp, slab, out_cols)
+
+    def one_body(stacked):
+        sub = jnp.einsum(
+            "uk,kptc->uptc", reorder.astype(stacked.dtype), stacked,
+            preferred_element_type=jnp.float32,
+        ).astype(stacked.dtype)
+        sub = sub.reshape(p_grp, slab // NVT, NVT, AS, TILE)
+        return jnp.einsum(
+            "pkqsd,bjqd->pkbsj", sub, fock_four, preferred_element_type=jnp.float32
+        ).reshape(p_grp, slab, out_cols)
 
     own_mask = lax.dynamic_index_in_dim(blk_mask, device, 0, keepdims=False)
     own_mask = own_mask.astype(jnp.float32)
@@ -62,9 +68,12 @@
         cols = integrals[0, :, c * width:(c + 1) * width]
         product = jnp.dot(chosen, cols, preferred_element_type=jnp.float32)
         product = (product * own_mask).astype(jnp.bfloat16)
+        product, stacked = lax.optimization_barrier((product, stacked))
         held = lax.all_to_all(
             product.reshape(n_pair, p_grp, width), "pair", 0, 0, tiled=True
         )
+        onebody = one_body(stacked)
+        held, onebody = lax.optimization_barrier((held, onebody))
         blocks = [held]
         srcs = [virt_idx]
         for bit in bits:

time: 61.9 us -> 58.7 us (0.948)
  waiting for transfers between devices: 23.2 us -> 20.2 us
  starting transfers between devices: 13.9 us -> 14.8 us
    all_to_all x1, waiting for transfers between devices: 14.3 us -> 1.91 us  [per_device(): chosen = lax.all_to_all(picked, ('pair', 'virt'), 0, 0, tiled=True)]
    ppermute x3, waiting for transfers between devices: 0.01 us -> 9.62 us  [per_device(): got.append(lax.ppermute(part, 'virt', perm))]
    all_to_all x1, waiting for transfers between devices: 7.1 us -> 2.51 us  [per_device(): lax.all_to_all(product.reshape(n_pair, p_grp, width), 'pair', 0, 0, tiled...]
    ppermute x3, waiting for transfers between devices: 1.8 us -> 6.15 us  [per_device(): got = [lax.ppermute(x, 'virt', perm) for x in blocks]]
    gather x2 -> x0, local copies, waits for them, and re-layouts: 2.62 us -> none  [per_device(): sub = jnp.take(stacked, order, axis=0)]
    reshape x1 -> x2, local copies, waits for them, and re-layouts: 0.65 us -> 2.69 us  [the longest x1 2.04 us: one_body(): sub = sub.reshape(p_grp, slab // NVT, NVT, AS, TILE)]
    dot_general x1, matrix products: 2.26 us -> 1.15 us  [per_device(): jnp.einsum('rpo,rt->pto', allb, one_hot, preferred_element_type=jnp.float32)]
    dot_general x1 -> x2, matrix products: 2.51 us -> 3.04 us  [the longest x1 2.49 us: one_body(): jnp.einsum('pkqsd,bjqd->pkbsj', sub, fock_four, preferred_element_type=jn...]
  transfers between devices with their start and end apart: 8 -> 8, of which waited for: 3 -> 6; matrix products, arithmetic and copies ran while one was open for 13% -> 13% of each run, Pallas kernels for 0% -> 0%
where the time goes in v9:
time: 58.7 us; the launch traced here: 58.3 us
  waiting for transfers between devices  20.2 us (34%)
  matrix products  15.3 us (26%)
  starting transfers between devices  14.8 us (25%)
  local copies, waits for them, and re-layouts  6.76 us (12%)
  between operations  0.81 us (1%)
    ppermute x3, waiting for transfers between devices, per_device(): got.append(lax.ppermute(part, 'virt', perm))  9.62 us
    dot_general x1, matrix products, per_device(): product = jnp.dot(chosen, cols, preferred_element_type=jnp.float32)  9.5 us
    all_to_all x1, starting transfers between devices, per_device(): chosen = lax.all_to_all(picked, ('pair', 'virt'), 0, 0, tiled=True)  7.33 us
    ppermute x3, waiting for transfers between devices, per_device(): got = [lax.ppermute(x, 'virt', perm) for x in blocks]  6.15 us
    all_to_all x1, starting transfers between devices, per_device(): lax.all_to_all(product.reshape(n_pair, p_grp, width), 'pair', 0, 0, tiled...  4.03 us
    all_to_all x1, waiting for transfers between devices, per_device(): lax.all_to_all(product.reshape(n_pair, p_grp, width), 'pair', 0, 0, tiled...  2.51 us
    dot_general x1, matrix products, one_body(): jnp.einsum('pkqsd,bjqd->pkbsj', sub, fock_four, preferred_element_type=jn...  2.49 us
    ppermute x3, starting transfers between devices, per_device(): got.append(lax.ppermute(part, 'virt', perm))  2.05 us
  transfers between devices with their start and end apart: 8, of which 6 were waited for; matrix products, arithmetic and copies ran while one was open for 13% of the time, Pallas kernels for 0%

profile of v9, /device:TPU:0, one launch (start us, length us, event | category | flops | bytes accessed | tf_op | source)
XLA Modules:
  0.0 58.3 jit_solution(17750113889555257261)
XLA Ops:
  0.0 0.8 %slice_reduce_fusion = (s32[32]{0:T(128)S(1)}, s32[32]{0:T(128)S(1)}) fusion(s32[32,2]{0,1:T(2,128)} %param.10), kind=kLoop, calls=%fused_computation.46 | loop fusion | bytes 512 | tf_op jit(solution)/shard_map/slice | solution.py:57
  0.8 1.6 %convolution_convert_fusion = bf16[32,2,4096]{2,0,1:T(8,128)(2,1)S(1)} fusion(bf16[2,64,4096]{2,1,0:T(8,128)(2,1)} %param.7, s32[32]{0:T(128)S(1)} %get-tuple-element.34), kind=kOutput, calls=%fused_computation.2 | convolution fusion | flops 33818624 | bytes 1572992 | tf_op jit(solution)/shard_map/dt,itc->dic/dot_general | solution.py:26
  2.4 0.0 copy-start.1
  2.4 1.3 %copy.14 = bf16[32,2,4096]{2,1,0:T(2,128)(2,1)} copy(bf16[32,2,4096]{2,0,1:T(8,128)(2,1)S(1)} %convolution_convert_fusion) | data formatting | bytes 1048576 | tf_op jit(solution)/shard_map/convert_element_type | solution.py:28
  3.8 7.3 %all-to-all-start = ((bf16[32,2,4096]{2,1,0:T(2,128)(2,1)}), bf16[32,2,4096]{2,1,0:T(2,128)(2,1)S(1)}, u32[]{:S(2)}, u32[]{:S(2)}) async-start(bf16[32,2,4096]{2,1,0:T(2,128)(2,1)} %copy.14), calls=%async_computation | async-start | bytes 1048576 | tf_op jit(solution)/shard_map/all_to_all | solution.py:29
  11.2 0.1 dynamic-slice_bitcast_fusion
  11.2 1.5 %collective-permute-start.2 = (bf16[2,16,2048]{2,1,0:T(8,128)(2,1)S(1)}, bf16[2,16,2048]{2,1,0:T(8,128)(2,1)S(1)}, u32[]{:S(2)}, u32[]{:S(2)}) collective-permute-start(bf16[2,16,2048]{2,1,0:T(8,128)(2,1)S(1)} %get-tuple-element.30), channel_id=1, source_target_pairs={{0,3},{1,0},{2,1},{3,2},{4,7},{5,4},{6,5},{7,6},{8,11},{9,8},{10,9... | collective-permute-start | bytes 393224 | tf_op jit(solution)/shard_map/ppermute | solution.py:38
  12.8 0.4 collective-permute-start.1
  13.2 0.1 collective-permute-start
  13.3 0.6 %dynamic_slice.16 = s32[1]{0:T(128)} dynamic-slice(s32[32]{0:T(128)S(1)} %copy-done.1, s32[]{:T(128)S(6)} %select_n.47), dynamic_slice_sizes={1} | dynamic-slice | bytes 12 | tf_op jit(solution)/shard_map/jit(dynamic_index_in_dim)/dynamic_slice | solution.py:54
  14.6 0.5 reshape.40
  15.1 3.9 %collective-permute-done.2 = bf16[2,16,2048]{2,1,0:T(8,128)(2,1)S(1)} collective-permute-done((bf16[2,16,2048]{2,1,0:T(8,128)(2,1)S(1)}, bf16[2,16,2048]{2,1,0:T(8,128)(2,1)S(1)}, u32[]{:S(2)}, u32[]{:S(2)}) %collective-permute-start.2) | collective-permute-done | bytes 131104 | tf_op jit(solution)/shard_map/ppermute | solution.py:38
  19.1 5.7 %collective-permute-done.1 = bf16[2,16,2048]{2,1,0:T(8,128)(2,1)S(1)} collective-permute-done((bf16[2,16,2048]{2,1,0:T(8,128)(2,1)S(1)}, bf16[2,16,2048]{2,1,0:T(8,128)(2,1)S(1)}, u32[]{:S(2)}, u32[]{:S(2)}) %collective-permute-start.1) | collective-permute-done | bytes 131104 | tf_op jit(solution)/shard_map/ppermute | solution.py:38
  24.8 0.1 pad_maximum_fusion
  24.8 1.9 %all-to-all-done = bf16[32,2,4096]{2,1,0:T(2,128)(2,1)S(1)} async-done(((bf16[32,2,4096]{2,1,0:T(2,128)(2,1)}), bf16[32,2,4096]{2,1,0:T(2,128)(2,1)S(1)}, u32[]{:S(2)}, u32[]{:S(2)}) %all-to-all-start) | async-done | bytes 524320 | tf_op jit(solution)/shard_map/all_to_all | solution.py:29
  26.7 0.2 reshape.37
  26.9 9.5 %fusion.7 = bf16[64,2048]{1,0:T(8,128)(2,1)} fusion(bf16[64,4096]{1,0:T(8,128)(2,1)S(1)} %reshape.37, bf16[1,4096,2048]{2,1,0:T(8,128)(2,1)} %param.8, f32[]{:T(128)} %bitcast.4), kind=kOutput, calls=%fused_computation.8 | convolution fusion | flops 1074003968 | bytes 17563652 | tf_op jit(solution)/shard_map/dot_general | solution.py:69
  36.4 4.0 %all-to-all-start.1 = ((bf16[8,8,2048]{2,1,0:T(8,128)(2,1)}), bf16[8,8,2048]{2,1,0:T(8,128)(2,1)S(1)}, u32[]{:S(2)}, u32[]{:S(2)}) async-start(bf16[8,8,2048]{2,1,0:T(8,128)(2,1)} %bitcast.9), calls=%async_computation.1 | async-start | bytes 524288 | tf_op jit(solution)/shard_map/all_to_all | solution.py:72
  40.5 0.5 convolution_convert_fusion.1
  41.0 0.3 copy.16
  41.3 2.0 %reshape.137 = bf16[8,2,8,32,64,1]{4,3,2,1,0,5:T(8,128)(2,1)} reshape(bf16[4,2,16,2048]{3,2,1,0:T(8,128)(2,1)S(1)} %copy.16) | data formatting | bytes 1048576 | tf_op jit(solution)/shard_map/reshape | solution.py:49
  43.4 2.5 %convolution_bitcast_fusion.1 = f32[8,2,8,32,64]{4,3,2,1,0:T(8,128)S(1)} fusion(bf16[8,64,8,64,1,1]{3,2,1,0,5,4:T(8,128)(2,1)S(1)} %bitcast.48, bf16[8,2,8,32,64,1]{4,3,2,1,0,5:T(8,128)(2,1)} %reshape.137), kind=kOutput, calls=%fused_computation.9 | convolution fusion | flops 268435456 | bytes 2097152 | tf_op jit(solution)/shard_map/pkqsd,bjqd->pkbsj/dot_general | solution.py:50
  45.9 0.7 %reshape.41 = f32[8,16,2048]{2,1,0:T(8,128)S(1)} reshape(f32[8,2,8,32,64]{4,3,2,1,0:T(8,128)S(1)} %convolution_bitcast_fusion.1) | data formatting | bytes 2097152 | tf_op jit(solution)/shard_map/reshape | solution.py:52
  46.5 2.5 %all-to-all-done.1 = bf16[8,8,2048]{2,1,0:T(8,128)(2,1)S(1)} async-done(((bf16[8,8,2048]{2,1,0:T(8,128)(2,1)}), bf16[8,8,2048]{2,1,0:T(8,128)(2,1)S(1)}, u32[]{:S(2)}, u32[]{:S(2)}) %all-to-all-start.1) | async-done | bytes 262176 | tf_op jit(solution)/shard_map/all_to_all | solution.py:72
  49.0 0.1 copy.20
  49.2 1.4 %collective-permute-start.3 = (bf16[8,8,2048]{2,0,1:T(8,128)(2,1)S(1)}, bf16[8,8,2048]{2,0,1:T(8,128)(2,1)S(1)}, u32[]{:S(2)}, u32[]{:S(2)}) collective-permute-start(bf16[8,8,2048]{2,0,1:T(8,128)(2,1)S(1)} %copy.20), channel_id=1, source_target_pairs={{0,2},{1,3},{2,0},{3,1},{4,6},{5,7},{6,4},{7,5},{8,10},{9,11},{10,... | collective-permute-start | bytes 786440 | tf_op jit(solution)/shard_map/ppermute | solution.py:81
  50.6 5.0 %collective-permute-done.3 = bf16[8,8,2048]{2,0,1:T(8,128)(2,1)S(1)} collective-permute-done((bf16[8,8,2048]{2,0,1:T(8,128)(2,1)S(1)}, bf16[8,8,2048]{2,0,1:T(8,128)(2,1)S(1)}, u32[]{:S(2)}, u32[]{:S(2)}) %collective-permute-start.3) | collective-permute-done | bytes 262176 | tf_op jit(solution)/shard_map/ppermute | solution.py:81
  55.6 0.1 reshape_squeeze.3
  55.7 0.2 select_reduce_fusion.3
  55.9 0.1 pad_add_fusion
  56.0 1.1 %collective-permute-done.5 = bf16[8,8,2048]{2,0,1:T(8,128)(2,1)S(1)} collective-permute-done((bf16[8,8,2048]{2,0,1:T(8,128)(2,1)S(1)}, bf16[8,8,2048]{2,0,1:T(8,128)(2,1)S(1)}, u32[]{:S(2)}, u32[]{:S(2)}) %collective-permute-start.5) | collective-permute-done | bytes 262176 | tf_op jit(solution)/shard_map/ppermute | solution.py:81
  57.1 1.2 %fusion.3 = bf16[8,16,2048]{2,1,0:T(8,128)(2,1)} fusion(f32[8,16,2048]{2,1,0:T(8,128)S(1)} %reshape.41, bf16[8,8,2048]{2,0,1:T(8,128)(2,1)S(1)} %collective-permute-done.5, bf16[8,8,2048]{2,0,1:T(8,128)(2,1)S(1)} %collective-permute-done.4, bf16[8,8,2048]{2,0,1:T(8,128)(2,1)S(1)} %collective-permute-done.3, bf16[8,8,2048]{2,0,1:T(8,128)(2,1)S(1)} %copy.20, ...), kind=kOutput, calls=%fused_computation.5 | convolution fusion | flops 21496320 | bytes 2621632 | tf_op jit(solution)/shard_map/rpo,rt->pto/dot_general | solution.py:88
  (11 shorter events, 0.0 us)
Async XLA Ops:
  0.8 10.4 %slice-start = ((bf16[2,64,4096]{2,1,0:T(8,128)(2,1)}), bf16[2,64,2048]{2,1,0:T(8,128)(2,1)S(1)}, s32[]{:S(2)}) async-start(bf16[2,64,4096]{2,1,0:T(8,128)(2,1)} %param.7), calls=%async_computation.2 | async-start | bytes 1048576 | tf_op jit(solution)/shard_map/slice | solution.py:32
  2.4 10.9 %copy-start.1 = (s32[32]{0:T(128)S(1)}, s32[32]{0:T(128)}, u32[]{:S(2)}) copy-start(s32[32]{0:T(128)} %param.11) | copy-start | bytes 388
  2.4 12.1 %copy-start = (bf16[512,512]{1,0:T(8,128)(2,1)S(1)}, bf16[512,512]{1,0:T(8,128)(2,1)}, u32[]{:S(2)}) copy-start(bf16[512,512]{1,0:T(8,128)(2,1)} %param.9) | copy-start | bytes 1572868
  3.8 22.9 %all-to-all-start = ((bf16[32,2,4096]{2,1,0:T(2,128)(2,1)}), bf16[32,2,4096]{2,1,0:T(2,128)(2,1)S(1)}, u32[]{:S(2)}, u32[]{:S(2)}) async-start(bf16[32,2,4096]{2,1,0:T(2,128)(2,1)} %copy.14), calls=%async_computation | async-start | bytes 1048576 | tf_op jit(solution)/shard_map/all_to_all | solution.py:29
  11.2 7.8 %collective-permute-start.2 = (bf16[2,16,2048]{2,1,0:T(8,128)(2,1)S(1)}, bf16[2,16,2048]{2,1,0:T(8,128)(2,1)S(1)}, u32[]{:S(2)}, u32[]{:S(2)}) collective-permute-start(bf16[2,16,2048]{2,1,0:T(8,128)(2,1)S(1)} %get-tuple-element.30), channel_id=1, source_target_pairs={{0,3},{1,0},{2,1},{3,2},{4,7},{5,4},{6,5},{7,6},{8,11},{9,8},{10,9... | collective-permute-start | bytes 393224 | tf_op jit(solution)/shard_map/ppermute | solution.py:38
  12.8 12.0 %collective-permute-start.1 = (bf16[2,16,2048]{2,1,0:T(8,128)(2,1)S(1)}, bf16[2,16,2048]{2,1,0:T(8,128)(2,1)S(1)}, u32[]{:S(2)}, u32[]{:S(2)}) collective-permute-start(bf16[2,16,2048]{2,1,0:T(8,128)(2,1)S(1)} %get-tuple-element.31), channel_id=1, source_target_pairs={{0,2},{1,3},{2,0},{3,1},{4,6},{5,7},{6,4},{7,5},{8,10},{9,11},{10,... | collective-permute-start | bytes 393224 | tf_op jit(solution)/shard_map/ppermute | solution.py:38
  13.2 11.6 %collective-permute-start = (bf16[2,16,2048]{2,1,0:T(8,128)(2,1)S(1)}, bf16[2,16,2048]{2,1,0:T(8,128)(2,1)S(1)}, u32[]{:S(2)}, u32[]{:S(2)}) collective-permute-start(bf16[2,16,2048]{2,1,0:T(8,128)(2,1)S(1)} %get-tuple-element.32), channel_id=1, source_target_pairs={{0,1},{1,2},{2,3},{3,0},{4,5},{5,6},{6,7},{7,4},{8,9},{9,10},{10,1... | collective-permute-start | bytes 393224 | tf_op jit(solution)/shard_map/ppermute | solution.py:38
  36.4 12.6 %all-to-all-start.1 = ((bf16[8,8,2048]{2,1,0:T(8,128)(2,1)}), bf16[8,8,2048]{2,1,0:T(8,128)(2,1)S(1)}, u32[]{:S(2)}, u32[]{:S(2)}) async-start(bf16[8,8,2048]{2,1,0:T(8,128)(2,1)} %bitcast.9), calls=%async_computation.1 | async-start | bytes 524288 | tf_op jit(solution)/shard_map/all_to_all | solution.py:72
  49.2 6.4 %collective-permute-start.3 = (bf16[8,8,2048]{2,0,1:T(8,128)(2,1)S(1)}, bf16[8,8,2048]{2,0,1:T(8,128)(2,1)S(1)}, u32[]{:S(2)}, u32[]{:S(2)}) collective-permute-start(bf16[8,8,2048]{2,0,1:T(8,128)(2,1)S(1)} %copy.20), channel_id=1, source_target_pairs={{0,2},{1,3},{2,0},{3,1},{4,6},{5,7},{6,4},{7,5},{8,10},{9,11},{10,... | collective-permute-start | bytes 786440 | tf_op jit(solution)/shard_map/ppermute | solution.py:81
  50.6 5.4 %collective-permute-start.4 = (bf16[8,8,2048]{2,0,1:T(8,128)(2,1)S(1)}, bf16[8,8,2048]{2,0,1:T(8,128)(2,1)S(1)}, u32[]{:S(2)}, u32[]{:S(2)}) collective-permute-start(bf16[8,8,2048]{2,0,1:T(8,128)(2,1)S(1)} %copy.20), channel_id=1, source_target_pairs={{0,1},{1,0},{2,3},{3,2},{4,5},{5,4},{6,7},{7,6},{8,9},{9,8},{10,11... | collective-permute-start | bytes 786440 | tf_op jit(solution)/shard_map/ppermute | solution.py:81
  55.6 1.5 %collective-permute-start.5 = (bf16[8,8,2048]{2,0,1:T(8,128)(2,1)S(1)}, bf16[8,8,2048]{2,0,1:T(8,128)(2,1)S(1)}, u32[]{:S(2)}, u32[]{:S(2)}) collective-permute-start(bf16[8,8,2048]{2,0,1:T(8,128)(2,1)S(1)} %collective-permute-done.3), channel_id=1, source_target_pairs={{0,1},{1,0},{2,3},{3,2},{4,5},{5,4},{6,7},{7,6},{8,9},{9,8},{10,11... | collective-permute-start | bytes 786440 | tf_op jit(solution)/shard_map/ppermute | solution.py:81

commit v10 on v9

--- a/solution.py
+++ b/solution.py
@@ -29,10 +29,11 @@
     chosen = lax.all_to_all(picked, ("pair", "virt"), 0, 0, tiled=True)
     chosen = chosen.reshape(n_dev * pm_rows, tile_len)
 
-    got = [lax.dynamic_slice_in_dim(amps_pm[:, :, :out_cols], virt_idx * slab, slab, 1)]
+    chosen, ob_src = lax.optimization_barrier((chosen, amps_pm[:, :, :out_cols]))
+    got = [lax.dynamic_slice_in_dim(ob_src, virt_idx * slab, slab, 1)]
     for k in range(1, n_virt):
         part = lax.dynamic_slice_in_dim(
-            amps_pm[:, :, :out_cols], ((virt_idx + k) % n_virt) * slab, slab, 1
+            ob_src, ((virt_idx + k) % n_virt) * slab, slab, 1
         )
         perm = [(u, (u + k) % n_virt) for u in range(n_virt)]
         got.append(lax.ppermute(part, "virt", perm))

time: 58.7 us -> 63.2 us (1.077)
  waiting for transfers between devices: 20.2 us -> 25.1 us
    all_to_all x1, waiting for transfers between devices: 1.91 us -> 13.7 us  [per_device(): chosen = lax.all_to_all(picked, ('pair', 'virt'), 0, 0, tiled=True)]
    ppermute x3, waiting for transfers between devices: 9.62 us -> 0.01 us  [per_device(): got.append(lax.ppermute(part, 'virt', perm))]
    ppermute x3, waiting for transfers between devices: 6.15 us -> 8.06 us  [per_device(): got = [lax.ppermute(x, 'virt', perm) for x in blocks]]
    all_to_all x1, waiting for transfers between devices: 2.51 us -> 3.36 us  [per_device(): lax.all_to_all(product.reshape(n_pair, p_grp, width), 'pair', 0, 0, tiled...]
  transfers between devices with their start and end apart: 8 -> 8, of which waited for: 6 -> 4; matrix products, arithmetic and copies ran while one was open for 13% -> 27% of each run, Pallas kernels for 0% -> 0%
where the time goes in v10:
time: 63.2 us; the launch traced here: 62.8 us
  waiting for transfers between devices  25.1 us (40%)
  matrix products  15.3 us (24%)
  starting transfers between devices  14.3 us (23%)
  local copies, waits for them, and re-layouts  6.77 us (11%)
  between operations  0.85 us (1%)
    all_to_all x1, waiting for transfers between devices, per_device(): chosen = lax.all_to_all(picked, ('pair', 'virt'), 0, 0, tiled=True)  13.7 us
    dot_general x1, matrix products, per_device(): product = jnp.dot(chosen, cols, preferred_element_type=jnp.float32)  9.49 us
    ppermute x3, waiting for transfers between devices, per_device(): got = [lax.ppermute(x, 'virt', perm) for x in blocks]  8.06 us
    all_to_all x1, starting transfers between devices, per_device(): chosen = lax.all_to_all(picked, ('pair', 'virt'), 0, 0, tiled=True)  7.33 us
    all_to_all x1, starting transfers between devices, per_device(): lax.all_to_all(product.reshape(n_pair, p_grp, width), 'pair', 0, 0, tiled...  3.42 us
    all_to_all x1, waiting for transfers between devices, per_device(): lax.all_to_all(product.reshape(n_pair, p_grp, width), 'pair', 0, 0, tiled...  3.36 us
    dot_general x1, matrix products, one_body(): jnp.einsum('pkqsd,bjqd->pkbsj', sub, fock_four, preferred_element_type=jn...  2.49 us
    reshape x1, local copies, waits for them, and re-layouts, one_body(): sub = sub.reshape(p_grp, slab // NVT, NVT, AS, TILE)  2.04 us
  transfers between devices with their start and end apart: 8, of which 4 were waited for; matrix products, arithmetic and copies ran while one was open for 27% of the time, Pallas kernels for 0%

profile of v10, /device:TPU:0, one launch (start us, length us, event | category | flops | bytes accessed | tf_op | source)
XLA Modules:
  0.0 62.8 jit_solution(5060843443983883812)
XLA Ops:
  0.0 0.8 %slice_reduce_fusion = (s32[32]{0:T(128)S(1)}, s32[32]{0:T(128)S(1)}) fusion(s32[32,2]{0,1:T(2,128)} %param.10), kind=kLoop, calls=%fused_computation.46 | loop fusion | bytes 512 | tf_op jit(solution)/shard_map/slice | solution.py:58
  0.8 0.0 copy-start
  0.8 1.6 %convolution_convert_fusion = bf16[32,2,4096]{2,0,1:T(8,128)(2,1)S(1)} fusion(bf16[2,64,4096]{2,1,0:T(8,128)(2,1)} %param.7, s32[32]{0:T(128)S(1)} %get-tuple-element.38), kind=kOutput, calls=%fused_computation.2 | convolution fusion | flops 33818624 | bytes 1572992 | tf_op jit(solution)/shard_map/dt,itc->dic/dot_general | solution.py:26
  2.4 1.3 %copy.14 = bf16[32,2,4096]{2,1,0:T(2,128)(2,1)} copy(bf16[32,2,4096]{2,0,1:T(8,128)(2,1)S(1)} %convolution_convert_fusion) | data formatting | bytes 1048576 | tf_op jit(solution)/shard_map/convert_element_type | solution.py:28
  3.8 7.3 %all-to-all-start = ((bf16[32,2,4096]{2,1,0:T(2,128)(2,1)}), bf16[32,2,4096]{2,1,0:T(2,128)(2,1)S(1)}, u32[]{:S(2)}, u32[]{:S(2)}) async-start(bf16[32,2,4096]{2,1,0:T(2,128)(2,1)} %copy.14), calls=%async_computation | async-start | bytes 1048576 | tf_op jit(solution)/shard_map/all_to_all | solution.py:29
  11.1 0.0 slice-start
  11.2 0.7 %dynamic_slice.16 = s32[1]{0:T(128)} dynamic-slice(s32[32]{0:T(128)S(1)} %copy-done.1, s32[]{:T(128)S(6)} %select_n.47), dynamic_slice_sizes={1} | dynamic-slice | bytes 12 | tf_op jit(solution)/shard_map/jit(dynamic_index_in_dim)/dynamic_slice | solution.py:55
  12.5 0.5 reshape.40
  13.0 13.7 %all-to-all-done = bf16[32,2,4096]{2,1,0:T(2,128)(2,1)S(1)} async-done(((bf16[32,2,4096]{2,1,0:T(2,128)(2,1)}), bf16[32,2,4096]{2,1,0:T(2,128)(2,1)S(1)}, u32[]{:S(2)}, u32[]{:S(2)}) %all-to-all-start) | async-done | bytes 524320 | tf_op jit(solution)/shard_map/all_to_all | solution.py:29
  26.7 0.2 reshape.37
  26.9 0.1 dynamic-slice_bitcast_fusion
  27.0 0.9 %collective-permute-start.2 = (bf16[2,16,2048]{2,1,0:T(8,128)(2,1)S(1)}, bf16[2,16,2048]{2,1,0:T(8,128)(2,1)S(1)}, u32[]{:S(2)}, u32[]{:S(2)}) collective-permute-start(bf16[2,16,2048]{2,1,0:T(8,128)(2,1)S(1)} %get-tuple-element.34), channel_id=1, source_target_pairs={{0,3},{1,0},{2,1},{3,2},{4,7},{5,4},{6,5},{7,6},{8,11},{9,8},{10,9... | collective-permute-start | bytes 393224 | tf_op jit(solution)/shard_map/ppermute | solution.py:39
  27.9 0.7 %collective-permute-start.1 = (bf16[2,16,2048]{2,1,0:T(8,128)(2,1)S(1)}, bf16[2,16,2048]{2,1,0:T(8,128)(2,1)S(1)}, u32[]{:S(2)}, u32[]{:S(2)}) collective-permute-start(bf16[2,16,2048]{2,1,0:T(8,128)(2,1)S(1)} %get-tuple-element.35), channel_id=1, source_target_pairs={{0,2},{1,3},{2,0},{3,1},{4,6},{5,7},{6,4},{7,5},{8,10},{9,11},{10,... | collective-permute-start | bytes 393224 | tf_op jit(solution)/shard_map/ppermute | solution.py:39
  28.5 0.0 collective-permute-start
  28.5 9.5 %fusion.7 = bf16[64,2048]{1,0:T(8,128)(2,1)} fusion(bf16[64,4096]{1,0:T(8,128)(2,1)S(1)} %reshape.37, bf16[1,4096,2048]{2,1,0:T(8,128)(2,1)} %param.8, f32[]{:T(128)} %bitcast.4), kind=kOutput, calls=%fused_computation.8 | convolution fusion | flops 1074003968 | bytes 17563652 | tf_op jit(solution)/shard_map/dot_general | solution.py:70
  38.0 0.0 collective-permute-done.2
  38.0 0.1 pad_maximum_fusion
  38.1 3.4 %all-to-all-start.1 = ((bf16[8,8,2048]{2,1,0:T(8,128)(2,1)}), bf16[8,8,2048]{2,1,0:T(8,128)(2,1)S(1)}, u32[]{:S(2)}, u32[]{:S(2)}) async-start(bf16[8,8,2048]{2,1,0:T(8,128)(2,1)} %bitcast.9), calls=%async_computation.1 | async-start | bytes 524288 | tf_op jit(solution)/shard_map/all_to_all | solution.py:73
  41.6 0.5 convolution_convert_fusion.1
  42.1 0.3 copy.16
  42.4 2.0 %reshape.137 = bf16[8,2,8,32,64,1]{4,3,2,1,0,5:T(8,128)(2,1)} reshape(bf16[4,2,16,2048]{3,2,1,0:T(8,128)(2,1)S(1)} %copy.16) | data formatting | bytes 1048576 | tf_op jit(solution)/shard_map/reshape | solution.py:50
  44.4 2.5 %convolution_bitcast_fusion.1 = f32[8,2,8,32,64]{4,3,2,1,0:T(8,128)S(1)} fusion(bf16[8,64,8,64,1,1]{3,2,1,0,5,4:T(8,128)(2,1)S(1)} %bitcast.48, bf16[8,2,8,32,64,1]{4,3,2,1,0,5:T(8,128)(2,1)} %reshape.137), kind=kOutput, calls=%fused_computation.9 | convolution fusion | flops 268435456 | bytes 2097152 | tf_op jit(solution)/shard_map/pkqsd,bjqd->pkbsj/dot_general | solution.py:51
  46.9 0.7 %reshape.41 = f32[8,16,2048]{2,1,0:T(8,128)S(1)} reshape(f32[8,2,8,32,64]{4,3,2,1,0:T(8,128)S(1)} %convolution_bitcast_fusion.1) | data formatting | bytes 2097152 | tf_op jit(solution)/shard_map/reshape | solution.py:53
  47.6 3.4 %all-to-all-done.1 = bf16[8,8,2048]{2,1,0:T(8,128)(2,1)S(1)} async-done(((bf16[8,8,2048]{2,1,0:T(8,128)(2,1)}), bf16[8,8,2048]{2,1,0:T(8,128)(2,1)S(1)}, u32[]{:S(2)}, u32[]{:S(2)}) %all-to-all-start.1) | async-done | bytes 262176 | tf_op jit(solution)/shard_map/all_to_all | solution.py:73
  51.0 0.1 copy.20
  51.1 2.0 %collective-permute-start.3 = (bf16[8,8,2048]{2,0,1:T(8,128)(2,1)S(1)}, bf16[8,8,2048]{2,0,1:T(8,128)(2,1)S(1)}, u32[]{:S(2)}, u32[]{:S(2)}) collective-permute-start(bf16[8,8,2048]{2,0,1:T(8,128)(2,1)S(1)} %copy.20), channel_id=1, source_target_pairs={{0,2},{1,3},{2,0},{3,1},{4,6},{5,7},{6,4},{7,5},{8,10},{9,11},{10,... | collective-permute-start | bytes 786440 | tf_op jit(solution)/shard_map/ppermute | solution.py:82
  53.1 6.9 %collective-permute-done.3 = bf16[8,8,2048]{2,0,1:T(8,128)(2,1)S(1)} collective-permute-done((bf16[8,8,2048]{2,0,1:T(8,128)(2,1)S(1)}, bf16[8,8,2048]{2,0,1:T(8,128)(2,1)S(1)}, u32[]{:S(2)}, u32[]{:S(2)}) %collective-permute-start.3) | collective-permute-done | bytes 262176 | tf_op jit(solution)/shard_map/ppermute | solution.py:82
  60.1 0.1 reshape_squeeze.3
  60.2 0.2 select_reduce_fusion.3
  60.4 0.1 pad_add_fusion
  60.5 1.1 %collective-permute-done.5 = bf16[8,8,2048]{2,0,1:T(8,128)(2,1)S(1)} collective-permute-done((bf16[8,8,2048]{2,0,1:T(8,128)(2,1)S(1)}, bf16[8,8,2048]{2,0,1:T(8,128)(2,1)S(1)}, u32[]{:S(2)}, u32[]{:S(2)}) %collective-permute-start.5) | collective-permute-done | bytes 262176 | tf_op jit(solution)/shard_map/ppermute | solution.py:82
  61.6 1.2 %fusion.3 = bf16[8,16,2048]{2,1,0:T(8,128)(2,1)} fusion(f32[8,16,2048]{2,1,0:T(8,128)S(1)} %reshape.41, bf16[8,8,2048]{2,0,1:T(8,128)(2,1)S(1)} %collective-permute-done.5, bf16[8,8,2048]{2,0,1:T(8,128)(2,1)S(1)} %collective-permute-done.4, bf16[8,8,2048]{2,0,1:T(8,128)(2,1)S(1)} %collective-permute-done.3, bf16[8,8,2048]{2,0,1:T(8,128)(2,1)S(1)} %copy.20, ...), kind=kOutput, calls=%fused_computation.5 | convolution fusion | flops 21496320 | bytes 2621632 | tf_op jit(solution)/shard_map/rpo,rt->pto/dot_general | solution.py:89
  (11 shorter events, 0.0 us)
Async XLA Ops:
  0.8 10.4 %copy-start.1 = (s32[32]{0:T(128)S(1)}, s32[32]{0:T(128)}, u32[]{:S(2)}) copy-start(s32[32]{0:T(128)} %param.11) | copy-start | bytes 388
  0.8 11.7 %copy-start = (bf16[512,512]{1,0:T(8,128)(2,1)S(1)}, bf16[512,512]{1,0:T(8,128)(2,1)}, u32[]{:S(2)}) copy-start(bf16[512,512]{1,0:T(8,128)(2,1)} %param.9) | copy-start | bytes 1572868
  3.8 22.9 %all-to-all-start = ((bf16[32,2,4096]{2,1,0:T(2,128)(2,1)}), bf16[32,2,4096]{2,1,0:T(2,128)(2,1)S(1)}, u32[]{:S(2)}, u32[]{:S(2)}) async-start(bf16[32,2,4096]{2,1,0:T(2,128)(2,1)} %copy.14), calls=%async_computation | async-start | bytes 1048576 | tf_op jit(solution)/shard_map/all_to_all | solution.py:29
  11.1 15.8 %slice-start = ((bf16[2,64,4096]{2,1,0:T(8,128)(2,1)}), bf16[2,64,2048]{2,1,0:T(8,128)(2,1)S(1)}, s32[]{:S(2)}) async-start(bf16[2,64,4096]{2,1,0:T(8,128)(2,1)} %param.7), calls=%async_computation.2 | async-start | bytes 1048576 | tf_op jit(solution)/shard_map/slice | solution.py:32
  27.0 11.0 %collective-permute-start.2 = (bf16[2,16,2048]{2,1,0:T(8,128)(2,1)S(1)}, bf16[2,16,2048]{2,1,0:T(8,128)(2,1)S(1)}, u32[]{:S(2)}, u32[]{:S(2)}) collective-permute-start(bf16[2,16,2048]{2,1,0:T(8,128)(2,1)S(1)} %get-tuple-element.34), channel_id=1, source_target_pairs={{0,3},{1,0},{2,1},{3,2},{4,7},{5,4},{6,5},{7,6},{8,11},{9,8},{10,9... | collective-permute-start | bytes 393224 | tf_op jit(solution)/shard_map/ppermute | solution.py:39
  27.9 10.2 %collective-permute-start.1 = (bf16[2,16,2048]{2,1,0:T(8,128)(2,1)S(1)}, bf16[2,16,2048]{2,1,0:T(8,128)(2,1)S(1)}, u32[]{:S(2)}, u32[]{:S(2)}) collective-permute-start(bf16[2,16,2048]{2,1,0:T(8,128)(2,1)S(1)} %get-tuple-element.35), channel_id=1, source_target_pairs={{0,2},{1,3},{2,0},{3,1},{4,6},{5,7},{6,4},{7,5},{8,10},{9,11},{10,... | collective-permute-start | bytes 393224 | tf_op jit(solution)/shard_map/ppermute | solution.py:39
  28.5 9.5 %collective-permute-start = (bf16[2,16,2048]{2,1,0:T(8,128)(2,1)S(1)}, bf16[2,16,2048]{2,1,0:T(8,128)(2,1)S(1)}, u32[]{:S(2)}, u32[]{:S(2)}) collective-permute-start(bf16[2,16,2048]{2,1,0:T(8,128)(2,1)S(1)} %get-tuple-element.36), channel_id=1, source_target_pairs={{0,1},{1,2},{2,3},{3,0},{4,5},{5,6},{6,7},{7,4},{8,9},{9,10},{10,1... | collective-permute-start | bytes 393224 | tf_op jit(solution)/shard_map/ppermute | solution.py:39
  38.1 12.8 %all-to-all-start.1 = ((bf16[8,8,2048]{2,1,0:T(8,128)(2,1)}), bf16[8,8,2048]{2,1,0:T(8,128)(2,1)S(1)}, u32[]{:S(2)}, u32[]{:S(2)}) async-start(bf16[8,8,2048]{2,1,0:T(8,128)(2,1)} %bitcast.9), calls=%async_computation.1 | async-start | bytes 524288 | tf_op jit(solution)/shard_map/all_to_all | solution.py:73
  51.1 9.0 %collective-permute-start.3 = (bf16[8,8,2048]{2,0,1:T(8,128)(2,1)S(1)}, bf16[8,8,2048]{2,0,1:T(8,128)(2,1)S(1)}, u32[]{:S(2)}, u32[]{:S(2)}) collective-permute-start(bf16[8,8,2048]{2,0,1:T(8,128)(2,1)S(1)} %copy.20), channel_id=1, source_target_pairs={{0,2},{1,3},{2,0},{3,1},{4,6},{5,7},{6,4},{7,5},{8,10},{9,11},{10,... | collective-permute-start | bytes 786440 | tf_op jit(solution)/shard_map/ppermute | solution.py:82
  53.1 7.3 %collective-permute-start.4 = (bf16[8,8,2048]{2,0,1:T(8,128)(2,1)S(1)}, bf16[8,8,2048]{2,0,1:T(8,128)(2,1)S(1)}, u32[]{:S(2)}, u32[]{:S(2)}) collective-permute-start(bf16[8,8,2048]{2,0,1:T(8,128)(2,1)S(1)} %copy.20), channel_id=1, source_target_pairs={{0,1},{1,0},{2,3},{3,2},{4,5},{5,4},{6,7},{7,6},{8,9},{9,8},{10,11... | collective-permute-start | bytes 786440 | tf_op jit(solution)/shard_map/ppermute | solution.py:82
  60.1 1.5 %collective-permute-start.5 = (bf16[8,8,2048]{2,0,1:T(8,128)(2,1)S(1)}, bf16[8,8,2048]{2,0,1:T(8,128)(2,1)S(1)}, u32[]{:S(2)}, u32[]{:S(2)}) collective-permute-start(bf16[8,8,2048]{2,0,1:T(8,128)(2,1)S(1)} %collective-permute-done.3), channel_id=1, source_target_pairs={{0,1},{1,0},{2,3},{3,2},{4,5},{5,4},{6,7},{7,6},{8,9},{9,8},{10,11... | collective-permute-start | bytes 786440 | tf_op jit(solution)/shard_map/ppermute | solution.py:82

commit v11 on v9

--- a/solution.py
+++ b/solution.py
@@ -7,6 +7,7 @@
 NVT = 8
 AS = 32
 N_CHUNK = 1
+N_CORE = 2
 
 
 def per_device(amps_pm, integrals, fock_vv, blk_tiles, blk_mask):
@@ -52,6 +53,7 @@
         ).reshape(p_grp, slab, out_cols)
 
     own_mask = lax.dynamic_index_in_dim(blk_mask, device, 0, keepdims=False)
+    own_tout = lax.dynamic_index_in_dim(blk_tiles[:, 1], device, 0, keepdims=False)
     own_mask = own_mask.astype(jnp.float32)
 
     tout = blk_tiles[:, 1].reshape(n_pair, n_virt)
@@ -69,20 +71,26 @@
         product = jnp.dot(chosen, cols, preferred_element_type=jnp.float32)
         product = (product * own_mask).astype(jnp.bfloat16)
         product, stacked = lax.optimization_barrier((product, stacked))
+        n_x = n_virt // N_CORE
+        dest_x = (own_tout // slab) // N_CORE
+        sel = (jnp.arange(n_x, dtype=jnp.int32) == dest_x).astype(product.dtype)
+        outgoing = product.reshape(n_pair, 1, p_grp, width) * sel[None, :, None, None]
+        outgoing = outgoing.reshape(n_pair * n_x, p_grp, width)
+        groups = [[d for d in range(n_dev) if d % N_CORE == c] for c in range(N_CORE)]
         held = lax.all_to_all(
-            product.reshape(n_pair, p_grp, width), "pair", 0, 0, tiled=True
+            outgoing, ("pair", "virt"), 0, 0, tiled=True, axis_index_groups=groups
         )
         onebody = one_body(stacked)
         held, onebody = lax.optimization_barrier((held, onebody))
-        blocks = [held]
-        srcs = [virt_idx]
-        for bit in bits:
-            perm = [(v, v ^ bit) for v in range(n_virt)]
-            got = [lax.ppermute(x, "virt", perm) for x in blocks]
-            blocks = blocks + got
-            srcs = srcs + [s ^ bit for s in srcs]
-        allb = jnp.concatenate(blocks, axis=0)
-        src_tiles = jnp.concatenate([jnp.take(tout, s, axis=1) for s in srcs])
+        perm = [(v, v ^ 1) for v in range(n_virt)]
+        other = lax.ppermute(held, "virt", perm)
+        allb = jnp.concatenate([held, other], axis=0)
+        my_core = virt_idx % N_CORE
+        members = jnp.arange(n_dev // N_CORE, dtype=jnp.int32) * N_CORE
+        tout_all = blk_tiles[:, 1]
+        src_tiles = jnp.concatenate(
+            [tout_all[members + my_core], tout_all[members + (1 - my_core)]]
+        )
         one_hot = (src_tiles[:, None] == my_tiles[None, :]).astype(jnp.bfloat16)
         pieces.append(
             jnp.einsum("rpo,rt->pto", allb, one_hot, preferred_element_type=jnp.float32)

time: 58.7 us -> 61.2 us (1.043)
  local copies, waits for them, and re-layouts: 6.76 us -> 10.9 us
  waiting for transfers between devices: 20.2 us -> 16.4 us
  between operations: 0.81 us -> 3.43 us
  starting transfers between devices: 14.8 us -> 14 us
  other arithmetic: 0.39 us -> 1.08 us
    ppermute x3 -> x1, waiting for transfers between devices: 6.15 us -> 0.45 us  [per_device(): other = lax.ppermute(held, 'virt', perm)]
    all_to_all x1, waiting for transfers between devices: 2.51 us -> 7.45 us  [per_device(): lax.all_to_all(outgoing, ('pair', 'virt'), 0, 0, tiled=True, axis_index_g...]
    ppermute x3, waiting for transfers between devices: 9.62 us -> 5.85 us  [per_device(): got.append(lax.ppermute(part, 'virt', perm))]
    ppermute x3 -> x1, starting transfers between devices: 1.43 us -> 0.07 us  [per_device(): other = lax.ppermute(held, 'virt', perm)]
    gather x0 -> x2, local copies, waits for them, and re-layouts: none -> 1.32 us  [the longest x1 0.66 us: per_device(): tout_all[members + (1 - my_core)]]
    optimization_barrier x1, local copies, waits for them, and re-layouts: 0.15 us -> 1.34 us  [per_device(): held, onebody = lax.optimization_barrier((held, onebody))]
    reshape x1, local copies, waits for them, and re-layouts: 0.53 us -> 1.53 us  [per_device(): fock_four = fock_vv.reshape(NVT, TILE, NVT, TILE)]
    mul x0 -> x1, other arithmetic: none -> 0.9 us  [per_device(): product.reshape(n_pair, 1, p_grp, width) * sel[None, :, None, None]]
  transfers between devices with their start and end apart: 8 -> 6, of which waited for: 6 -> 6; matrix products, arithmetic and copies ran while one was open for 13% -> 18% of each run, Pallas kernels for 0% -> 0%
where the time goes in v11:
time: 61.2 us; the launch traced here: 60.8 us
  waiting for transfers between devices  16.4 us (27%)
  matrix products  15 us (25%)
  starting transfers between devices  14 us (23%)
  local copies, waits for them, and re-layouts  10.9 us (18%)
  between operations  3.43 us (6%)
  other arithmetic  1.08 us (2%)
    dot_general x1, matrix products, per_device(): product = jnp.dot(chosen, cols, preferred_element_type=jnp.float32)  8.82 us
    all_to_all x1, waiting for transfers between devices, per_device(): lax.all_to_all(outgoing, ('pair', 'virt'), 0, 0, tiled=True, axis_index_g...  7.45 us
    all_to_all x1, starting transfers between devices, per_device(): chosen = lax.all_to_all(picked, ('pair', 'virt'), 0, 0, tiled=True)  7.33 us
    ppermute x3, waiting for transfers between devices, per_device(): got.append(lax.ppermute(part, 'virt', perm))  5.85 us
    all_to_all x1, starting transfers between devices, per_device(): lax.all_to_all(outgoing, ('pair', 'virt'), 0, 0, tiled=True, axis_index_g...  4.25 us
    dot_general x1, matrix products, one_body(): jnp.einsum('pkqsd,bjqd->pkbsj', sub, fock_four, preferred_element_type=jn...  2.81 us
    all_to_all x1, waiting for transfers between devices, per_device(): chosen = lax.all_to_all(picked, ('pair', 'virt'), 0, 0, tiled=True)  2.67 us
    ppermute x3, starting transfers between devices, per_device(): got.append(lax.ppermute(part, 'virt', perm))  2.34 us
  transfers between devices with their start and end apart: 6, of which 6 were waited for; matrix products, arithmetic and copies ran while one was open for 18% of the time, Pallas kernels for 0%

profile of v11, /device:TPU:0, one launch (start us, length us, event | category | flops | bytes accessed | tf_op | source)
XLA Modules:
  0.0 60.8 jit_solution(1476849211119275101)
XLA Ops:
  0.0 0.8 %slice_bitcast_fusion.1 = (s32[32]{0:T(128)S(1)}, s32[32]{0:T(128)S(1)}, s32[32,1]{0,1:T(1,128)S(1)}) fusion(s32[32,2]{0,1:T(2,128)} %param.8), kind=kLoop, calls=%fused_computation.51 | loop fusion | bytes 640 | tf_op jit(solution)/shard_map/squeeze | solution.py:90
  0.8 1.6 %convolution_convert_fusion = bf16[32,2,4096]{2,0,1:T(8,128)(2,1)S(1)} fusion(bf16[2,64,4096]{2,1,0:T(8,128)(2,1)} %param.5, s32[32]{0:T(128)S(1)} %get-tuple-element.18), kind=kOutput, calls=%fused_computation.4 | convolution fusion | flops 33818624 | bytes 1572992 | tf_op jit(solution)/shard_map/dt,itc->dic/dot_general | solution.py:27
  2.4 1.3 %copy.14 = bf16[32,2,4096]{2,1,0:T(2,128)(2,1)} copy(bf16[32,2,4096]{2,0,1:T(8,128)(2,1)S(1)} %convolution_convert_fusion) | data formatting | bytes 1048576 | tf_op jit(solution)/shard_map/convert_element_type | solution.py:29
  3.8 7.3 %all-to-all-start = ((bf16[32,2,4096]{2,1,0:T(2,128)(2,1)}), bf16[32,2,4096]{2,1,0:T(2,128)(2,1)S(1)}, u32[]{:S(2)}, u32[]{:S(2)}) async-start(bf16[32,2,4096]{2,1,0:T(2,128)(2,1)} %copy.14), calls=%async_computation | async-start | bytes 1048576 | tf_op jit(solution)/shard_map/all_to_all | solution.py:30
  11.2 1.8 %collective-permute-start.1 = (bf16[2,16,2048]{2,1,0:T(8,128)(2,1)S(1)}, bf16[2,16,2048]{2,1,0:T(8,128)(2,1)S(1)}, u32[]{:S(2)}, u32[]{:S(2)}) collective-permute-start(bf16[2,16,2048]{2,1,0:T(8,128)(2,1)S(1)} %get-tuple-element.15), channel_id=1, source_target_pairs={{0,2},{1,3},{2,0},{3,1},{4,6},{5,7},{6,4},{7,5},{8,10},{9,11},{10,... | collective-permute-start | bytes 393224 | tf_op jit(solution)/shard_map/ppermute | solution.py:39
  13.0 0.5 collective-permute-start
  13.5 0.6 %constant_dynamic-slice_fusion = s32[1,1]{0,1:T(1,128)} fusion(s32[32,1]{0,1:T(1,128)S(1)} %get-tuple-element.19, s32[]{:T(128)S(6)} %select_n.76), kind=kLoop, calls=%fused_computation.38 | loop fusion | bytes 12 | tf_op jit(solution)/shard_map/jit(dynamic_index_in_dim)/dynamic_slice | solution.py:56
  16.7 0.6 %dynamic_slice.19 = s32[1]{0:T(128)} dynamic-slice(s32[32]{0:T(128)S(1)} %copy-done.1, s32[]{:T(128)S(6)} %select_n.76), dynamic_slice_sizes={1} | dynamic-slice | bytes 12 | tf_op jit(solution)/shard_map/jit(dynamic_index_in_dim)/dynamic_slice | solution.py:55
  18.0 0.1 mul.72
  18.1 3.5 %collective-permute-done.1 = bf16[2,16,2048]{2,1,0:T(8,128)(2,1)S(1)} collective-permute-done((bf16[2,16,2048]{2,1,0:T(8,128)(2,1)S(1)}, bf16[2,16,2048]{2,1,0:T(8,128)(2,1)S(1)}, u32[]{:S(2)}, u32[]{:S(2)}) %collective-permute-start.1) | collective-permute-done | bytes 131104 | tf_op jit(solution)/shard_map/ppermute | solution.py:39
  21.6 0.8 %collective-permute-done.2 = bf16[2,16,2048]{2,1,0:T(8,128)(2,1)S(1)} collective-permute-done((bf16[2,16,2048]{2,1,0:T(8,128)(2,1)S(1)}, bf16[2,16,2048]{2,1,0:T(8,128)(2,1)S(1)}, u32[]{:S(2)}, u32[]{:S(2)}) %collective-permute-start.2) | collective-permute-done | bytes 131104 | tf_op jit(solution)/shard_map/ppermute | solution.py:39
  22.4 1.6 %collective-permute-done = bf16[2,16,2048]{2,1,0:T(8,128)(2,1)S(1)} collective-permute-done((bf16[2,16,2048]{2,1,0:T(8,128)(2,1)S(1)}, bf16[2,16,2048]{2,1,0:T(8,128)(2,1)S(1)}, u32[]{:S(2)}, u32[]{:S(2)}) %collective-permute-start) | collective-permute-done | bytes 131104 | tf_op jit(solution)/shard_map/ppermute | solution.py:39
  24.0 0.1 pad_maximum_fusion
  24.0 2.7 %all-to-all-done = bf16[32,2,4096]{2,1,0:T(2,128)(2,1)S(1)} async-done(((bf16[32,2,4096]{2,1,0:T(2,128)(2,1)}), bf16[32,2,4096]{2,1,0:T(2,128)(2,1)S(1)}, u32[]{:S(2)}, u32[]{:S(2)}) %all-to-all-start) | async-done | bytes 524320 | tf_op jit(solution)/shard_map/all_to_all | solution.py:30
  26.7 0.2 reshape.77
  26.9 8.8 %fusion.7 = bf16[64,2048]{1,0:T(8,128)(2,1)S(1)} fusion(bf16[64,4096]{1,0:T(8,128)(2,1)S(1)} %reshape.77, bf16[1,4096,2048]{2,1,0:T(8,128)(2,1)} %param.6, f32[]{:T(128)} %bitcast.7), kind=kOutput, calls=%fused_computation.10 | convolution fusion | flops 1074003968 | bytes 17563652 | tf_op jit(solution)/shard_map/dot_general | solution.py:71
  35.7 0.9 %bitcast_multiply_fusion = bf16[16,8,2048]{2,1,0:T(8,128)(2,1)} fusion(bf16[16]{0:T(256)(128)(2,1)S(1)} %mul.72, bf16[8,8,2048]{2,1,0:T(8,128)(2,1)S(1)} %bitcast.57), kind=kLoop, calls=%fused_computation.18 | loop fusion | flops 262144 | bytes 786464 | tf_op jit(solution)/shard_map/mul | solution.py:77
  36.6 4.2 %all-to-all-start.1 = ((bf16[16,8,2048]{2,1,0:T(8,128)(2,1)}), bf16[16,8,2048]{2,1,0:T(8,128)(2,1)}, u32[]{:S(2)}, u32[]{:S(2)}) async-start(bf16[16,8,2048]{2,1,0:T(8,128)(2,1)} %bitcast_multiply_fusion), calls=%async_computation.1 | async-start | bytes 1048576 | tf_op jit(solution)/shard_map/all_to_all | solution.py:80
  40.9 1.5 %reshape.79 = bf16[8,64,8,64]{3,2,1,0:T(8,128)(2,1)} reshape(bf16[512,512]{1,0:T(8,128)(2,1)S(1)} %copy-done) | data formatting | bytes 1048576 | tf_op jit(solution)/shard_map/reshape | solution.py:43
  42.5 0.6 convolution_convert_fusion.1
  43.0 0.3 copy.16
  43.3 2.1 %reshape.99 = bf16[8,2,8,32,64,1]{4,3,2,1,0,5:T(8,128)(2,1)} reshape(bf16[4,2,16,2048]{3,2,1,0:T(8,128)(2,1)S(1)} %copy.16) | data formatting | bytes 1048576 | tf_op jit(solution)/shard_map/reshape | solution.py:50
  45.4 2.8 %convolution_bitcast_fusion.1 = f32[8,2,8,32,64]{4,3,2,1,0:T(8,128)S(1)} fusion(bf16[8,64,8,64,1,1]{3,2,1,0,5,4:T(8,128)(2,1)} %bitcast.58, bf16[8,2,8,32,64,1]{4,3,2,1,0,5:T(8,128)(2,1)} %reshape.99), kind=kOutput, calls=%fused_computation.11 | convolution fusion | flops 268435456 | bytes 2097152 | tf_op jit(solution)/shard_map/pkqsd,bjqd->pkbsj/dot_general | solution.py:51
  48.2 0.7 %reshape.80 = f32[8,16,2048]{2,1,0:T(8,128)S(1)} reshape(f32[8,2,8,32,64]{4,3,2,1,0:T(8,128)S(1)} %convolution_bitcast_fusion.1) | data formatting | bytes 2097152 | tf_op jit(solution)/shard_map/reshape | solution.py:53
  48.8 7.4 %all-to-all-done.1 = bf16[16,8,2048]{2,1,0:T(8,128)(2,1)} async-done(((bf16[16,8,2048]{2,1,0:T(8,128)(2,1)}), bf16[16,8,2048]{2,1,0:T(8,128)(2,1)}, u32[]{:S(2)}, u32[]{:S(2)}) %all-to-all-start.1) | async-done | bytes 524320 | tf_op jit(solution)/shard_map/all_to_all | solution.py:80
  56.3 1.3 %copy.19 = bf16[16,8,2048]{2,0,1:T(8,128)(2,1)S(1)} copy(bf16[16,8,2048]{2,1,0:T(8,128)(2,1)} %all-to-all-done.1) | data formatting | bytes 1048576 | tf_op jit(solution)/shard_map/optimization_barrier | solution.py:84
  57.6 0.1 collective-permute-start.3
  57.7 0.7 %gather_fusion = s32[16]{0:T(128)S(1)} fusion(s32[32]{0:T(128)S(1)} %get-tuple-element.17, s32[1024]{0:T(1024)S(1)} %pad_clamp_fusion.1), kind=kCustom, calls=%fused_computation | custom fusion | bytes 192 | tf_op jit(solution)/shard_map/gather | solution.py:92
  58.4 0.7 %gather_fusion.1 = s32[16]{0:T(128)S(1)} fusion(s32[32]{0:T(128)S(1)} %get-tuple-element.17, s32[1024]{0:T(1024)S(1)} %pad_clamp_fusion), kind=kCustom, calls=%fused_computation.1 | custom fusion | bytes 192 | tf_op jit(solution)/shard_map/gather | solution.py:92
  59.1 0.1 pad_add_fusion
  59.2 0.4 collective-permute-done.3
  59.6 1.1 %fusion.3 = bf16[8,16,2048]{2,1,0:T(8,128)(2,1)} fusion(f32[8,16,2048]{2,1,0:T(8,128)S(1)} %reshape.80, bf16[16,8,2048]{2,0,1:T(8,128)(2,1)S(1)} %collective-permute-done.3, bf16[16,8,2048]{2,0,1:T(8,128)(2,1)S(1)} %copy.19, s32[32]{0:T(128)S(1)} %pad_add_fusion, s32[16]{0:T(128)S(1)} %iota_add_fusion), kind=kOutput, calls=%fused_computation.7 | convolution fusion | flops 19399168 | bytes 2621632 | tf_op jit(solution)/shard_map/rpo,rt->pto/dot_general | solution.py:96
  (15 shorter events, 0.1 us)
Async XLA Ops:
  0.8 10.4 %slice-start = ((bf16[2,64,4096]{2,1,0:T(8,128)(2,1)}), bf16[2,64,2048]{2,1,0:T(8,128)(2,1)S(1)}, s32[]{:S(2)}) async-start(bf16[2,64,4096]{2,1,0:T(8,128)(2,1)} %param.5), calls=%async_computation.2 | async-start | bytes 1048576 | tf_op jit(solution)/shard_map/slice | solution.py:33
  2.4 14.3 %copy-start.1 = (s32[32]{0:T(128)S(1)}, s32[32]{0:T(128)}, u32[]{:S(2)}) copy-start(s32[32]{0:T(128)} %param.9) | copy-start | bytes 388
  3.8 22.9 %all-to-all-start = ((bf16[32,2,4096]{2,1,0:T(2,128)(2,1)}), bf16[32,2,4096]{2,1,0:T(2,128)(2,1)S(1)}, u32[]{:S(2)}, u32[]{:S(2)}) async-start(bf16[32,2,4096]{2,1,0:T(2,128)(2,1)} %copy.14), calls=%async_computation | async-start | bytes 1048576 | tf_op jit(solution)/shard_map/all_to_all | solution.py:30
  11.2 10.4 %collective-permute-start.1 = (bf16[2,16,2048]{2,1,0:T(8,128)(2,1)S(1)}, bf16[2,16,2048]{2,1,0:T(8,128)(2,1)S(1)}, u32[]{:S(2)}, u32[]{:S(2)}) collective-permute-start(bf16[2,16,2048]{2,1,0:T(8,128)(2,1)S(1)} %get-tuple-element.15), channel_id=1, source_target_pairs={{0,2},{1,3},{2,0},{3,1},{4,6},{5,7},{6,4},{7,5},{8,10},{9,11},{10,... | collective-permute-start | bytes 393224 | tf_op jit(solution)/shard_map/ppermute | solution.py:39
  13.0 9.3 %collective-permute-start.2 = (bf16[2,16,2048]{2,1,0:T(8,128)(2,1)S(1)}, bf16[2,16,2048]{2,1,0:T(8,128)(2,1)S(1)}, u32[]{:S(2)}, u32[]{:S(2)}) collective-permute-start(bf16[2,16,2048]{2,1,0:T(8,128)(2,1)S(1)} %get-tuple-element.14), channel_id=1, source_target_pairs={{0,3},{1,0},{2,1},{3,2},{4,7},{5,4},{6,5},{7,6},{8,11},{9,8},{10,9... | collective-permute-start | bytes 393224 | tf_op jit(solution)/shard_map/ppermute | solution.py:39
  13.0 10.9 %collective-permute-start = (bf16[2,16,2048]{2,1,0:T(8,128)(2,1)S(1)}, bf16[2,16,2048]{2,1,0:T(8,128)(2,1)S(1)}, u32[]{:S(2)}, u32[]{:S(2)}) collective-permute-start(bf16[2,16,2048]{2,1,0:T(8,128)(2,1)S(1)} %get-tuple-element.16), channel_id=1, source_target_pairs={{0,1},{1,2},{2,3},{3,0},{4,5},{5,6},{6,7},{7,4},{8,9},{9,10},{10,1... | collective-permute-start | bytes 393224 | tf_op jit(solution)/shard_map/ppermute | solution.py:39
  35.7 5.2 %copy-start = (bf16[512,512]{1,0:T(8,128)(2,1)S(1)}, bf16[512,512]{1,0:T(8,128)(2,1)}, u32[]{:S(2)}) copy-start(bf16[512,512]{1,0:T(8,128)(2,1)} %param.7) | copy-start | bytes 1572868
  36.6 19.7 %all-to-all-start.1 = ((bf16[16,8,2048]{2,1,0:T(8,128)(2,1)}), bf16[16,8,2048]{2,1,0:T(8,128)(2,1)}, u32[]{:S(2)}, u32[]{:S(2)}) async-start(bf16[16,8,2048]{2,1,0:T(8,128)(2,1)} %bitcast_multiply_fusion), calls=%async_computation.1 | async-start | bytes 1048576 | tf_op jit(solution)/shard_map/all_to_all | solution.py:80
  57.6 2.0 %collective-permute-start.3 = (bf16[16,8,2048]{2,0,1:T(8,128)(2,1)S(1)}, bf16[16,8,2048]{2,0,1:T(8,128)(2,1)S(1)}, u32[]{:S(2)}, u32[]{:S(2)}) collective-permute-start(bf16[16,8,2048]{2,0,1:T(8,128)(2,1)S(1)} %copy.19), channel_id=1, source_target_pairs={{0,1},{1,0},{2,3},{3,2},{4,5},{5,4},{6,7},{7,6},{8,9},{9,8},{10,11... | collective-permute-start | bytes 1572872 | tf_op jit(solution)/shard_map/ppermute | solution.py:86

commit v12 on v9

--- a/solution.py
+++ b/solution.py
@@ -20,14 +20,17 @@
     virt_idx = lax.axis_index("virt")
     p_grp = pm_rows * n_virt
 
-    tin_all = blk_tiles[:, 0]
+    slot = jnp.arange(n_dev, dtype=jnp.int32)
+    tin_all = blk_tiles[(slot % n_pair) * n_virt + slot // n_pair, 0]
     tile_ids = jnp.arange(n_tiles, dtype=jnp.int32)
     pick = (tin_all[:, None] == tile_ids[None, :]).astype(amps_pm.dtype)
     picked = jnp.einsum(
         "dt,itc->dic", pick, amps_pm, preferred_element_type=jnp.float32
     ).astype(amps_pm.dtype)
-    chosen = lax.all_to_all(picked, ("pair", "virt"), 0, 0, tiled=True)
-    chosen = chosen.reshape(n_dev * pm_rows, tile_len)
+    chosen = lax.all_to_all(picked, ("virt", "pair"), 0, 0, tiled=True)
+    chosen = jnp.transpose(
+        chosen.reshape(n_virt, n_pair, pm_rows, tile_len), (1, 0, 2, 3)
+    ).reshape(n_dev * pm_rows, tile_len)
 
     got = [lax.dynamic_slice_in_dim(amps_pm[:, :, :out_cols], virt_idx * slab, slab, 1)]
     for k in range(1, n_virt):

time: 58.7 us -> 60.5 us (1.031)
  waiting for transfers between devices: 20.2 us -> 21.5 us
  local copies, waits for them, and re-layouts: 6.76 us -> 7.92 us
  starting transfers between devices: 14.8 us -> 14.1 us
    gather x0 -> x1, local copies, waits for them, and re-layouts: none -> 1.44 us  [per_device(): tin_all = blk_tiles[slot % n_pair * n_virt + slot // n_pair, 0]]
    all_to_all x1, waiting for transfers between devices: 1.91 us -> 2.76 us  [per_device(): chosen = lax.all_to_all(picked, ('virt', 'pair'), 0, 0, tiled=True)]
    slice x1, local copies, waits for them, and re-layouts: 0.77 us -> 0.02 us  [per_device(): tout = blk_tiles[:, 1].reshape(n_pair, n_virt)]
where the time goes in v12:
time: 60.5 us; the launch traced here: 60.1 us
  waiting for transfers between devices  21.5 us (36%)
  matrix products  15.3 us (25%)
  starting transfers between devices  14.1 us (23%)
  local copies, waits for them, and re-layouts  7.92 us (13%)
  between operations  0.85 us (1%)
    dot_general x1, matrix products, per_device(): product = jnp.dot(chosen, cols, preferred_element_type=jnp.float32)  9.5 us
    ppermute x3, waiting for transfers between devices, per_device(): got.append(lax.ppermute(part, 'virt', perm))  9.39 us
    all_to_all x1, starting transfers between devices, per_device(): chosen = lax.all_to_all(picked, ('virt', 'pair'), 0, 0, tiled=True)  7.32 us
    ppermute x3, waiting for transfers between devices, per_device(): got = [lax.ppermute(x, 'virt', perm) for x in blocks]  6.42 us
    all_to_all x1, starting transfers between devices, per_device(): lax.all_to_all(product.reshape(n_pair, p_grp, width), 'pair', 0, 0, tiled...  3.46 us
    all_to_all x1, waiting for transfers between devices, per_device(): lax.all_to_all(product.reshape(n_pair, p_grp, width), 'pair', 0, 0, tiled...  2.96 us
    all_to_all x1, waiting for transfers between devices, per_device(): chosen = lax.all_to_all(picked, ('virt', 'pair'), 0, 0, tiled=True)  2.76 us
    dot_general x1, matrix products, one_body(): jnp.einsum('pkqsd,bjqd->pkbsj', sub, fock_four, preferred_element_type=jn...  2.49 us
  transfers between devices with their start and end apart: 8, of which 6 were waited for; matrix products, arithmetic and copies ran while one was open for 13% of the time, Pallas kernels for 0%

profile of v12, /device:TPU:0, one launch (start us, length us, event | category | flops | bytes accessed | tf_op | source)
XLA Modules:
  0.0 60.1 jit_solution(740013916608391037)
XLA Ops:
  0.0 1.4 %gather_fusion = s32[32]{0:T(128)S(1)} fusion(s32[32,2]{0,1:T(2,128)} %param.10, s32[32]{0:T(128)S(1)} %fusion.34), kind=kCustom, calls=%fused_computation | custom fusion | bytes 512 | tf_op jit(solution)/shard_map/gather | solution.py:24
  1.5 1.6 %convolution_convert_fusion = bf16[32,2,4096]{2,0,1:T(8,128)(2,1)S(1)} fusion(bf16[2,64,4096]{2,1,0:T(8,128)(2,1)} %param.7, s32[32]{0:T(128)S(1)} %gather_fusion), kind=kOutput, calls=%fused_computation.3 | convolution fusion | flops 33818624 | bytes 1572992 | tf_op jit(solution)/shard_map/dt,itc->dic/dot_general | solution.py:27
  3.1 0.0 copy-start.2
  3.1 1.3 %copy.14 = bf16[32,2,4096]{2,1,0:T(2,128)(2,1)} copy(bf16[32,2,4096]{2,0,1:T(8,128)(2,1)S(1)} %convolution_convert_fusion) | data formatting | bytes 1048576 | tf_op jit(solution)/shard_map/convert_element_type | solution.py:29
  4.5 7.3 %all-to-all-start = ((bf16[32,2,4096]{2,1,0:T(2,128)(2,1)}), bf16[32,2,4096]{2,1,0:T(2,128)(2,1)S(1)}, u32[]{:S(2)}, u32[]{:S(2)}) async-start(bf16[32,2,4096]{2,1,0:T(2,128)(2,1)} %copy.14), calls=%async_computation | async-start | bytes 1048576 | tf_op jit(solution)/shard_map/all_to_all | solution.py:30
  11.9 1.5 %collective-permute-start.2 = (bf16[2,16,2048]{2,1,0:T(8,128)(2,1)S(1)}, bf16[2,16,2048]{2,1,0:T(8,128)(2,1)S(1)}, u32[]{:S(2)}, u32[]{:S(2)}) collective-permute-start(bf16[2,16,2048]{2,1,0:T(8,128)(2,1)S(1)} %get-tuple-element.30), channel_id=1, source_target_pairs={{0,3},{1,0},{2,1},{3,2},{4,7},{5,4},{6,5},{7,6},{8,11},{9,8},{10,9... | collective-permute-start | bytes 393224 | tf_op jit(solution)/shard_map/ppermute | solution.py:41
  13.4 0.4 collective-permute-start.1
  13.8 0.1 collective-permute-start
  14.0 0.6 %dynamic_slice.16 = s32[1]{0:T(128)} dynamic-slice(s32[32]{0:T(128)S(1)} %copy-done.2, s32[]{:T(128)S(6)} %select_n.85), dynamic_slice_sizes={1} | dynamic-slice | bytes 12 | tf_op jit(solution)/shard_map/jit(dynamic_index_in_dim)/dynamic_slice | solution.py:57
  15.3 0.5 reshape.109
  15.8 3.5 %collective-permute-done.2 = bf16[2,16,2048]{2,1,0:T(8,128)(2,1)S(1)} collective-permute-done((bf16[2,16,2048]{2,1,0:T(8,128)(2,1)S(1)}, bf16[2,16,2048]{2,1,0:T(8,128)(2,1)S(1)}, u32[]{:S(2)}, u32[]{:S(2)}) %collective-permute-start.2) | collective-permute-done | bytes 131104 | tf_op jit(solution)/shard_map/ppermute | solution.py:41
  19.3 5.9 %collective-permute-done.1 = bf16[2,16,2048]{2,1,0:T(8,128)(2,1)S(1)} collective-permute-done((bf16[2,16,2048]{2,1,0:T(8,128)(2,1)S(1)}, bf16[2,16,2048]{2,1,0:T(8,128)(2,1)S(1)}, u32[]{:S(2)}, u32[]{:S(2)}) %collective-permute-start.1) | collective-permute-done | bytes 131104 | tf_op jit(solution)/shard_map/ppermute | solution.py:41
  25.2 0.1 pad_maximum_fusion
  25.3 2.8 %all-to-all-done = bf16[32,2,4096]{2,1,0:T(2,128)(2,1)S(1)} async-done(((bf16[32,2,4096]{2,1,0:T(2,128)(2,1)}), bf16[32,2,4096]{2,1,0:T(2,128)(2,1)S(1)}, u32[]{:S(2)}, u32[]{:S(2)}) %all-to-all-start) | async-done | bytes 524320 | tf_op jit(solution)/shard_map/all_to_all | solution.py:30
  28.0 0.5 copy.33
  28.5 0.2 reshape.106
  28.7 9.5 %fusion.7 = bf16[64,2048]{1,0:T(8,128)(2,1)} fusion(bf16[64,4096]{1,0:T(8,128)(2,1)S(1)} %reshape.106, bf16[1,4096,2048]{2,1,0:T(8,128)(2,1)} %param.8, f32[]{:T(128)} %bitcast.6), kind=kOutput, calls=%fused_computation.9 | convolution fusion | flops 1074003968 | bytes 17563652 | tf_op jit(solution)/shard_map/dot_general | solution.py:72
  38.2 3.5 %all-to-all-start.1 = ((bf16[8,8,2048]{2,1,0:T(8,128)(2,1)}), bf16[8,8,2048]{2,1,0:T(8,128)(2,1)S(1)}, u32[]{:S(2)}, u32[]{:S(2)}) async-start(bf16[8,8,2048]{2,1,0:T(8,128)(2,1)} %bitcast.11), calls=%async_computation.1 | async-start | bytes 524288 | tf_op jit(solution)/shard_map/all_to_all | solution.py:75
  41.7 0.5 convolution_convert_fusion.1
  42.2 0.3 copy.17
  42.5 2.0 %reshape.212 = bf16[8,2,8,32,64,1]{4,3,2,1,0,5:T(8,128)(2,1)} reshape(bf16[4,2,16,2048]{3,2,1,0:T(8,128)(2,1)S(1)} %copy.17) | data formatting | bytes 1048576 | tf_op jit(solution)/shard_map/reshape | solution.py:52
  44.6 2.5 %convolution_bitcast_fusion.1 = f32[8,2,8,32,64]{4,3,2,1,0:T(8,128)S(1)} fusion(bf16[8,64,8,64,1,1]{3,2,1,0,5,4:T(8,128)(2,1)S(1)} %bitcast.54, bf16[8,2,8,32,64,1]{4,3,2,1,0,5:T(8,128)(2,1)} %reshape.212), kind=kOutput, calls=%fused_computation.10 | convolution fusion | flops 268435456 | bytes 2097152 | tf_op jit(solution)/shard_map/pkqsd,bjqd->pkbsj/dot_general | solution.py:53
  47.1 0.7 %reshape.110 = f32[8,16,2048]{2,1,0:T(8,128)S(1)} reshape(f32[8,2,8,32,64]{4,3,2,1,0:T(8,128)S(1)} %convolution_bitcast_fusion.1) | data formatting | bytes 2097152 | tf_op jit(solution)/shard_map/reshape | solution.py:55
  47.7 3.0 %all-to-all-done.1 = bf16[8,8,2048]{2,1,0:T(8,128)(2,1)S(1)} async-done(((bf16[8,8,2048]{2,1,0:T(8,128)(2,1)}), bf16[8,8,2048]{2,1,0:T(8,128)(2,1)S(1)}, u32[]{:S(2)}, u32[]{:S(2)}) %all-to-all-start.1) | async-done | bytes 262176 | tf_op jit(solution)/shard_map/all_to_all | solution.py:75
  50.7 0.1 copy.21
  50.9 1.2 %collective-permute-start.3 = (bf16[8,8,2048]{2,0,1:T(8,128)(2,1)S(1)}, bf16[8,8,2048]{2,0,1:T(8,128)(2,1)S(1)}, u32[]{:S(2)}, u32[]{:S(2)}) collective-permute-start(bf16[8,8,2048]{2,0,1:T(8,128)(2,1)S(1)} %copy.21), channel_id=1, source_target_pairs={{0,2},{1,3},{2,0},{3,1},{4,6},{5,7},{6,4},{7,5},{8,10},{9,11},{10,... | collective-permute-start | bytes 786440 | tf_op jit(solution)/shard_map/ppermute | solution.py:84
  52.1 5.3 %collective-permute-done.3 = bf16[8,8,2048]{2,0,1:T(8,128)(2,1)S(1)} collective-permute-done((bf16[8,8,2048]{2,0,1:T(8,128)(2,1)S(1)}, bf16[8,8,2048]{2,0,1:T(8,128)(2,1)S(1)}, u32[]{:S(2)}, u32[]{:S(2)}) %collective-permute-start.3) | collective-permute-done | bytes 262176 | tf_op jit(solution)/shard_map/ppermute | solution.py:84
  57.5 0.1 reshape_squeeze.3
  57.6 0.2 select_reduce_fusion.3
  57.8 0.1 pad_add_fusion
  57.9 1.1 %collective-permute-done.5 = bf16[8,8,2048]{2,0,1:T(8,128)(2,1)S(1)} collective-permute-done((bf16[8,8,2048]{2,0,1:T(8,128)(2,1)S(1)}, bf16[8,8,2048]{2,0,1:T(8,128)(2,1)S(1)}, u32[]{:S(2)}, u32[]{:S(2)}) %collective-permute-start.5) | collective-permute-done | bytes 262176 | tf_op jit(solution)/shard_map/ppermute | solution.py:84
  59.0 1.2 %fusion.3 = bf16[8,16,2048]{2,1,0:T(8,128)(2,1)} fusion(f32[8,16,2048]{2,1,0:T(8,128)S(1)} %reshape.110, bf16[8,8,2048]{2,0,1:T(8,128)(2,1)S(1)} %collective-permute-done.5, bf16[8,8,2048]{2,0,1:T(8,128)(2,1)S(1)} %collective-permute-done.4, bf16[8,8,2048]{2,0,1:T(8,128)(2,1)S(1)} %collective-permute-done.3, bf16[8,8,2048]{2,0,1:T(8,128)(2,1)S(1)} %copy.21, ...), kind=kOutput, calls=%fused_computation.6 | convolution fusion | flops 21496320 | bytes 2621632 | tf_op jit(solution)/shard_map/rpo,rt->pto/dot_general | solution.py:91
  (16 shorter events, 0.1 us)
Async XLA Ops:
  1.4 10.4 %slice-start = ((bf16[2,64,4096]{2,1,0:T(8,128)(2,1)}), bf16[2,64,2048]{2,1,0:T(8,128)(2,1)S(1)}, s32[]{:S(2)}) async-start(bf16[2,64,4096]{2,1,0:T(8,128)(2,1)} %param.7), calls=%async_computation.2 | async-start | bytes 1048576 | tf_op jit(solution)/shard_map/slice | solution.py:35
  3.1 10.9 %copy-start.2 = (s32[32]{0:T(128)S(1)}, s32[32]{0:T(128)}, u32[]{:S(2)}) copy-start(s32[32]{0:T(128)} %param.11) | copy-start | bytes 388
  3.1 12.1 %copy-start.1 = (bf16[512,512]{1,0:T(8,128)(2,1)S(1)}, bf16[512,512]{1,0:T(8,128)(2,1)}, u32[]{:S(2)}) copy-start(bf16[512,512]{1,0:T(8,128)(2,1)} %param.9) | copy-start | bytes 1572868
  4.5 23.6 %all-to-all-start = ((bf16[32,2,4096]{2,1,0:T(2,128)(2,1)}), bf16[32,2,4096]{2,1,0:T(2,128)(2,1)S(1)}, u32[]{:S(2)}, u32[]{:S(2)}) async-start(bf16[32,2,4096]{2,1,0:T(2,128)(2,1)} %copy.14), calls=%async_computation | async-start | bytes 1048576 | tf_op jit(solution)/shard_map/all_to_all | solution.py:30
  11.9 7.4 %collective-permute-start.2 = (bf16[2,16,2048]{2,1,0:T(8,128)(2,1)S(1)}, bf16[2,16,2048]{2,1,0:T(8,128)(2,1)S(1)}, u32[]{:S(2)}, u32[]{:S(2)}) collective-permute-start(bf16[2,16,2048]{2,1,0:T(8,128)(2,1)S(1)} %get-tuple-element.30), channel_id=1, source_target_pairs={{0,3},{1,0},{2,1},{3,2},{4,7},{5,4},{6,5},{7,6},{8,11},{9,8},{10,9... | collective-permute-start | bytes 393224 | tf_op jit(solution)/shard_map/ppermute | solution.py:41
  13.4 11.7 %collective-permute-start.1 = (bf16[2,16,2048]{2,1,0:T(8,128)(2,1)S(1)}, bf16[2,16,2048]{2,1,0:T(8,128)(2,1)S(1)}, u32[]{:S(2)}, u32[]{:S(2)}) collective-permute-start(bf16[2,16,2048]{2,1,0:T(8,128)(2,1)S(1)} %get-tuple-element.31), channel_id=1, source_target_pairs={{0,2},{1,3},{2,0},{3,1},{4,6},{5,7},{6,4},{7,5},{8,10},{9,11},{10,... | collective-permute-start | bytes 393224 | tf_op jit(solution)/shard_map/ppermute | solution.py:41
  13.8 11.4 %collective-permute-start = (bf16[2,16,2048]{2,1,0:T(8,128)(2,1)S(1)}, bf16[2,16,2048]{2,1,0:T(8,128)(2,1)S(1)}, u32[]{:S(2)}, u32[]{:S(2)}) collective-permute-start(bf16[2,16,2048]{2,1,0:T(8,128)(2,1)S(1)} %get-tuple-element.32), channel_id=1, source_target_pairs={{0,1},{1,2},{2,3},{3,0},{4,5},{5,6},{6,7},{7,4},{8,9},{9,10},{10,1... | collective-permute-start | bytes 393224 | tf_op jit(solution)/shard_map/ppermute | solution.py:41
  38.2 12.5 %all-to-all-start.1 = ((bf16[8,8,2048]{2,1,0:T(8,128)(2,1)}), bf16[8,8,2048]{2,1,0:T(8,128)(2,1)S(1)}, u32[]{:S(2)}, u32[]{:S(2)}) async-start(bf16[8,8,2048]{2,1,0:T(8,128)(2,1)} %bitcast.11), calls=%async_computation.1 | async-start | bytes 524288 | tf_op jit(solution)/shard_map/all_to_all | solution.py:75
  47.1 10.4 %copy-start = (s32[32,2]{0,1:T(2,128)S(1)}, s32[32,2]{0,1:T(2,128)}, u32[]{:S(2)}) copy-start(s32[32,2]{0,1:T(2,128)} %param.10) | copy-start | bytes 772
  50.9 6.6 %collective-permute-start.3 = (bf16[8,8,2048]{2,0,1:T(8,128)(2,1)S(1)}, bf16[8,8,2048]{2,0,1:T(8,128)(2,1)S(1)}, u32[]{:S(2)}, u32[]{:S(2)}) collective-permute-start(bf16[8,8,2048]{2,0,1:T(8,128)(2,1)S(1)} %copy.21), channel_id=1, source_target_pairs={{0,2},{1,3},{2,0},{3,1},{4,6},{5,7},{6,4},{7,5},{8,10},{9,11},{10,... | collective-permute-start | bytes 786440 | tf_op jit(solution)/shard_map/ppermute | solution.py:84
  52.1 5.8 %collective-permute-start.4 = (bf16[8,8,2048]{2,0,1:T(8,128)(2,1)S(1)}, bf16[8,8,2048]{2,0,1:T(8,128)(2,1)S(1)}, u32[]{:S(2)}, u32[]{:S(2)}) collective-permute-start(bf16[8,8,2048]{2,0,1:T(8,128)(2,1)S(1)} %copy.21), channel_id=1, source_target_pairs={{0,1},{1,0},{2,3},{3,2},{4,5},{5,4},{6,7},{7,6},{8,9},{9,8},{10,11... | collective-permute-start | bytes 786440 | tf_op jit(solution)/shard_map/ppermute | solution.py:84
  57.4 1.5 %collective-permute-start.5 = (bf16[8,8,2048]{2,0,1:T(8,128)(2,1)S(1)}, bf16[8,8,2048]{2,0,1:T(8,128)(2,1)S(1)}, u32[]{:S(2)}, u32[]{:S(2)}) collective-permute-start(bf16[8,8,2048]{2,0,1:T(8,128)(2,1)S(1)} %collective-permute-done.3), channel_id=1, source_target_pairs={{0,1},{1,0},{2,3},{3,2},{4,5},{5,4},{6,7},{7,6},{8,9},{9,8},{10,11... | collective-permute-start | bytes 786440 | tf_op jit(solution)/shard_map/ppermute | solution.py:84

commit v13 on v9

--- a/solution.py
+++ b/solution.py
@@ -20,9 +20,11 @@
     virt_idx = lax.axis_index("virt")
     p_grp = pm_rows * n_virt
 
-    tin_all = blk_tiles[:, 0]
     tile_ids = jnp.arange(n_tiles, dtype=jnp.int32)
-    pick = (tin_all[:, None] == tile_ids[None, :]).astype(amps_pm.dtype)
+    col_in = (jnp.arange(2, dtype=jnp.int32) == 0)[None, :, None]
+    pick = jnp.any(
+        (blk_tiles[:, :, None] == tile_ids[None, None, :]) & col_in, axis=1
+    ).astype(amps_pm.dtype)
     picked = jnp.einsum(
         "dt,itc->dic", pick, amps_pm, preferred_element_type=jnp.float32
     ).astype(amps_pm.dtype)

time: 58.7 us -> 58.6 us (level)
  other arithmetic: 0.39 us -> 1.15 us
  local copies, waits for them, and re-layouts: 6.76 us -> 6.06 us
    reduce_or x0 -> x1, other arithmetic: none -> 0.76 us  [per_device(): jnp.any((blk_tiles[:, :, None] == tile_ids[None, None, :]) & col_in, axis=1)]
    slice x1, local copies, waits for them, and re-layouts: 0.77 us -> 0.02 us  [per_device(): tout = blk_tiles[:, 1].reshape(n_pair, n_virt)]
where the time goes in v13:
time: 58.6 us; the launch traced here: 58.2 us
  waiting for transfers between devices  20 us (34%)
  matrix products  15.3 us (26%)
  starting transfers between devices  14.8 us (25%)
  local copies, waits for them, and re-layouts  6.06 us (10%)
  other arithmetic  1.15 us (2%)
  between operations  0.92 us (2%)
    ppermute x3, waiting for transfers between devices, per_device(): got.append(lax.ppermute(part, 'virt', perm))  9.54 us
    dot_general x1, matrix products, per_device(): product = jnp.dot(chosen, cols, preferred_element_type=jnp.float32)  9.5 us
    all_to_all x1, starting transfers between devices, per_device(): chosen = lax.all_to_all(picked, ('pair', 'virt'), 0, 0, tiled=True)  7.33 us
    ppermute x3, waiting for transfers between devices, per_device(): got = [lax.ppermute(x, 'virt', perm) for x in blocks]  6.09 us
    all_to_all x1, starting transfers between devices, per_device(): lax.all_to_all(product.reshape(n_pair, p_grp, width), 'pair', 0, 0, tiled...  4.03 us
    dot_general x1, matrix products, one_body(): jnp.einsum('pkqsd,bjqd->pkbsj', sub, fock_four, preferred_element_type=jn...  2.49 us
    all_to_all x1, waiting for transfers between devices, per_device(): lax.all_to_all(product.reshape(n_pair, p_grp, width), 'pair', 0, 0, tiled...  2.48 us
    reshape x1, local copies, waits for them, and re-layouts, one_body(): sub = sub.reshape(p_grp, slab // NVT, NVT, AS, TILE)  2.06 us
  transfers between devices with their start and end apart: 8, of which 6 were waited for; matrix products, arithmetic and copies ran while one was open for 13% of the time, Pallas kernels for 0%

profile of v13, /device:TPU:0, one launch (start us, length us, event | category | flops | bytes accessed | tf_op | source)
XLA Modules:
  0.0 58.2 jit_solution(11321129174042103015)
XLA Ops:
  0.0 0.8 %fusion.21 = pred[32,64]{1,0:T(8,128)(4,1)S(1)} fusion(s32[32,2]{0,1:T(2,128)} %param.10, pred[2]{0:T(512)(128)(4,1)S(1)} %iota_compare_fusion.2), kind=kLoop, calls=%fused_computation.24 | loop fusion | flops 10240 | bytes 2306 | tf_op jit(solution)/shard_map/reduce_or | solution.py:25
  0.8 0.0 slice-start
  0.8 1.6 %convolution_convert_fusion = bf16[32,2,4096]{2,0,1:T(8,128)(2,1)S(1)} fusion(bf16[2,64,4096]{2,1,0:T(8,128)(2,1)} %param.7, pred[32,64]{1,0:T(8,128)(4,1)S(1)} %fusion.21), kind=kOutput, calls=%fused_computation.2 | convolution fusion | flops 33816576 | bytes 1574912 | tf_op jit(solution)/shard_map/dt,itc->dic/dot_general | solution.py:28
  2.4 1.3 %copy.24 = bf16[32,2,4096]{2,1,0:T(2,128)(2,1)} copy(bf16[32,2,4096]{2,0,1:T(8,128)(2,1)S(1)} %convolution_convert_fusion) | data formatting | bytes 1048576 | tf_op jit(solution)/shard_map/convert_element_type | solution.py:30
  3.7 7.3 %all-to-all-start = ((bf16[32,2,4096]{2,1,0:T(2,128)(2,1)}), bf16[32,2,4096]{2,1,0:T(2,128)(2,1)S(1)}, u32[]{:S(2)}, u32[]{:S(2)}) async-start(bf16[32,2,4096]{2,1,0:T(2,128)(2,1)} %copy.24), calls=%async_computation | async-start | bytes 1048576 | tf_op jit(solution)/shard_map/all_to_all | solution.py:31
  11.1 0.1 dynamic-slice_bitcast_fusion
  11.2 1.5 %collective-permute-start.2 = (bf16[2,16,2048]{2,1,0:T(8,128)(2,1)S(1)}, bf16[2,16,2048]{2,1,0:T(8,128)(2,1)S(1)}, u32[]{:S(2)}, u32[]{:S(2)}) collective-permute-start(bf16[2,16,2048]{2,1,0:T(8,128)(2,1)S(1)} %get-tuple-element.30), channel_id=1, source_target_pairs={{0,3},{1,0},{2,1},{3,2},{4,7},{5,4},{6,5},{7,6},{8,11},{9,8},{10,9... | collective-permute-start | bytes 393224 | tf_op jit(solution)/shard_map/ppermute | solution.py:40
  12.7 0.4 collective-permute-start.1
  13.1 0.1 collective-permute-start
  13.2 0.7 %dynamic_slice.16 = s32[1]{0:T(128)} dynamic-slice(s32[32]{0:T(128)S(1)} %copy-done.2, s32[]{:T(128)S(6)} %select_n.47), dynamic_slice_sizes={1} | dynamic-slice | bytes 12 | tf_op jit(solution)/shard_map/jit(dynamic_index_in_dim)/dynamic_slice | solution.py:56
  14.6 0.5 reshape.45
  15.1 3.9 %collective-permute-done.2 = bf16[2,16,2048]{2,1,0:T(8,128)(2,1)S(1)} collective-permute-done((bf16[2,16,2048]{2,1,0:T(8,128)(2,1)S(1)}, bf16[2,16,2048]{2,1,0:T(8,128)(2,1)S(1)}, u32[]{:S(2)}, u32[]{:S(2)}) %collective-permute-start.2) | collective-permute-done | bytes 131104 | tf_op jit(solution)/shard_map/ppermute | solution.py:40
  19.0 5.7 %collective-permute-done.1 = bf16[2,16,2048]{2,1,0:T(8,128)(2,1)S(1)} collective-permute-done((bf16[2,16,2048]{2,1,0:T(8,128)(2,1)S(1)}, bf16[2,16,2048]{2,1,0:T(8,128)(2,1)S(1)}, u32[]{:S(2)}, u32[]{:S(2)}) %collective-permute-start.1) | collective-permute-done | bytes 131104 | tf_op jit(solution)/shard_map/ppermute | solution.py:40
  24.7 0.1 pad_maximum_fusion
  24.8 1.9 %all-to-all-done = bf16[32,2,4096]{2,1,0:T(2,128)(2,1)S(1)} async-done(((bf16[32,2,4096]{2,1,0:T(2,128)(2,1)}), bf16[32,2,4096]{2,1,0:T(2,128)(2,1)S(1)}, u32[]{:S(2)}, u32[]{:S(2)}) %all-to-all-start) | async-done | bytes 524320 | tf_op jit(solution)/shard_map/all_to_all | solution.py:31
  26.7 0.2 reshape.42
  26.9 9.5 %fusion.7 = bf16[64,2048]{1,0:T(8,128)(2,1)} fusion(bf16[64,4096]{1,0:T(8,128)(2,1)S(1)} %reshape.42, bf16[1,4096,2048]{2,1,0:T(8,128)(2,1)} %param.8, f32[]{:T(128)} %bitcast.3), kind=kOutput, calls=%fused_computation.8 | convolution fusion | flops 1074003968 | bytes 17563652 | tf_op jit(solution)/shard_map/dot_general | solution.py:71
  36.4 4.0 %all-to-all-start.1 = ((bf16[8,8,2048]{2,1,0:T(8,128)(2,1)}), bf16[8,8,2048]{2,1,0:T(8,128)(2,1)S(1)}, u32[]{:S(2)}, u32[]{:S(2)}) async-start(bf16[8,8,2048]{2,1,0:T(8,128)(2,1)} %bitcast.8), calls=%async_computation.1 | async-start | bytes 524288 | tf_op jit(solution)/shard_map/all_to_all | solution.py:74
  40.4 0.5 convolution_convert_fusion.1
  41.0 0.3 copy.26
  41.3 2.1 %reshape.142 = bf16[8,2,8,32,64,1]{4,3,2,1,0,5:T(8,128)(2,1)} reshape(bf16[4,2,16,2048]{3,2,1,0:T(8,128)(2,1)S(1)} %copy.26) | data formatting | bytes 1048576 | tf_op jit(solution)/shard_map/reshape | solution.py:51
  43.3 2.5 %convolution_bitcast_fusion.1 = f32[8,2,8,32,64]{4,3,2,1,0:T(8,128)S(1)} fusion(bf16[8,64,8,64,1,1]{3,2,1,0,5,4:T(8,128)(2,1)S(1)} %bitcast.46, bf16[8,2,8,32,64,1]{4,3,2,1,0,5:T(8,128)(2,1)} %reshape.142), kind=kOutput, calls=%fused_computation.9 | convolution fusion | flops 268435456 | bytes 2097152 | tf_op jit(solution)/shard_map/pkqsd,bjqd->pkbsj/dot_general | solution.py:52
  45.8 0.7 %reshape.46 = f32[8,16,2048]{2,1,0:T(8,128)S(1)} reshape(f32[8,2,8,32,64]{4,3,2,1,0:T(8,128)S(1)} %convolution_bitcast_fusion.1) | data formatting | bytes 2097152 | tf_op jit(solution)/shard_map/reshape | solution.py:54
  46.5 2.5 %all-to-all-done.1 = bf16[8,8,2048]{2,1,0:T(8,128)(2,1)S(1)} async-done(((bf16[8,8,2048]{2,1,0:T(8,128)(2,1)}), bf16[8,8,2048]{2,1,0:T(8,128)(2,1)S(1)}, u32[]{:S(2)}, u32[]{:S(2)}) %all-to-all-start.1) | async-done | bytes 262176 | tf_op jit(solution)/shard_map/all_to_all | solution.py:74
  49.0 0.1 copy.30
  49.1 1.4 %collective-permute-start.3 = (bf16[8,8,2048]{2,0,1:T(8,128)(2,1)S(1)}, bf16[8,8,2048]{2,0,1:T(8,128)(2,1)S(1)}, u32[]{:S(2)}, u32[]{:S(2)}) collective-permute-start(bf16[8,8,2048]{2,0,1:T(8,128)(2,1)S(1)} %copy.30), channel_id=1, source_target_pairs={{0,2},{1,3},{2,0},{3,1},{4,6},{5,7},{6,4},{7,5},{8,10},{9,11},{10,... | collective-permute-start | bytes 786440 | tf_op jit(solution)/shard_map/ppermute | solution.py:83
  50.5 5.0 %collective-permute-done.3 = bf16[8,8,2048]{2,0,1:T(8,128)(2,1)S(1)} collective-permute-done((bf16[8,8,2048]{2,0,1:T(8,128)(2,1)S(1)}, bf16[8,8,2048]{2,0,1:T(8,128)(2,1)S(1)}, u32[]{:S(2)}, u32[]{:S(2)}) %collective-permute-start.3) | collective-permute-done | bytes 262176 | tf_op jit(solution)/shard_map/ppermute | solution.py:83
  55.6 0.1 reshape_squeeze.3
  55.7 0.2 select_reduce_fusion.3
  55.9 0.1 pad_add_fusion
  56.0 1.1 %collective-permute-done.5 = bf16[8,8,2048]{2,0,1:T(8,128)(2,1)S(1)} collective-permute-done((bf16[8,8,2048]{2,0,1:T(8,128)(2,1)S(1)}, bf16[8,8,2048]{2,0,1:T(8,128)(2,1)S(1)}, u32[]{:S(2)}, u32[]{:S(2)}) %collective-permute-start.5) | collective-permute-done | bytes 262176 | tf_op jit(solution)/shard_map/ppermute | solution.py:83
  57.1 1.2 %fusion.3 = bf16[8,16,2048]{2,1,0:T(8,128)(2,1)} fusion(f32[8,16,2048]{2,1,0:T(8,128)S(1)} %reshape.46, bf16[8,8,2048]{2,0,1:T(8,128)(2,1)S(1)} %collective-permute-done.5, bf16[8,8,2048]{2,0,1:T(8,128)(2,1)S(1)} %collective-permute-done.4, bf16[8,8,2048]{2,0,1:T(8,128)(2,1)S(1)} %collective-permute-done.3, bf16[8,8,2048]{2,0,1:T(8,128)(2,1)S(1)} %copy.30, ...), kind=kOutput, calls=%fused_computation.5 | convolution fusion | flops 21496320 | bytes 2621632 | tf_op jit(solution)/shard_map/rpo,rt->pto/dot_general | solution.py:90
  (15 shorter events, 0.1 us)
Async XLA Ops:
  0.8 10.3 %slice-start = ((bf16[2,64,4096]{2,1,0:T(8,128)(2,1)}), bf16[2,64,2048]{2,1,0:T(8,128)(2,1)S(1)}, s32[]{:S(2)}) async-start(bf16[2,64,4096]{2,1,0:T(8,128)(2,1)} %param.7), calls=%async_computation.2 | async-start | bytes 1048576 | tf_op jit(solution)/shard_map/slice | solution.py:34
  2.4 10.9 %copy-start.2 = (s32[32]{0:T(128)S(1)}, s32[32]{0:T(128)}, u32[]{:S(2)}) copy-start(s32[32]{0:T(128)} %param.11) | copy-start | bytes 388
  2.4 12.2 %copy-start = (bf16[512,512]{1,0:T(8,128)(2,1)S(1)}, bf16[512,512]{1,0:T(8,128)(2,1)}, u32[]{:S(2)}) copy-start(bf16[512,512]{1,0:T(8,128)(2,1)} %param.9) | copy-start | bytes 1572868
  3.7 23.0 %all-to-all-start = ((bf16[32,2,4096]{2,1,0:T(2,128)(2,1)}), bf16[32,2,4096]{2,1,0:T(2,128)(2,1)S(1)}, u32[]{:S(2)}, u32[]{:S(2)}) async-start(bf16[32,2,4096]{2,1,0:T(2,128)(2,1)} %copy.24), calls=%async_computation | async-start | bytes 1048576 | tf_op jit(solution)/shard_map/all_to_all | solution.py:31
  11.2 7.8 %collective-permute-start.2 = (bf16[2,16,2048]{2,1,0:T(8,128)(2,1)S(1)}, bf16[2,16,2048]{2,1,0:T(8,128)(2,1)S(1)}, u32[]{:S(2)}, u32[]{:S(2)}) collective-permute-start(bf16[2,16,2048]{2,1,0:T(8,128)(2,1)S(1)} %get-tuple-element.30), channel_id=1, source_target_pairs={{0,3},{1,0},{2,1},{3,2},{4,7},{5,4},{6,5},{7,6},{8,11},{9,8},{10,9... | collective-permute-start | bytes 393224 | tf_op jit(solution)/shard_map/ppermute | solution.py:40
  12.7 12.0 %collective-permute-start.1 = (bf16[2,16,2048]{2,1,0:T(8,128)(2,1)S(1)}, bf16[2,16,2048]{2,1,0:T(8,128)(2,1)S(1)}, u32[]{:S(2)}, u32[]{:S(2)}) collective-permute-start(bf16[2,16,2048]{2,1,0:T(8,128)(2,1)S(1)} %get-tuple-element.31), channel_id=1, source_target_pairs={{0,2},{1,3},{2,0},{3,1},{4,6},{5,7},{6,4},{7,5},{8,10},{9,11},{10,... | collective-permute-start | bytes 393224 | tf_op jit(solution)/shard_map/ppermute | solution.py:40
  13.1 11.6 %collective-permute-start = (bf16[2,16,2048]{2,1,0:T(8,128)(2,1)S(1)}, bf16[2,16,2048]{2,1,0:T(8,128)(2,1)S(1)}, u32[]{:S(2)}, u32[]{:S(2)}) collective-permute-start(bf16[2,16,2048]{2,1,0:T(8,128)(2,1)S(1)} %get-tuple-element.32), channel_id=1, source_target_pairs={{0,1},{1,2},{2,3},{3,0},{4,5},{5,6},{6,7},{7,4},{8,9},{9,10},{10,1... | collective-permute-start | bytes 393224 | tf_op jit(solution)/shard_map/ppermute | solution.py:40
  36.4 12.6 %all-to-all-start.1 = ((bf16[8,8,2048]{2,1,0:T(8,128)(2,1)}), bf16[8,8,2048]{2,1,0:T(8,128)(2,1)S(1)}, u32[]{:S(2)}, u32[]{:S(2)}) async-start(bf16[8,8,2048]{2,1,0:T(8,128)(2,1)} %bitcast.8), calls=%async_computation.1 | async-start | bytes 524288 | tf_op jit(solution)/shard_map/all_to_all | solution.py:74
  45.8 9.7 %copy-start.1 = (s32[32,2]{0,1:T(2,128)S(1)}, s32[32,2]{0,1:T(2,128)}, u32[]{:S(2)}) copy-start(s32[32,2]{0,1:T(2,128)} %param.10) | copy-start | bytes 772
  49.1 6.4 %collective-permute-start.3 = (bf16[8,8,2048]{2,0,1:T(8,128)(2,1)S(1)}, bf16[8,8,2048]{2,0,1:T(8,128)(2,1)S(1)}, u32[]{:S(2)}, u32[]{:S(2)}) collective-permute-start(bf16[8,8,2048]{2,0,1:T(8,128)(2,1)S(1)} %copy.30), channel_id=1, source_target_pairs={{0,2},{1,3},{2,0},{3,1},{4,6},{5,7},{6,4},{7,5},{8,10},{9,11},{10,... | collective-permute-start | bytes 786440 | tf_op jit(solution)/shard_map/ppermute | solution.py:83
  50.5 5.5 %collective-permute-start.4 = (bf16[8,8,2048]{2,0,1:T(8,128)(2,1)S(1)}, bf16[8,8,2048]{2,0,1:T(8,128)(2,1)S(1)}, u32[]{:S(2)}, u32[]{:S(2)}) collective-permute-start(bf16[8,8,2048]{2,0,1:T(8,128)(2,1)S(1)} %copy.30), channel_id=1, source_target_pairs={{0,1},{1,0},{2,3},{3,2},{4,5},{5,4},{6,7},{7,6},{8,9},{9,8},{10,11... | collective-permute-start | bytes 786440 | tf_op jit(solution)/shard_map/ppermute | solution.py:83
  55.5 1.5 %collective-permute-start.5 = (bf16[8,8,2048]{2,0,1:T(8,128)(2,1)S(1)}, bf16[8,8,2048]{2,0,1:T(8,128)(2,1)S(1)}, u32[]{:S(2)}, u32[]{:S(2)}) collective-permute-start(bf16[8,8,2048]{2,0,1:T(8,128)(2,1)S(1)} %collective-permute-done.3), channel_id=1, source_target_pairs={{0,1},{1,0},{2,3},{3,2},{4,5},{5,4},{6,7},{7,6},{8,9},{9,8},{10,11... | collective-permute-start | bytes 786440 | tf_op jit(solution)/shard_map/ppermute | solution.py:83

commit v14 on v9

--- a/solution.py
+++ b/solution.py
@@ -81,14 +81,20 @@
             got = [lax.ppermute(x, "virt", perm) for x in blocks]
             blocks = blocks + got
             srcs = srcs + [s ^ bit for s in srcs]
-        allb = jnp.concatenate(blocks, axis=0)
-        src_tiles = jnp.concatenate([jnp.take(tout, s, axis=1) for s in srcs])
-        one_hot = (src_tiles[:, None] == my_tiles[None, :]).astype(jnp.bfloat16)
-        pieces.append(
-            jnp.einsum("rpo,rt->pto", allb, one_hot, preferred_element_type=jnp.float32)
+        early = jnp.concatenate(blocks[:-1], axis=0)
+        early_tiles = jnp.concatenate([jnp.take(tout, s, axis=1) for s in srcs[:-1]])
+        one_hot = (early_tiles[:, None] == my_tiles[None, :]).astype(jnp.bfloat16)
+        acc = onebody + jnp.einsum(
+            "rpo,rt->pto", early, one_hot, preferred_element_type=jnp.float32
         )
-    ladder = jnp.concatenate(pieces, axis=2) if N_CHUNK > 1 else pieces[0]
-    return (ladder + onebody).astype(jnp.bfloat16)
+        acc = lax.optimization_barrier(acc)
+        late_hit = jnp.take(tout, srcs[-1], axis=1)[:, None] == my_tiles[None, :]
+        late = blocks[-1].astype(jnp.float32)
+        for r in range(late.shape[0]):
+            acc = acc + jnp.where(late_hit[r][None, :, None], late[r][:, None, :], 0.0)
+        pieces.append(acc)
+    total = jnp.concatenate(pieces, axis=2) if N_CHUNK > 1 else pieces[0]
+    return total.astype(jnp.bfloat16)
 
 
 def solution(mesh):

time: 58.7 us -> 62 us (1.056)
  local copies, waits for them, and re-layouts: 6.76 us -> 8.35 us
  other arithmetic: 0.39 us -> 1.96 us
    ppermute x3, waiting for transfers between devices: 6.15 us -> 8.37 us  [per_device(): got = [lax.ppermute(x, 'virt', perm) for x in blocks]]
    convert_element_type x0 -> x1, other arithmetic: none -> 1.5 us  [per_device(): return total.astype(jnp.bfloat16)]
    ppermute x3, waiting for transfers between devices: 9.62 us -> 8.2 us  [per_device(): got.append(lax.ppermute(part, 'virt', perm))]
    reshape x1, local copies, waits for them, and re-layouts: 0.53 us -> 1.51 us  [per_device(): fock_four = fock_vv.reshape(NVT, TILE, NVT, TILE)]
    dot_general x1, matrix products: 1.15 us -> 0.35 us  [per_device(): jnp.einsum('rpo,rt->pto', early, one_hot, preferred_element_type=jnp.floa...]
  transfers between devices with their start and end apart: 8 -> 8, of which waited for: 6 -> 6; matrix products, arithmetic and copies ran while one was open for 13% -> 15% of each run, Pallas kernels for 0% -> 0%
where the time goes in v14:
time: 62 us; the launch traced here: 61.6 us
  waiting for transfers between devices  20.6 us (33%)
  starting transfers between devices  14.9 us (24%)
  matrix products  14.8 us (24%)
  local copies, waits for them, and re-layouts  8.35 us (13%)
  other arithmetic  1.96 us (3%)
  between operations  0.9 us (1%)
    dot_general x1, matrix products, per_device(): product = jnp.dot(chosen, cols, preferred_element_type=jnp.float32)  9.5 us
    ppermute x3, waiting for transfers between devices, per_device(): got = [lax.ppermute(x, 'virt', perm) for x in blocks]  8.37 us
    ppermute x3, waiting for transfers between devices, per_device(): got.append(lax.ppermute(part, 'virt', perm))  8.2 us
    all_to_all x1, starting transfers between devices, per_device(): chosen = lax.all_to_all(picked, ('pair', 'virt'), 0, 0, tiled=True)  7.33 us
    all_to_all x1, starting transfers between devices, per_device(): lax.all_to_all(product.reshape(n_pair, p_grp, width), 'pair', 0, 0, tiled...  4.03 us
    dot_general x1, matrix products, one_body(): jnp.einsum('pkqsd,bjqd->pkbsj', sub, fock_four, preferred_element_type=jn...  2.81 us
    all_to_all x1, waiting for transfers between devices, per_device(): lax.all_to_all(product.reshape(n_pair, p_grp, width), 'pair', 0, 0, tiled...  2.13 us
    reshape x1, local copies, waits for them, and re-layouts, one_body(): sub = sub.reshape(p_grp, slab // NVT, NVT, AS, TILE)  2.09 us
  transfers between devices with their start and end apart: 8, of which 6 were waited for; matrix products, arithmetic and copies ran while one was open for 15% of the time, Pallas kernels for 0%

profile of v14, /device:TPU:0, one launch (start us, length us, event | category | flops | bytes accessed | tf_op | source)
XLA Modules:
  0.0 61.6 jit_solution(394815985485012086)
XLA Ops:
  0.0 0.8 %slice_reduce_fusion = (s32[32]{0:T(128)S(1)}, s32[32]{0:T(128)S(1)}) fusion(s32[32,2]{0,1:T(2,128)} %param.10), kind=kLoop, calls=%fused_computation.60 | loop fusion | bytes 512 | tf_op jit(solution)/shard_map/slice | solution.py:57
  0.8 1.6 %convolution_convert_fusion = bf16[32,2,4096]{2,0,1:T(8,128)(2,1)S(1)} fusion(bf16[2,64,4096]{2,1,0:T(8,128)(2,1)} %param.7, s32[32]{0:T(128)S(1)} %get-tuple-element.50), kind=kOutput, calls=%fused_computation.2 | convolution fusion | flops 33818624 | bytes 1572992 | tf_op jit(solution)/shard_map/dt,itc->dic/dot_general | solution.py:26
  2.4 1.3 %copy.14 = bf16[32,2,4096]{2,1,0:T(2,128)(2,1)} copy(bf16[32,2,4096]{2,0,1:T(8,128)(2,1)S(1)} %convolution_convert_fusion) | data formatting | bytes 1048576 | tf_op jit(solution)/shard_map/convert_element_type | solution.py:28
  3.8 7.3 %all-to-all-start = ((bf16[32,2,4096]{2,1,0:T(2,128)(2,1)}), bf16[32,2,4096]{2,1,0:T(2,128)(2,1)S(1)}, u32[]{:S(2)}, u32[]{:S(2)}) async-start(bf16[32,2,4096]{2,1,0:T(2,128)(2,1)} %copy.14), calls=%async_computation | async-start | bytes 1048576 | tf_op jit(solution)/shard_map/all_to_all | solution.py:29
  11.2 1.5 %collective-permute-start.2 = (bf16[2,16,2048]{2,1,0:T(8,128)(2,1)S(1)}, bf16[2,16,2048]{2,1,0:T(8,128)(2,1)S(1)}, u32[]{:S(2)}, u32[]{:S(2)}) collective-permute-start(bf16[2,16,2048]{2,1,0:T(8,128)(2,1)S(1)} %get-tuple-element.30), channel_id=1, source_target_pairs={{0,3},{1,0},{2,1},{3,2},{4,7},{5,4},{6,5},{7,6},{8,11},{9,8},{10,9... | collective-permute-start | bytes 393224 | tf_op jit(solution)/shard_map/ppermute | solution.py:38
  12.8 0.4 collective-permute-start.1
  13.2 0.1 collective-permute-start
  13.3 0.1 reshape_squeeze.3
  13.4 0.2 select_reduce_fusion
  13.6 0.1 broadcast_compare_fusion
  13.7 0.7 %dynamic_slice.16 = s32[1]{0:T(128)} dynamic-slice(s32[32]{0:T(128)S(1)} %copy-done.1, s32[]{:T(128)S(6)} %select_n.72), dynamic_slice_sizes={1} | dynamic-slice | bytes 12 | tf_op jit(solution)/shard_map/jit(dynamic_index_in_dim)/dynamic_slice | solution.py:54
  15.0 1.5 %reshape.57 = bf16[8,64,8,64]{3,2,1,0:T(8,128)(2,1)} reshape(bf16[512,512]{1,0:T(8,128)(2,1)S(1)} %copy-done) | data formatting | bytes 1048576 | tf_op jit(solution)/shard_map/reshape | solution.py:42
  16.5 2.5 %collective-permute-done.2 = bf16[2,16,2048]{2,1,0:T(8,128)(2,1)S(1)} collective-permute-done((bf16[2,16,2048]{2,1,0:T(8,128)(2,1)S(1)}, bf16[2,16,2048]{2,1,0:T(8,128)(2,1)S(1)}, u32[]{:S(2)}, u32[]{:S(2)}) %collective-permute-start.2) | collective-permute-done | bytes 131104 | tf_op jit(solution)/shard_map/ppermute | solution.py:38
  19.1 5.7 %collective-permute-done.1 = bf16[2,16,2048]{2,1,0:T(8,128)(2,1)S(1)} collective-permute-done((bf16[2,16,2048]{2,1,0:T(8,128)(2,1)S(1)}, bf16[2,16,2048]{2,1,0:T(8,128)(2,1)S(1)}, u32[]{:S(2)}, u32[]{:S(2)}) %collective-permute-start.1) | collective-permute-done | bytes 131104 | tf_op jit(solution)/shard_map/ppermute | solution.py:38
  24.8 1.9 %all-to-all-done = bf16[32,2,4096]{2,1,0:T(2,128)(2,1)S(1)} async-done(((bf16[32,2,4096]{2,1,0:T(2,128)(2,1)}), bf16[32,2,4096]{2,1,0:T(2,128)(2,1)S(1)}, u32[]{:S(2)}, u32[]{:S(2)}) %all-to-all-start) | async-done | bytes 524320 | tf_op jit(solution)/shard_map/all_to_all | solution.py:29
  26.7 0.2 reshape.54
  26.9 9.5 %fusion.6 = bf16[64,2048]{1,0:T(8,128)(2,1)} fusion(bf16[64,4096]{1,0:T(8,128)(2,1)S(1)} %reshape.54, bf16[1,4096,2048]{2,1,0:T(8,128)(2,1)} %param.8, f32[]{:T(128)} %bitcast.3), kind=kOutput, calls=%fused_computation.7 | convolution fusion | flops 1074003968 | bytes 17563652 | tf_op jit(solution)/shard_map/dot_general | solution.py:69
  36.4 4.0 %all-to-all-start.1 = ((bf16[8,8,2048]{2,1,0:T(8,128)(2,1)}), bf16[8,8,2048]{2,1,0:T(8,128)(2,1)S(1)}, u32[]{:S(2)}, u32[]{:S(2)}) async-start(bf16[8,8,2048]{2,1,0:T(8,128)(2,1)} %bitcast.8), calls=%async_computation.1 | async-start | bytes 524288 | tf_op jit(solution)/shard_map/all_to_all | solution.py:72
  40.5 0.5 convolution_convert_fusion.1
  41.0 0.3 copy.16
  41.3 2.1 %reshape.154 = bf16[8,2,8,32,64,1]{4,3,2,1,0,5:T(8,128)(2,1)} reshape(bf16[4,2,16,2048]{3,2,1,0:T(8,128)(2,1)S(1)} %copy.16) | data formatting | bytes 1048576 | tf_op jit(solution)/shard_map/reshape | solution.py:49
  43.4 2.8 %convolution_bitcast_fusion.1 = f32[8,2,8,32,64]{4,3,2,1,0:T(8,128)S(1)} fusion(bf16[8,64,8,64,1,1]{3,2,1,0,5,4:T(8,128)(2,1)} %bitcast.78, bf16[8,2,8,32,64,1]{4,3,2,1,0,5:T(8,128)(2,1)} %reshape.154), kind=kOutput, calls=%fused_computation.8 | convolution fusion | flops 268435456 | bytes 2097152 | tf_op jit(solution)/shard_map/pkqsd,bjqd->pkbsj/dot_general | solution.py:50
  46.2 0.7 %reshape.58 = f32[8,16,2048]{2,1,0:T(8,128)S(1)} reshape(f32[8,2,8,32,64]{4,3,2,1,0:T(8,128)S(1)} %convolution_bitcast_fusion.1) | data formatting | bytes 2097152 | tf_op jit(solution)/shard_map/reshape | solution.py:52
  46.9 2.1 %all-to-all-done.1 = bf16[8,8,2048]{2,1,0:T(8,128)(2,1)S(1)} async-done(((bf16[8,8,2048]{2,1,0:T(8,128)(2,1)}), bf16[8,8,2048]{2,1,0:T(8,128)(2,1)S(1)}, u32[]{:S(2)}, u32[]{:S(2)}) %all-to-all-start.1) | async-done | bytes 262176 | tf_op jit(solution)/shard_map/all_to_all | solution.py:72
  49.0 0.1 copy.20
  49.2 1.4 %collective-permute-start.3 = (bf16[8,8,2048]{2,0,1:T(8,128)(2,1)S(1)}, bf16[8,8,2048]{2,0,1:T(8,128)(2,1)S(1)}, u32[]{:S(2)}, u32[]{:S(2)}) collective-permute-start(bf16[8,8,2048]{2,0,1:T(8,128)(2,1)S(1)} %copy.20), channel_id=1, source_target_pairs={{0,2},{1,3},{2,0},{3,1},{4,6},{5,7},{6,4},{7,5},{8,10},{9,11},{10,... | collective-permute-start | bytes 786440 | tf_op jit(solution)/shard_map/ppermute | solution.py:81
  50.7 0.1 pad_add_fusion
  50.8 7.2 %collective-permute-done.3 = bf16[8,8,2048]{2,0,1:T(8,128)(2,1)S(1)} collective-permute-done((bf16[8,8,2048]{2,0,1:T(8,128)(2,1)S(1)}, bf16[8,8,2048]{2,0,1:T(8,128)(2,1)S(1)}, u32[]{:S(2)}, u32[]{:S(2)}) %collective-permute-start.3) | collective-permute-done | bytes 262176 | tf_op jit(solution)/shard_map/ppermute | solution.py:81
  58.0 0.4 fusion.2
  58.3 1.2 %collective-permute-done.5 = bf16[8,8,2048]{2,0,1:T(8,128)(2,1)S(1)} collective-permute-done((bf16[8,8,2048]{2,0,1:T(8,128)(2,1)S(1)}, bf16[8,8,2048]{2,0,1:T(8,128)(2,1)S(1)}, u32[]{:S(2)}, u32[]{:S(2)}) %collective-permute-start.5) | collective-permute-done | bytes 262176 | tf_op jit(solution)/shard_map/ppermute | solution.py:81
  59.5 0.4 fusion.29
  60.1 1.5 %add_convert_fusion = bf16[8,16,2048]{2,1,0:T(8,128)(2,1)} fusion(f32[8,16,2048]{2,1,0:T(8,128)S(1)} %fusion.2, f32[8,2048]{1,0:T(8,128)S(1)} %get-tuple-element.51, f32[8,2048]{1,0:T(8,128)S(1)} %get-tuple-element.52, f32[8,2048]{1,0:T(8,128)S(1)} %get-tuple-element.53, f32[8,2048]{1,0:T(8,128)S(1)} %get-tuple-element.54, ...), kind=kLoop, calls=%fused_computation.11 | loop fusion | flops 4456448 | bytes 2097280 | tf_op jit(solution)/shard_map/convert_element_type | solution.py:97
  (19 shorter events, 0.4 us)
Async XLA Ops:
  0.8 10.4 %slice-start = ((bf16[2,64,4096]{2,1,0:T(8,128)(2,1)}), bf16[2,64,2048]{2,1,0:T(8,128)(2,1)S(1)}, s32[]{:S(2)}) async-start(bf16[2,64,4096]{2,1,0:T(8,128)(2,1)} %param.7), calls=%async_computation.2 | async-start | bytes 1048576 | tf_op jit(solution)/shard_map/slice | solution.py:32
  2.4 11.3 %copy-start.1 = (s32[32]{0:T(128)S(1)}, s32[32]{0:T(128)}, u32[]{:S(2)}) copy-start(s32[32]{0:T(128)} %param.11) | copy-start | bytes 388
  2.4 12.6 %copy-start = (bf16[512,512]{1,0:T(8,128)(2,1)S(1)}, bf16[512,512]{1,0:T(8,128)(2,1)}, u32[]{:S(2)}) copy-start(bf16[512,512]{1,0:T(8,128)(2,1)} %param.9) | copy-start | bytes 1572868
  3.8 22.9 %all-to-all-start = ((bf16[32,2,4096]{2,1,0:T(2,128)(2,1)}), bf16[32,2,4096]{2,1,0:T(2,128)(2,1)S(1)}, u32[]{:S(2)}, u32[]{:S(2)}) async-start(bf16[32,2,4096]{2,1,0:T(2,128)(2,1)} %copy.14), calls=%async_computation | async-start | bytes 1048576 | tf_op jit(solution)/shard_map/all_to_all | solution.py:29
  11.2 7.8 %collective-permute-start.2 = (bf16[2,16,2048]{2,1,0:T(8,128)(2,1)S(1)}, bf16[2,16,2048]{2,1,0:T(8,128)(2,1)S(1)}, u32[]{:S(2)}, u32[]{:S(2)}) collective-permute-start(bf16[2,16,2048]{2,1,0:T(8,128)(2,1)S(1)} %get-tuple-element.30), channel_id=1, source_target_pairs={{0,3},{1,0},{2,1},{3,2},{4,7},{5,4},{6,5},{7,6},{8,11},{9,8},{10,9... | collective-permute-start | bytes 393224 | tf_op jit(solution)/shard_map/ppermute | solution.py:38
  12.8 12.0 %collective-permute-start.1 = (bf16[2,16,2048]{2,1,0:T(8,128)(2,1)S(1)}, bf16[2,16,2048]{2,1,0:T(8,128)(2,1)S(1)}, u32[]{:S(2)}, u32[]{:S(2)}) collective-permute-start(bf16[2,16,2048]{2,1,0:T(8,128)(2,1)S(1)} %get-tuple-element.31), channel_id=1, source_target_pairs={{0,2},{1,3},{2,0},{3,1},{4,6},{5,7},{6,4},{7,5},{8,10},{9,11},{10,... | collective-permute-start | bytes 393224 | tf_op jit(solution)/shard_map/ppermute | solution.py:38
  13.2 11.6 %collective-permute-start = (bf16[2,16,2048]{2,1,0:T(8,128)(2,1)S(1)}, bf16[2,16,2048]{2,1,0:T(8,128)(2,1)S(1)}, u32[]{:S(2)}, u32[]{:S(2)}) collective-permute-start(bf16[2,16,2048]{2,1,0:T(8,128)(2,1)S(1)} %get-tuple-element.32), channel_id=1, source_target_pairs={{0,1},{1,2},{2,3},{3,0},{4,5},{5,6},{6,7},{7,4},{8,9},{9,10},{10,1... | collective-permute-start | bytes 393224 | tf_op jit(solution)/shard_map/ppermute | solution.py:38
  36.4 12.6 %all-to-all-start.1 = ((bf16[8,8,2048]{2,1,0:T(8,128)(2,1)}), bf16[8,8,2048]{2,1,0:T(8,128)(2,1)S(1)}, u32[]{:S(2)}, u32[]{:S(2)}) async-start(bf16[8,8,2048]{2,1,0:T(8,128)(2,1)} %bitcast.8), calls=%async_computation.1 | async-start | bytes 524288 | tf_op jit(solution)/shard_map/all_to_all | solution.py:72
  49.2 8.8 %collective-permute-start.4 = (bf16[8,8,2048]{2,0,1:T(8,128)(2,1)S(1)}, bf16[8,8,2048]{2,0,1:T(8,128)(2,1)S(1)}, u32[]{:S(2)}, u32[]{:S(2)}) collective-permute-start(bf16[8,8,2048]{2,0,1:T(8,128)(2,1)S(1)} %copy.20), channel_id=1, source_target_pairs={{0,1},{1,0},{2,3},{3,2},{4,5},{5,4},{6,7},{7,6},{8,9},{9,8},{10,11... | collective-permute-start | bytes 786440 | tf_op jit(solution)/shard_map/ppermute | solution.py:81
  49.2 8.7 %collective-permute-start.3 = (bf16[8,8,2048]{2,0,1:T(8,128)(2,1)S(1)}, bf16[8,8,2048]{2,0,1:T(8,128)(2,1)S(1)}, u32[]{:S(2)}, u32[]{:S(2)}) collective-permute-start(bf16[8,8,2048]{2,0,1:T(8,128)(2,1)S(1)} %copy.20), channel_id=1, source_target_pairs={{0,2},{1,3},{2,0},{3,1},{4,6},{5,7},{6,4},{7,5},{8,10},{9,11},{10,... | collective-permute-start | bytes 786440 | tf_op jit(solution)/shard_map/ppermute | solution.py:81
  58.0 1.5 %collective-permute-start.5 = (bf16[8,8,2048]{2,0,1:T(8,128)(2,1)S(1)}, bf16[8,8,2048]{2,0,1:T(8,128)(2,1)S(1)}, u32[]{:S(2)}, u32[]{:S(2)}) collective-permute-start(bf16[8,8,2048]{2,0,1:T(8,128)(2,1)S(1)} %collective-permute-done.3), channel_id=1, source_target_pairs={{0,1},{1,0},{2,3},{3,2},{4,5},{5,4},{6,7},{7,6},{8,9},{9,8},{10,11... | collective-permute-start | bytes 786440 | tf_op jit(solution)/shard_map/ppermute | solution.py:81

commit v15 on v9

--- a/solution.py
+++ b/solution.py
@@ -26,8 +26,13 @@
     picked = jnp.einsum(
         "dt,itc->dic", pick, amps_pm, preferred_element_type=jnp.float32
     ).astype(amps_pm.dtype)
-    chosen = lax.all_to_all(picked, ("pair", "virt"), 0, 0, tiled=True)
-    chosen = chosen.reshape(n_dev * pm_rows, tile_len)
+    half = tile_len // 2
+    chosen = [
+        lax.all_to_all(
+            picked[:, :, h * half:(h + 1) * half], ("pair", "virt"), 0, 0, tiled=True
+        ).reshape(n_dev * pm_rows, half)
+        for h in range(2)
+    ]
 
     got = [lax.dynamic_slice_in_dim(amps_pm[:, :, :out_cols], virt_idx * slab, slab, 1)]
     for k in range(1, n_virt):
@@ -66,7 +71,10 @@
     pieces = []
     for c in range(N_CHUNK):
         cols = integrals[0, :, c * width:(c + 1) * width]
-        product = jnp.dot(chosen, cols, preferred_element_type=jnp.float32)
+        product = jnp.dot(chosen[0], cols[:half], preferred_element_type=jnp.float32)
+        product = product + jnp.dot(
+            chosen[1], cols[half:], preferred_element_type=jnp.float32
+        )
         product = (product * own_mask).astype(jnp.bfloat16)
         product, stacked = lax.optimization_barrier((product, stacked))
         held = lax.all_to_all(

time: 58.7 us -> 66.4 us (1.13)
  starting transfers between devices: 14.8 us -> 18.4 us
  local copies, waits for them, and re-layouts: 6.76 us -> 10.2 us
  matrix products: 15.3 us -> 16.4 us
    ppermute x3, waiting for transfers between devices: 9.62 us -> 4.06 us  [per_device(): got.append(lax.ppermute(part, 'virt', perm))]
    all_to_all x1 -> x2, starting transfers between devices: 7.33 us -> 12 us  [per_device(): lax.all_to_all(picked[:, :, h * half:(h + 1) * half], ('pair', 'virt'), 0...]
    all_to_all x1 -> x2, waiting for transfers between devices: 1.91 us -> 5.51 us  [per_device(): lax.all_to_all(picked[:, :, h * half:(h + 1) * half], ('pair', 'virt'), 0...]
    slice x0 -> x3, local copies, waits for them, and re-layouts: none -> 1.97 us  [per_device(): picked[:, :, h * half:(h + 1) * half]]
    convert_element_type x1 -> x0, local copies, waits for them, and re-layouts: 1.34 us -> none  [per_device(): picked = jnp.einsum('dt,itc->dic', pick, amps_pm, preferred_element_type=...]
    dot_general x1 -> x2, matrix products: 9.5 us -> 10.6 us  [the longest x1 5.68 us: per_device(): jnp.dot(chosen[0], cols[:half], preferred_element_type=jnp.float32)]
    reshape x1, local copies, waits for them, and re-layouts: 0.53 us -> 1.64 us  [per_device(): fock_four = fock_vv.reshape(NVT, TILE, NVT, TILE)]
    slice x2 -> x1, local copies, waits for them, and re-layouts: 0.01 us -> 1.08 us  [per_device(): amps_pm[:, :, :out_cols]]
  transfers between devices with their start and end apart: 8 -> 9, of which waited for: 6 -> 5; matrix products, arithmetic and copies ran while one was open for 13% -> 25% of each run, Pallas kernels for 0% -> 0%
where the time goes in v15:
time: 66.4 us; the launch traced here: 65.8 us
  waiting for transfers between devices  19.6 us (30%)
  starting transfers between devices  18.4 us (28%)
  matrix products  16.4 us (25%)
  local copies, waits for them, and re-layouts  10.2 us (15%)
  between operations  0.85 us (1%)
    all_to_all x2, starting transfers between devices, per_device(): lax.all_to_all(picked[:, :, h * half:(h + 1) * half], ('pair', 'virt'), 0...  12 us
    ppermute x3, waiting for transfers between devices, per_device(): got = [lax.ppermute(x, 'virt', perm) for x in blocks]  6.85 us
    dot_general x1, matrix products, per_device(): jnp.dot(chosen[0], cols[:half], preferred_element_type=jnp.float32)  5.68 us
    all_to_all x2, waiting for transfers between devices, per_device(): lax.all_to_all(picked[:, :, h * half:(h + 1) * half], ('pair', 'virt'), 0...  5.51 us
    dot_general x1, matrix products, per_device(): jnp.dot(chosen[1], cols[half:], preferred_element_type=jnp.float32)  4.95 us
    ppermute x3, waiting for transfers between devices, per_device(): got.append(lax.ppermute(part, 'virt', perm))  4.06 us
    all_to_all x1, starting transfers between devices, per_device(): lax.all_to_all(product.reshape(n_pair, p_grp, width), 'pair', 0, 0, tiled...  3.41 us
    all_to_all x1, waiting for transfers between devices, per_device(): lax.all_to_all(product.reshape(n_pair, p_grp, width), 'pair', 0, 0, tiled...  3.16 us
  transfers between devices with their start and end apart: 9, of which 5 were waited for; matrix products, arithmetic and copies ran while one was open for 25% of the time, Pallas kernels for 0%

profile of v15, /device:TPU:0, one launch (start us, length us, event | category | flops | bytes accessed | tf_op | source)
XLA Modules:
  0.0 65.8 jit_solution(5246099680196311607)
XLA Ops:
  0.0 0.8 %slice_reduce_fusion = (s32[32]{0:T(128)S(1)}, s32[32]{0:T(128)S(1)}) fusion(s32[32,2]{0,1:T(2,128)} %param.10), kind=kLoop, calls=%fused_computation.51 | loop fusion | bytes 512 | tf_op jit(solution)/shard_map/slice | solution.py:62
  0.8 1.6 %convolution_convert_fusion = bf16[32,2,4096]{2,0,1:T(8,128)(2,1)S(1)} fusion(bf16[2,64,4096]{2,1,0:T(8,128)(2,1)} %param.7, s32[32]{0:T(128)S(1)} %get-tuple-element.36), kind=kOutput, calls=%fused_computation.6 | convolution fusion | flops 33818624 | bytes 1572992 | tf_op jit(solution)/shard_map/dt,itc->dic/dot_general | solution.py:26
  2.4 1.0 %copy.16 = bf16[32,2,2048]{2,1,0:T(2,128)(2,1)} copy(bf16[32,2,2048]{2,0,1:T(8,128)(2,1)S(1)} %get-tuple-element.34) | data formatting | bytes 524288 | tf_op jit(solution)/shard_map/slice | solution.py:32
  3.4 7.3 %all-to-all-start.1 = ((bf16[32,2,2048]{2,1,0:T(2,128)(2,1)}), bf16[32,2,2048]{2,1,0:T(2,128)(2,1)S(1)}, u32[]{:S(2)}, u32[]{:S(2)}) async-start(bf16[32,2,2048]{2,1,0:T(2,128)(2,1)} %copy.16), calls=%async_computation.1 | async-start | bytes 524288 | tf_op jit(solution)/shard_map/all_to_all | solution.py:31
  10.8 1.1 %slice.38 = bf16[2,64,2048]{2,1,0:T(8,128)(2,1)S(1)} slice(bf16[2,64,4096]{2,1,0:T(8,128)(2,1)} %param.7), slice={[0:2], [0:64], [0:2048]} | slice | bytes 1048576 | tf_op jit(solution)/shard_map/slice | solution.py:37
  11.9 1.5 %collective-permute-start.2 = (bf16[2,16,2048]{2,1,0:T(8,128)(2,1)S(1)}, bf16[2,16,2048]{2,1,0:T(8,128)(2,1)S(1)}, u32[]{:S(2)}, u32[]{:S(2)}) collective-permute-start(bf16[2,16,2048]{2,1,0:T(8,128)(2,1)S(1)} %get-tuple-element.30), channel_id=1, source_target_pairs={{0,3},{1,0},{2,1},{3,2},{4,7},{5,4},{6,5},{7,6},{8,11},{9,8},{10,9... | collective-permute-start | bytes 393224 | tf_op jit(solution)/shard_map/ppermute | solution.py:43
  13.5 0.4 collective-permute-start.1
  13.8 0.1 collective-permute-start
  14.0 1.3 %dynamic_slice.16 = s32[1]{0:T(128)} dynamic-slice(s32[32]{0:T(128)} %param.11, s32[]{:T(128)S(6)} %select_n.47), dynamic_slice_sizes={1} | dynamic-slice | bytes 12 | tf_op jit(solution)/shard_map/jit(dynamic_index_in_dim)/dynamic_slice | solution.py:59
  15.9 1.0 %copy.15 = bf16[32,2,2048]{2,1,0:T(2,128)(2,1)} copy(bf16[32,2,2048]{2,0,1:T(8,128)(2,1)S(1)} %get-tuple-element.33) | data formatting | bytes 524288 | tf_op jit(solution)/shard_map/slice | solution.py:32
  16.8 1.6 %reshape.46 = bf16[8,64,8,64]{3,2,1,0:T(8,128)(2,1)S(1)} reshape(bf16[512,512]{1,0:T(8,128)(2,1)} %param.9) | data formatting | bytes 1048576 | tf_op jit(solution)/shard_map/reshape | solution.py:47
  18.5 4.1 %collective-permute-done.1 = bf16[2,16,2048]{2,1,0:T(8,128)(2,1)S(1)} collective-permute-done((bf16[2,16,2048]{2,1,0:T(8,128)(2,1)S(1)}, bf16[2,16,2048]{2,1,0:T(8,128)(2,1)S(1)}, u32[]{:S(2)}, u32[]{:S(2)}) %collective-permute-start.1) | collective-permute-done | bytes 131104 | tf_op jit(solution)/shard_map/ppermute | solution.py:43
  22.6 4.6 %all-to-all-start = ((bf16[32,2,2048]{2,1,0:T(2,128)(2,1)}), bf16[32,2,2048]{2,1,0:T(2,128)(2,1)S(1)}, u32[]{:S(2)}, u32[]{:S(2)}) async-start(bf16[32,2,2048]{2,1,0:T(2,128)(2,1)} %copy.15), calls=%async_computation | async-start | bytes 524288 | tf_op jit(solution)/shard_map/all_to_all | solution.py:31
  27.3 0.1 reshape.43
  27.4 4.9 %fusion = f32[64,2048]{1,0:T(8,128)S(1)} fusion(bf16[64,2048]{1,0:T(8,128)(2,1)S(1)} %reshape.43, bf16[1,4096,2048]{2,1,0:T(8,128)(2,1)} %param.8), kind=kOutput, calls=%fused_computation | convolution fusion | flops 536870912 | bytes 9175040 | tf_op jit(solution)/shard_map/dot_general | solution.py:75
  32.3 5.5 %all-to-all-done = bf16[32,2,2048]{2,1,0:T(2,128)(2,1)S(1)} async-done(((bf16[32,2,2048]{2,1,0:T(2,128)(2,1)}), bf16[32,2,2048]{2,1,0:T(2,128)(2,1)S(1)}, u32[]{:S(2)}, u32[]{:S(2)}) %all-to-all-start) | async-done | bytes 262176 | tf_op jit(solution)/shard_map/all_to_all | solution.py:31
  37.9 0.1 reshape.42
  38.0 5.7 %fusion.14 = bf16[64,2048]{1,0:T(8,128)(2,1)} fusion(f32[64,2048]{1,0:T(8,128)S(1)} %fusion, bf16[64,2048]{1,0:T(8,128)(2,1)S(1)} %reshape.42, bf16[1,4096,2048]{2,1,0:T(8,128)(2,1)} %param.8, f32[]{:T(128)} %bitcast.5), kind=kOutput, calls=%fused_computation.13 | convolution fusion | flops 537264128 | bytes 9437696 | tf_op jit(solution)/shard_map/dot_general | solution.py:74
  43.6 3.4 %all-to-all-start.2 = ((bf16[8,8,2048]{2,1,0:T(8,128)(2,1)}), bf16[8,8,2048]{2,1,0:T(8,128)(2,1)S(1)}, u32[]{:S(2)}, u32[]{:S(2)}) async-start(bf16[8,8,2048]{2,1,0:T(8,128)(2,1)} %bitcast.10), calls=%async_computation.2 | async-start | bytes 524288 | tf_op jit(solution)/shard_map/all_to_all | solution.py:80
  47.1 0.5 convolution_convert_fusion.1
  47.6 0.3 copy.18
  47.9 2.0 %reshape.143 = bf16[8,2,8,32,64,1]{4,3,2,1,0,5:T(8,128)(2,1)} reshape(bf16[4,2,16,2048]{3,2,1,0:T(8,128)(2,1)S(1)} %copy.18) | data formatting | bytes 1048576 | tf_op jit(solution)/shard_map/reshape | solution.py:54
  50.0 2.5 %convolution_bitcast_fusion.1 = f32[8,2,8,32,64]{4,3,2,1,0:T(8,128)S(1)} fusion(bf16[8,64,8,64,1,1]{3,2,1,0,5,4:T(8,128)(2,1)S(1)} %bitcast.54, bf16[8,2,8,32,64,1]{4,3,2,1,0,5:T(8,128)(2,1)} %reshape.143), kind=kOutput, calls=%fused_computation.14 | convolution fusion | flops 268435456 | bytes 2097152 | tf_op jit(solution)/shard_map/pkqsd,bjqd->pkbsj/dot_general | solution.py:55
  52.5 0.7 reshape.47
  53.1 3.2 %all-to-all-done.2 = bf16[8,8,2048]{2,1,0:T(8,128)(2,1)S(1)} async-done(((bf16[8,8,2048]{2,1,0:T(8,128)(2,1)}), bf16[8,8,2048]{2,1,0:T(8,128)(2,1)S(1)}, u32[]{:S(2)}, u32[]{:S(2)}) %all-to-all-start.2) | async-done | bytes 262176 | tf_op jit(solution)/shard_map/all_to_all | solution.py:80
  56.3 0.1 copy.22
  56.4 1.0 %collective-permute-start.3 = (bf16[8,8,2048]{2,0,1:T(8,128)(2,1)S(1)}, bf16[8,8,2048]{2,0,1:T(8,128)(2,1)S(1)}, u32[]{:S(2)}, u32[]{:S(2)}) collective-permute-start(bf16[8,8,2048]{2,0,1:T(8,128)(2,1)S(1)} %copy.22), channel_id=1, source_target_pairs={{0,2},{1,3},{2,0},{3,1},{4,6},{5,7},{6,4},{7,5},{8,10},{9,11},{10,... | collective-permute-start | bytes 786440 | tf_op jit(solution)/shard_map/ppermute | solution.py:89
  57.4 5.7 %collective-permute-done.3 = bf16[8,8,2048]{2,0,1:T(8,128)(2,1)S(1)} collective-permute-done((bf16[8,8,2048]{2,0,1:T(8,128)(2,1)S(1)}, bf16[8,8,2048]{2,0,1:T(8,128)(2,1)S(1)}, u32[]{:S(2)}, u32[]{:S(2)}) %collective-permute-start.3) | collective-permute-done | bytes 262176 | tf_op jit(solution)/shard_map/ppermute | solution.py:89
  63.2 0.2 select_reduce_fusion.3
  63.4 0.1 pad_add_fusion
  63.5 1.1 %collective-permute-done.5 = bf16[8,8,2048]{2,0,1:T(8,128)(2,1)S(1)} collective-permute-done((bf16[8,8,2048]{2,0,1:T(8,128)(2,1)S(1)}, bf16[8,8,2048]{2,0,1:T(8,128)(2,1)S(1)}, u32[]{:S(2)}, u32[]{:S(2)}) %collective-permute-start.5) | collective-permute-done | bytes 262176 | tf_op jit(solution)/shard_map/ppermute | solution.py:89
  64.7 1.2 %fusion.7 = bf16[8,16,2048]{2,1,0:T(8,128)(2,1)} fusion(f32[8,16,2048]{2,1,0:T(8,128)S(1)} %reshape.47, bf16[8,8,2048]{2,0,1:T(8,128)(2,1)S(1)} %collective-permute-done.5, bf16[8,8,2048]{2,0,1:T(8,128)(2,1)S(1)} %collective-permute-done.4, bf16[8,8,2048]{2,0,1:T(8,128)(2,1)S(1)} %collective-permute-done.3, bf16[8,8,2048]{2,0,1:T(8,128)(2,1)S(1)} %copy.22, ...), kind=kOutput, calls=%fused_computation.9 | convolution fusion | flops 21496320 | bytes 2621632 | tf_op jit(solution)/shard_map/rpo,rt->pto/dot_general | solution.py:96
  (12 shorter events, 0.3 us)
Async XLA Ops:
  3.4 19.3 %all-to-all-start.1 = ((bf16[32,2,2048]{2,1,0:T(2,128)(2,1)}), bf16[32,2,2048]{2,1,0:T(2,128)(2,1)S(1)}, u32[]{:S(2)}, u32[]{:S(2)}) async-start(bf16[32,2,2048]{2,1,0:T(2,128)(2,1)} %copy.16), calls=%async_computation.1 | async-start | bytes 524288 | tf_op jit(solution)/shard_map/all_to_all | solution.py:31
  11.9 6.6 %collective-permute-start.2 = (bf16[2,16,2048]{2,1,0:T(8,128)(2,1)S(1)}, bf16[2,16,2048]{2,1,0:T(8,128)(2,1)S(1)}, u32[]{:S(2)}, u32[]{:S(2)}) collective-permute-start(bf16[2,16,2048]{2,1,0:T(8,128)(2,1)S(1)} %get-tuple-element.30), channel_id=1, source_target_pairs={{0,3},{1,0},{2,1},{3,2},{4,7},{5,4},{6,5},{7,6},{8,11},{9,8},{10,9... | collective-permute-start | bytes 393224 | tf_op jit(solution)/shard_map/ppermute | solution.py:43
  13.5 9.1 %collective-permute-start.1 = (bf16[2,16,2048]{2,1,0:T(8,128)(2,1)S(1)}, bf16[2,16,2048]{2,1,0:T(8,128)(2,1)S(1)}, u32[]{:S(2)}, u32[]{:S(2)}) collective-permute-start(bf16[2,16,2048]{2,1,0:T(8,128)(2,1)S(1)} %get-tuple-element.31), channel_id=1, source_target_pairs={{0,2},{1,3},{2,0},{3,1},{4,6},{5,7},{6,4},{7,5},{8,10},{9,11},{10,... | collective-permute-start | bytes 393224 | tf_op jit(solution)/shard_map/ppermute | solution.py:43
  13.8 8.7 %collective-permute-start = (bf16[2,16,2048]{2,1,0:T(8,128)(2,1)S(1)}, bf16[2,16,2048]{2,1,0:T(8,128)(2,1)S(1)}, u32[]{:S(2)}, u32[]{:S(2)}) collective-permute-start(bf16[2,16,2048]{2,1,0:T(8,128)(2,1)S(1)} %get-tuple-element.32), channel_id=1, source_target_pairs={{0,1},{1,2},{2,3},{3,0},{4,5},{5,6},{6,7},{7,4},{8,9},{9,10},{10,1... | collective-permute-start | bytes 393224 | tf_op jit(solution)/shard_map/ppermute | solution.py:43
  22.6 15.2 %all-to-all-start = ((bf16[32,2,2048]{2,1,0:T(2,128)(2,1)}), bf16[32,2,2048]{2,1,0:T(2,128)(2,1)S(1)}, u32[]{:S(2)}, u32[]{:S(2)}) async-start(bf16[32,2,2048]{2,1,0:T(2,128)(2,1)} %copy.15), calls=%async_computation | async-start | bytes 524288 | tf_op jit(solution)/shard_map/all_to_all | solution.py:31
  43.6 12.6 %all-to-all-start.2 = ((bf16[8,8,2048]{2,1,0:T(8,128)(2,1)}), bf16[8,8,2048]{2,1,0:T(8,128)(2,1)S(1)}, u32[]{:S(2)}, u32[]{:S(2)}) async-start(bf16[8,8,2048]{2,1,0:T(8,128)(2,1)} %bitcast.10), calls=%async_computation.2 | async-start | bytes 524288 | tf_op jit(solution)/shard_map/all_to_all | solution.py:80
  56.4 6.7 %collective-permute-start.3 = (bf16[8,8,2048]{2,0,1:T(8,128)(2,1)S(1)}, bf16[8,8,2048]{2,0,1:T(8,128)(2,1)S(1)}, u32[]{:S(2)}, u32[]{:S(2)}) collective-permute-start(bf16[8,8,2048]{2,0,1:T(8,128)(2,1)S(1)} %copy.22), channel_id=1, source_target_pairs={{0,2},{1,3},{2,0},{3,1},{4,6},{5,7},{6,4},{7,5},{8,10},{9,11},{10,... | collective-permute-start | bytes 786440 | tf_op jit(solution)/shard_map/ppermute | solution.py:89
  57.4 6.1 %collective-permute-start.4 = (bf16[8,8,2048]{2,0,1:T(8,128)(2,1)S(1)}, bf16[8,8,2048]{2,0,1:T(8,128)(2,1)S(1)}, u32[]{:S(2)}, u32[]{:S(2)}) collective-permute-start(bf16[8,8,2048]{2,0,1:T(8,128)(2,1)S(1)} %copy.22), channel_id=1, source_target_pairs={{0,1},{1,0},{2,3},{3,2},{4,5},{5,4},{6,7},{7,6},{8,9},{9,8},{10,11... | collective-permute-start | bytes 786440 | tf_op jit(solution)/shard_map/ppermute | solution.py:89
  63.1 1.5 %collective-permute-start.5 = (bf16[8,8,2048]{2,0,1:T(8,128)(2,1)S(1)}, bf16[8,8,2048]{2,0,1:T(8,128)(2,1)S(1)}, u32[]{:S(2)}, u32[]{:S(2)}) collective-permute-start(bf16[8,8,2048]{2,0,1:T(8,128)(2,1)S(1)} %collective-permute-done.3), channel_id=1, source_target_pairs={{0,1},{1,0},{2,3},{3,2},{4,5},{5,4},{6,7},{7,6},{8,9},{9,8},{10,11... | collective-permute-start | bytes 786440 | tf_op jit(solution)/shard_map/ppermute | solution.py:89

commit v16 on v9

--- a/solution.py
+++ b/solution.py
@@ -20,13 +20,16 @@
     virt_idx = lax.axis_index("virt")
     p_grp = pm_rows * n_virt
 
-    tin_all = blk_tiles[:, 0]
+    tin_all = jnp.transpose(blk_tiles[:, 0].reshape(n_pair, n_virt)).reshape(-1)
     tile_ids = jnp.arange(n_tiles, dtype=jnp.int32)
     pick = (tin_all[:, None] == tile_ids[None, :]).astype(amps_pm.dtype)
     picked = jnp.einsum(
         "dt,itc->dic", pick, amps_pm, preferred_element_type=jnp.float32
     ).astype(amps_pm.dtype)
-    chosen = lax.all_to_all(picked, ("pair", "virt"), 0, 0, tiled=True)
+    picked = picked.reshape(n_virt, n_pair, pm_rows, tile_len)
+    mid = lax.all_to_all(picked, "virt", 0, 0, tiled=True)
+    mid = jnp.transpose(mid, (1, 0, 2, 3))
+    chosen = lax.all_to_all(mid, "pair", 0, 0, tiled=True)
     chosen = chosen.reshape(n_dev * pm_rows, tile_len)
 
     got = [lax.dynamic_slice_in_dim(amps_pm[:, :, :out_cols], virt_idx * slab, slab, 1)]

time: 58.7 us -> 69.4 us (1.18)
  blocking collectives: 0 us -> 13 us
  starting transfers between devices: 14.8 us -> 11.5 us
  local copies, waits for them, and re-layouts: 6.76 us -> 7.54 us
    all_to_all x0 -> x1, blocking collectives: none -> 13 us  [per_device(): mid = lax.all_to_all(picked, 'virt', 0, 0, tiled=True)]
    ppermute x3, waiting for transfers between devices: 9.62 us -> 5.23 us  [per_device(): got.append(lax.ppermute(part, 'virt', perm))]
    all_to_all x1, waiting for transfers between devices: 1.91 us -> 6 us  [per_device(): chosen = lax.all_to_all(mid, 'pair', 0, 0, tiled=True)]
    all_to_all x1, starting transfers between devices: 7.33 us -> 5.83 us  [per_device(): chosen = lax.all_to_all(mid, 'pair', 0, 0, tiled=True)]
    transpose x0 -> x2, local copies, waits for them, and re-layouts: none -> 1.37 us  [the longest x1 1.29 us: per_device(): mid = jnp.transpose(mid, (1, 0, 2, 3))]
    convert_element_type x1 -> x0, local copies, waits for them, and re-layouts: 1.34 us -> none  [per_device(): picked = jnp.einsum('dt,itc->dic', pick, amps_pm, preferred_element_type=...]
    ppermute x3, starting transfers between devices: 2.05 us -> 0.87 us  [per_device(): got.append(lax.ppermute(part, 'virt', perm))]
  transfers between devices with their start and end apart: 8 -> 8, of which waited for: 6 -> 7; matrix products, arithmetic and copies ran while one was open for 13% -> 11% of each run, Pallas kernels for 0% -> 0%
where the time goes in v16:
time: 69.4 us; the launch traced here: 68.9 us
  waiting for transfers between devices  20.5 us (30%)
  matrix products  15.3 us (22%)
  blocking collectives  13 us (19%)
  starting transfers between devices  11.5 us (17%)
  local copies, waits for them, and re-layouts  7.54 us (11%)
  between operations  0.81 us (1%)
    all_to_all x1, blocking collectives, per_device(): mid = lax.all_to_all(picked, 'virt', 0, 0, tiled=True)  13 us
    dot_general x1, matrix products, per_device(): product = jnp.dot(chosen, cols, preferred_element_type=jnp.float32)  9.5 us
    ppermute x3, waiting for transfers between devices, per_device(): got = [lax.ppermute(x, 'virt', perm) for x in blocks]  6.46 us
    all_to_all x1, waiting for transfers between devices, per_device(): chosen = lax.all_to_all(mid, 'pair', 0, 0, tiled=True)  6 us
    all_to_all x1, starting transfers between devices, per_device(): chosen = lax.all_to_all(mid, 'pair', 0, 0, tiled=True)  5.83 us
    ppermute x3, waiting for transfers between devices, per_device(): got.append(lax.ppermute(part, 'virt', perm))  5.23 us
    all_to_all x1, starting transfers between devices, per_device(): lax.all_to_all(product.reshape(n_pair, p_grp, width), 'pair', 0, 0, tiled...  3.64 us
    all_to_all x1, waiting for transfers between devices, per_device(): lax.all_to_all(product.reshape(n_pair, p_grp, width), 'pair', 0, 0, tiled...  2.8 us
  transfers between devices with their start and end apart: 8, of which 7 were waited for; matrix products, arithmetic and copies ran while one was open for 11% of the time, Pallas kernels for 0%

profile of v16, /device:TPU:0, one launch (start us, length us, event | category | flops | bytes accessed | tf_op | source)
XLA Modules:
  0.0 68.9 jit_solution(11247598470266203494)
XLA Ops:
  0.0 0.8 %slice_reduce_fusion.1 = (s32[32]{0:T(128)S(1)}, s32[32]{0:T(128)S(1)}) fusion(s32[32,2]{0,1:T(2,128)} %param.10), kind=kLoop, calls=%fused_computation.47 | loop fusion | bytes 512 | tf_op jit(solution)/shard_map/slice | solution.py:60
  0.8 0.1 reshape_squeeze.7
  0.9 0.1 copy.25
  0.9 0.1 eq.50
  1.0 1.6 %fusion.2 = bf16[4,8,2,4096]{3,1,0,2:T(8,128)(2,1)S(1)} fusion(bf16[2,64,4096]{2,1,0:T(8,128)(2,1)} %param.7, s32[32]{0:T(128)S(1)} %eq.50), kind=kOutput, calls=%fused_computation.3 | convolution fusion | flops 33818624 | bytes 1572992 | tf_op jit(solution)/shard_map/dt,itc->dic/dot_general | solution.py:26
  2.6 0.5 copy.26
  3.2 13.0 %all_to_all.15 = bf16[4,8,2,4096]{3,2,1,0:T(2,128)(2,1)S(1)} all-to-all(bf16[4,8,2,4096]{3,2,1,0:T(2,128)(2,1)S(1)} %copy.26), channel_id=1, replica_groups=mesh['pair'=8,'virt'=4] {'virt'}, dimensions={0} | all-to-all | bytes 1048576 | tf_op jit(solution)/shard_map/all_to_all | solution.py:30
  16.2 1.3 %copy.27 = bf16[8,4,2,4096]{3,2,1,0:T(2,128)(2,1)} copy(bf16[8,4,2,4096]{3,2,0,1:T(2,128)(2,1)S(1)} %bitcast.50) | data formatting | bytes 1048576 | tf_op jit(solution)/shard_map/transpose | solution.py:31
  17.4 5.8 %all-to-all-start.1 = ((bf16[8,4,2,4096]{3,2,1,0:T(2,128)(2,1)}), bf16[8,4,2,4096]{3,2,1,0:T(2,128)(2,1)S(1)}, u32[]{:S(2)}, u32[]{:S(2)}) async-start(bf16[8,4,2,4096]{3,2,1,0:T(2,128)(2,1)} %copy.27), calls=%async_computation.1 | async-start | bytes 1048576 | tf_op jit(solution)/shard_map/all_to_all | solution.py:32
  23.4 0.8 %collective-permute-start.1 = (bf16[2,16,2048]{2,1,0:T(8,128)(2,1)S(1)}, bf16[2,16,2048]{2,1,0:T(8,128)(2,1)S(1)}, u32[]{:S(2)}, u32[]{:S(2)}) collective-permute-start(bf16[2,16,2048]{2,1,0:T(8,128)(2,1)S(1)} %get-tuple-element.33), channel_id=1, source_target_pairs={{0,2},{1,3},{2,0},{3,1},{4,6},{5,7},{6,4},{7,5},{8,10},{9,11},{10,... | collective-permute-start | bytes 393224 | tf_op jit(solution)/shard_map/ppermute | solution.py:41
  24.2 0.7 dynamic_slice.16
  25.6 0.5 reshape.45
  26.1 1.1 %collective-permute-done.2 = bf16[2,16,2048]{2,1,0:T(8,128)(2,1)S(1)} collective-permute-done((bf16[2,16,2048]{2,1,0:T(8,128)(2,1)S(1)}, bf16[2,16,2048]{2,1,0:T(8,128)(2,1)S(1)}, u32[]{:S(2)}, u32[]{:S(2)}) %collective-permute-start.2) | collective-permute-done | bytes 131104 | tf_op jit(solution)/shard_map/ppermute | solution.py:41
  27.3 3.3 %collective-permute-done.1 = bf16[2,16,2048]{2,1,0:T(8,128)(2,1)S(1)} collective-permute-done((bf16[2,16,2048]{2,1,0:T(8,128)(2,1)S(1)}, bf16[2,16,2048]{2,1,0:T(8,128)(2,1)S(1)}, u32[]{:S(2)}, u32[]{:S(2)}) %collective-permute-start.1) | collective-permute-done | bytes 131104 | tf_op jit(solution)/shard_map/ppermute | solution.py:41
  30.6 0.8 %collective-permute-done = bf16[2,16,2048]{2,1,0:T(8,128)(2,1)S(1)} collective-permute-done((bf16[2,16,2048]{2,1,0:T(8,128)(2,1)S(1)}, bf16[2,16,2048]{2,1,0:T(8,128)(2,1)S(1)}, u32[]{:S(2)}, u32[]{:S(2)}) %collective-permute-start) | collective-permute-done | bytes 131104 | tf_op jit(solution)/shard_map/ppermute | solution.py:41
  31.4 6.0 %all-to-all-done.1 = bf16[8,4,2,4096]{3,2,1,0:T(2,128)(2,1)S(1)} async-done(((bf16[8,4,2,4096]{3,2,1,0:T(2,128)(2,1)}), bf16[8,4,2,4096]{3,2,1,0:T(2,128)(2,1)S(1)}, u32[]{:S(2)}, u32[]{:S(2)}) %all-to-all-start.1) | async-done | bytes 524320 | tf_op jit(solution)/shard_map/all_to_all | solution.py:32
  37.4 0.2 reshape.42
  37.6 9.5 %fusion.8 = bf16[64,2048]{1,0:T(8,128)(2,1)} fusion(bf16[64,4096]{1,0:T(8,128)(2,1)S(1)} %reshape.42, bf16[1,4096,2048]{2,1,0:T(8,128)(2,1)} %param.8, f32[]{:T(128)} %bitcast.6), kind=kOutput, calls=%fused_computation.9 | convolution fusion | flops 1074003968 | bytes 17563652 | tf_op jit(solution)/shard_map/dot_general | solution.py:72
  47.1 3.6 %all-to-all-start.2 = ((bf16[8,8,2048]{2,1,0:T(8,128)(2,1)}), bf16[8,8,2048]{2,1,0:T(8,128)(2,1)S(1)}, u32[]{:S(2)}, u32[]{:S(2)}) async-start(bf16[8,8,2048]{2,1,0:T(8,128)(2,1)} %bitcast.11), calls=%async_computation.2 | async-start | bytes 524288 | tf_op jit(solution)/shard_map/all_to_all | solution.py:75
  50.8 0.5 convolution_convert_fusion.1
  51.3 0.3 copy.29
  51.6 2.1 %reshape.142 = bf16[8,2,8,32,64,1]{4,3,2,1,0,5:T(8,128)(2,1)} reshape(bf16[4,2,16,2048]{3,2,1,0:T(8,128)(2,1)S(1)} %copy.29) | data formatting | bytes 1048576 | tf_op jit(solution)/shard_map/reshape | solution.py:52
  53.7 2.5 %convolution_bitcast_fusion.1 = f32[8,2,8,32,64]{4,3,2,1,0:T(8,128)S(1)} fusion(bf16[8,64,8,64,1,1]{3,2,1,0,5,4:T(8,128)(2,1)S(1)} %bitcast.51, bf16[8,2,8,32,64,1]{4,3,2,1,0,5:T(8,128)(2,1)} %reshape.142), kind=kOutput, calls=%fused_computation.10 | convolution fusion | flops 268435456 | bytes 2097152 | tf_op jit(solution)/shard_map/pkqsd,bjqd->pkbsj/dot_general | solution.py:53
  56.2 0.7 reshape.46
  56.8 2.8 %all-to-all-done.2 = bf16[8,8,2048]{2,1,0:T(8,128)(2,1)S(1)} async-done(((bf16[8,8,2048]{2,1,0:T(8,128)(2,1)}), bf16[8,8,2048]{2,1,0:T(8,128)(2,1)S(1)}, u32[]{:S(2)}, u32[]{:S(2)}) %all-to-all-start.2) | async-done | bytes 262176 | tf_op jit(solution)/shard_map/all_to_all | solution.py:75
  59.6 0.1 copy.33
  59.8 1.1 %collective-permute-start.3 = (bf16[8,8,2048]{2,0,1:T(8,128)(2,1)S(1)}, bf16[8,8,2048]{2,0,1:T(8,128)(2,1)S(1)}, u32[]{:S(2)}, u32[]{:S(2)}) collective-permute-start(bf16[8,8,2048]{2,0,1:T(8,128)(2,1)S(1)} %copy.33), channel_id=1, source_target_pairs={{0,2},{1,3},{2,0},{3,1},{4,6},{5,7},{6,4},{7,5},{8,10},{9,11},{10,... | collective-permute-start | bytes 786440 | tf_op jit(solution)/shard_map/ppermute | solution.py:84
  60.9 5.3 %collective-permute-done.3 = bf16[8,8,2048]{2,0,1:T(8,128)(2,1)S(1)} collective-permute-done((bf16[8,8,2048]{2,0,1:T(8,128)(2,1)S(1)}, bf16[8,8,2048]{2,0,1:T(8,128)(2,1)S(1)}, u32[]{:S(2)}, u32[]{:S(2)}) %collective-permute-start.3) | collective-permute-done | bytes 262176 | tf_op jit(solution)/shard_map/ppermute | solution.py:84
  66.3 0.2 select_reduce_fusion.3
  66.6 0.1 pad_add_fusion
  66.6 1.1 %collective-permute-done.5 = bf16[8,8,2048]{2,0,1:T(8,128)(2,1)S(1)} collective-permute-done((bf16[8,8,2048]{2,0,1:T(8,128)(2,1)S(1)}, bf16[8,8,2048]{2,0,1:T(8,128)(2,1)S(1)}, u32[]{:S(2)}, u32[]{:S(2)}) %collective-permute-start.5) | collective-permute-done | bytes 262176 | tf_op jit(solution)/shard_map/ppermute | solution.py:84
  67.8 1.2 %fusion.4 = bf16[8,16,2048]{2,1,0:T(8,128)(2,1)} fusion(f32[8,16,2048]{2,1,0:T(8,128)S(1)} %reshape.46, bf16[8,8,2048]{2,0,1:T(8,128)(2,1)S(1)} %collective-permute-done.5, bf16[8,8,2048]{2,0,1:T(8,128)(2,1)S(1)} %collective-permute-done.4, bf16[8,8,2048]{2,0,1:T(8,128)(2,1)S(1)} %collective-permute-done.3, bf16[8,8,2048]{2,0,1:T(8,128)(2,1)S(1)} %copy.33, ...), kind=kOutput, calls=%fused_computation.6 | convolution fusion | flops 21496320 | bytes 2621632 | tf_op jit(solution)/shard_map/rpo,rt->pto/dot_general | solution.py:91
  (16 shorter events, 0.3 us)
Async XLA Ops:
  3.2 20.1 %slice-start = ((bf16[2,64,4096]{2,1,0:T(8,128)(2,1)}), bf16[2,64,2048]{2,1,0:T(8,128)(2,1)S(1)}, s32[]{:S(2)}) async-start(bf16[2,64,4096]{2,1,0:T(8,128)(2,1)} %param.7), calls=%async_computation.3 | async-start | bytes 1048576 | tf_op jit(solution)/shard_map/slice | solution.py:35
  16.2 8.1 %copy-start.1 = (s32[32]{0:T(128)S(1)}, s32[32]{0:T(128)}, u32[]{:S(2)}) copy-start(s32[32]{0:T(128)} %param.11) | copy-start | bytes 388
  16.2 9.4 %copy-start = (bf16[512,512]{1,0:T(8,128)(2,1)S(1)}, bf16[512,512]{1,0:T(8,128)(2,1)}, u32[]{:S(2)}) copy-start(bf16[512,512]{1,0:T(8,128)(2,1)} %param.9) | copy-start | bytes 1572868
  17.4 20.0 %all-to-all-start.1 = ((bf16[8,4,2,4096]{3,2,1,0:T(2,128)(2,1)}), bf16[8,4,2,4096]{3,2,1,0:T(2,128)(2,1)S(1)}, u32[]{:S(2)}, u32[]{:S(2)}) async-start(bf16[8,4,2,4096]{3,2,1,0:T(2,128)(2,1)} %copy.27), calls=%async_computation.1 | async-start | bytes 1048576 | tf_op jit(solution)/shard_map/all_to_all | solution.py:32
  23.3 3.9 %collective-permute-start.2 = (bf16[2,16,2048]{2,1,0:T(8,128)(2,1)S(1)}, bf16[2,16,2048]{2,1,0:T(8,128)(2,1)S(1)}, u32[]{:S(2)}, u32[]{:S(2)}) collective-permute-start(bf16[2,16,2048]{2,1,0:T(8,128)(2,1)S(1)} %get-tuple-element.32), channel_id=1, source_target_pairs={{0,3},{1,0},{2,1},{3,2},{4,7},{5,4},{6,5},{7,6},{8,11},{9,8},{10,9... | collective-permute-start | bytes 393224 | tf_op jit(solution)/shard_map/ppermute | solution.py:41
  23.4 7.2 %collective-permute-start.1 = (bf16[2,16,2048]{2,1,0:T(8,128)(2,1)S(1)}, bf16[2,16,2048]{2,1,0:T(8,128)(2,1)S(1)}, u32[]{:S(2)}, u32[]{:S(2)}) collective-permute-start(bf16[2,16,2048]{2,1,0:T(8,128)(2,1)S(1)} %get-tuple-element.33), channel_id=1, source_target_pairs={{0,2},{1,3},{2,0},{3,1},{4,6},{5,7},{6,4},{7,5},{8,10},{9,11},{10,... | collective-permute-start | bytes 393224 | tf_op jit(solution)/shard_map/ppermute | solution.py:41
  24.2 7.2 %collective-permute-start = (bf16[2,16,2048]{2,1,0:T(8,128)(2,1)S(1)}, bf16[2,16,2048]{2,1,0:T(8,128)(2,1)S(1)}, u32[]{:S(2)}, u32[]{:S(2)}) collective-permute-start(bf16[2,16,2048]{2,1,0:T(8,128)(2,1)S(1)} %get-tuple-element.34), channel_id=1, source_target_pairs={{0,1},{1,2},{2,3},{3,0},{4,5},{5,6},{6,7},{7,4},{8,9},{9,10},{10,1... | collective-permute-start | bytes 393224 | tf_op jit(solution)/shard_map/ppermute | solution.py:41
  47.1 12.5 %all-to-all-start.2 = ((bf16[8,8,2048]{2,1,0:T(8,128)(2,1)}), bf16[8,8,2048]{2,1,0:T(8,128)(2,1)S(1)}, u32[]{:S(2)}, u32[]{:S(2)}) async-start(bf16[8,8,2048]{2,1,0:T(8,128)(2,1)} %bitcast.11), calls=%async_computation.2 | async-start | bytes 524288 | tf_op jit(solution)/shard_map/all_to_all | solution.py:75
  59.8 6.4 %collective-permute-start.3 = (bf16[8,8,2048]{2,0,1:T(8,128)(2,1)S(1)}, bf16[8,8,2048]{2,0,1:T(8,128)(2,1)S(1)}, u32[]{:S(2)}, u32[]{:S(2)}) collective-permute-start(bf16[8,8,2048]{2,0,1:T(8,128)(2,1)S(1)} %copy.33), channel_id=1, source_target_pairs={{0,2},{1,3},{2,0},{3,1},{4,6},{5,7},{6,4},{7,5},{8,10},{9,11},{10,... | collective-permute-start | bytes 786440 | tf_op jit(solution)/shard_map/ppermute | solution.py:84
  60.9 5.7 %collective-permute-start.4 = (bf16[8,8,2048]{2,0,1:T(8,128)(2,1)S(1)}, bf16[8,8,2048]{2,0,1:T(8,128)(2,1)S(1)}, u32[]{:S(2)}, u32[]{:S(2)}) collective-permute-start(bf16[8,8,2048]{2,0,1:T(8,128)(2,1)S(1)} %copy.33), channel_id=1, source_target_pairs={{0,1},{1,0},{2,3},{3,2},{4,5},{5,4},{6,7},{7,6},{8,9},{9,8},{10,11... | collective-permute-start | bytes 786440 | tf_op jit(solution)/shard_map/ppermute | solution.py:84
  66.2 1.5 %collective-permute-start.5 = (bf16[8,8,2048]{2,0,1:T(8,128)(2,1)S(1)}, bf16[8,8,2048]{2,0,1:T(8,128)(2,1)S(1)}, u32[]{:S(2)}, u32[]{:S(2)}) collective-permute-start(bf16[8,8,2048]{2,0,1:T(8,128)(2,1)S(1)} %collective-permute-done.3), channel_id=1, source_target_pairs={{0,1},{1,0},{2,3},{3,2},{4,5},{5,4},{6,7},{7,6},{8,9},{9,8},{10,11... | collective-permute-start | bytes 786440 | tf_op jit(solution)/shard_map/ppermute | solution.py:84
